TPU v7x, 512 devices: a whole 4x8x8 slice. The times are simulated.
512 devices in a mesh: grp: 16 (over x_hi, y), blk: 32 (over z, x_lo, core).
Axes of the slice: x: 4 (x_hi: 2, x_lo: 2; x = x_hi * 2 + x_lo), y: 8, z: 8, core: 2. Of those that a mesh axis runs over, the one named last changes fastest.
Arguments:
- queries: bfloat16 [512, 8192], P('blk'), may hold values from -6 to 6
- prefix_keys: bfloat16 [65536, 1024], P(('grp', 'blk')), may hold values from -10 to 10
- prefix_values: bfloat16 [65536, 1024], P(('grp', 'blk')), may hold values from -6 to 6
- draft_keys: bfloat16 [512, 1024], P(('grp', 'blk')), may hold values from -12 to 12
- draft_values: bfloat16 [512, 1024], P(('grp', 'blk')), may hold values from -6 to 6
- draft_offset: int32 [512], replicated, may hold values from 0 to 511, as said below
Outputs:
- attended: float32 [512, 8192], P('blk')
Inputs may be any that keep to these rules, and one draw needn't show every extreme that they name: Draft token i sees draft keys i - draft_offset[i] through i, and draft_offset[i] <= i.
All inputs are finite; a program needn't handle non-finite values.
Results may differ from a plain program's by a relative error of at most 0.0005.
Values may be sent and summed in bfloat16 or wider, within the bound.
No kernel may reach another device: no remote copies, remote signals or barrier semaphores. Data moves between devices by JAX's collectives and lax.ppermute only.
A program may use at most 128 MiB of HBM per device.

v0:
```python
import math

import jax
import jax.numpy as jnp
from jax import lax
from jax.sharding import PartitionSpec as P

H = 64
KV = 8
HD = 128


NEGATIVE = -1e30


def merged(value, axis, join):
    pieces = jax.tree.map(lambda part: lax.all_gather(part, axis), value)
    head = jax.tree.map(lambda part: part[0], pieces)
    tail = jax.tree.map(lambda part: part[1:], pieces)
    subtotal, _ = lax.scan(lambda subtotal, slab: (join(subtotal, slab), None), head, tail)
    return subtotal


def absorb(carried, query_block, query_first, key_rows, value_rows, key_first, offsets, masked):
    running_max, totals, accumulated = carried
    head_size = query_block.shape[-1]
    scores = jnp.einsum(
        "rkgd,pkd->rkgp", query_block, key_rows, preferred_element_type=jnp.float32
    ) * (1.0 / math.sqrt(head_size))
    if masked:
        query_index = query_first + lax.iota(jnp.int32, query_block.shape[0])
        key_index = key_first + lax.iota(jnp.int32, key_rows.shape[0])
        visible = (key_index[None, :] <= query_index[:, None]) & (
            key_index[None, :] >= (query_index - offsets)[:, None]
        )
        visible = visible[:, None, None, :]
        scores = jnp.where(visible, scores, NEGATIVE)
    new_max = jnp.maximum(running_max, jnp.max(scores, axis=3))
    weights = jnp.exp(scores - new_max[..., None])
    if masked:
        weights = jnp.where(visible, weights, 0.0)
    factor = jnp.exp(running_max - new_max)
    totals = totals * factor + jnp.sum(weights, axis=3)
    accumulated = accumulated * factor[..., None] + jnp.einsum(
        "rkgp,pkd->rkgd", weights, value_rows.astype(jnp.float32), precision=lax.Precision.HIGHEST
    )
    return (new_max, totals, accumulated)


def start_state(row_count, kv_heads, group_heads):
    state_shape = (row_count, kv_heads, group_heads)
    return (
        jnp.full(state_shape, NEGATIVE, jnp.float32),
        jnp.zeros(state_shape, jnp.float32),
        jnp.zeros(state_shape + (HD,), jnp.float32),
    )


def combine_parts(first_part, second_part):
    joined = jnp.maximum(first_part[0], second_part[0])
    first_scale = jnp.exp(first_part[0] - joined)
    second_scale = jnp.exp(second_part[0] - joined)
    return (
        joined,
        first_part[1] * first_scale + second_part[1] * second_scale,
        first_part[2] * first_scale[..., None] + second_part[2] * second_scale[..., None],
    )


def merge_groups(carried):
    running_max, totals, accumulated = carried
    row_count = running_max.shape[0]
    head_total = running_max.shape[1] * running_max.shape[2]
    running_max, totals, accumulated = merged(
        (running_max, totals, accumulated), "grp", combine_parts
    )
    return (accumulated / totals[..., None]).reshape(row_count, head_total * HD)


def local(queries, prefix_keys, prefix_values, draft_keys, draft_values, draft_offset):
    group_heads = H // KV
    query_count = queries.shape[0]
    query_first = lax.axis_index("blk") * query_count
    own_offsets = lax.dynamic_slice_in_dim(draft_offset, query_first, query_count)
    query_block = queries.reshape(query_count, KV, group_heads, HD)
    carried = absorb(
        start_state(query_count, KV, group_heads),
        query_block,
        query_first,
        lax.all_gather(prefix_keys, "blk", axis=0, tiled=True).reshape(-1, KV, HD),
        lax.all_gather(prefix_values, "blk", axis=0, tiled=True).reshape(-1, KV, HD),
        0,
        None,
        False,
    )
    group_keys, group_values = (
        lax.all_gather(draft_keys, "blk", axis=0, tiled=True),
        lax.all_gather(draft_values, "blk", axis=0, tiled=True),
    )
    group_first = lax.axis_index("grp") * group_keys.shape[0]
    carried = absorb(
        carried,
        query_block,
        query_first,
        group_keys.reshape(-1, KV, HD),
        group_values.reshape(-1, KV, HD),
        group_first,
        own_offsets,
        True,
    )
    return merge_groups(carried)


def solution(mesh):
    return jax.shard_map(
        local,
        mesh=mesh,
        in_specs=(
            P("blk", None),
            P(("grp", "blk"), None),
            P(("grp", "blk"), None),
            P(("grp", "blk"), None),
            P(("grp", "blk"), None),
            P(),
        ),
        out_specs=P("blk", None),
        check_vma=False,
    )
```

profile of v0, /device:TPU:6, one launch (start us, length us, event | category | flops | bytes accessed | tf_op | source)
XLA Modules:
  0.0 414.3 jit_solution(3885214013326667396)
XLA Ops:
  6.5 1.8 copy.37
  8.4 1.8 copy.42
  10.3 1.0 copy.65
  11.3 38.5 %all-gather.1 = bf16[32,1,1024]{2,1,0:T(2,128)(2,1)S(1)} all-gather(bf16[1,1,1024]{2,1,0:T(2,128)(2,1)} %bitcast.122), channel_id=1, replica_groups=mesh['grp'=16,'blk'=32] {'blk'}, dimensions={0}, use_global_device_ids=true | all-gather | bytes 67584 | tf_op jit(solution)/shard_map/all_gather | solution.py:97
  49.8 0.4 reduce
  50.2 34.9 %all-gather.2 = bf16[32,1,1024]{2,1,0:T(2,128)(2,1)S(1)} all-gather(bf16[1,1,1024]{2,1,0:T(2,128)(2,1)} %bitcast.123), channel_id=1, replica_groups=mesh['grp'=16,'blk'=32] {'blk'}, dimensions={0}, use_global_device_ids=true | all-gather | bytes 67584 | tf_op jit(solution)/shard_map/all_gather | solution.py:98
  85.0 0.4 reduce.1
  85.4 0.8 dynamic-slice_subtract_fusion
  86.3 0.4 fusion.39
  86.6 21.3 %all-gather.7.cloned.1.call-done = bf16[4096,1024]{0,1:T(8,128)(2,1)} async-done(((bf16[128,1024]{0,1:T(8,128)(2,1)}), bf16[4096,1024]{0,1:T(8,128)(2,1)}) %all-gather.7.cloned.1.call-update) | async-done | bytes 8388624 | tf_op jit(solution)/shard_map/all_gather | solution.py:90
  107.9 11.5 %bitcast_reduce_fusion = (f32[16,8,8]{0,2,1:T(8,128)S(1)}, f32[8,4096,16,8]{1,2,3,0:T(8,128)}) fusion(bf16[4096,8,128,1]{0,2,3,1:T(8,128)(2,1)} %bitcast.124, bf16[16,8,8,128]{3,2,1,0:T(8,128)(2,1)S(1)} %bitcast.120), kind=kOutput, calls=%fused_computation.11 | convolution fusion | flops 1082129408 | bytes 25432064 | tf_op jit(solution)/shard_map/rkgd,pkd->rkgp/dot_general | solution.py:27
  119.5 80.8 %all-gather.9.cloned.1.call-done = bf16[4096,1024]{0,1:T(8,128)(2,1)} async-done(((bf16[128,1024]{0,1:T(8,128)(2,1)}), bf16[4096,1024]{0,1:T(8,128)(2,1)}) %all-gather.9.cloned.1.call-update) | async-done | bytes 8388624 | tf_op jit(solution)/shard_map/all_gather | solution.py:91
  200.3 14.8 %fusion.19 = f32[16,8,8,128]{3,0,2,1:T(8,128)S(1)} fusion(bf16[4096,8,128,1]{0,2,3,1:T(8,128)(2,1)} %bitcast.112, f32[8,4096,16,8]{1,2,3,0:T(8,128)} %get-tuple-element.91, f32[16,8,8]{0,2,1:T(8,128)S(1)} %get-tuple-element.89, f32[16,8,8]{0,2,1:T(8,128)S(1)} %get-tuple-element.84, f32[16,8,8]{0,2,1:T(8,128)S(1)} %get-tuple-element.88), kind=kOutput, calls=%fused_computation.24 | convolution fusion | flops 6451101696 | bytes 25702400 | tf_op jit(solution)/shard_map/rkgp,pkd->rkgd/dot_general | solution.py:44
  215.1 1.3 fusion.13
  216.4 0.4 fusion.22
  216.9 8.7 %fusion.7 = f32[16,8,8]{0,2,1:T(8,128)S(1)} fusion(f32[8,4096,16,8]{1,2,3,0:T(8,128)} %get-tuple-element.91, f32[16,8,8]{0,2,1:T(8,128)S(1)} %get-tuple-element.89), kind=kLoop, calls=%fused_computation.14 | loop fusion | flops 12581888 | bytes 16785408 | tf_op jit(solution)/shard_map/reduce_sum | solution.py:43
  225.5 43.8 %all_gather.28 = f32[16,16,8,8]{1,3,2,0:T(8,128)S(1)} all-gather(f32[1,16,8,8]{1,3,2,0:T(8,128)S(1)} %get-tuple-element.87), channel_id=1, replica_groups=mesh['grp'=16,'blk'=32] {'grp'}, dimensions={0}, use_global_device_ids=true | all-gather | bytes 69632 | tf_op jit(solution)/shard_map/all_gather | solution.py:17
  269.4 40.5 %all_gather.29 = f32[16,16,8,8]{1,3,2,0:T(8,128)S(1)} all-gather(f32[1,16,8,8]{1,3,2,0:T(8,128)S(1)} %get-tuple-element.86), channel_id=1, replica_groups=mesh['grp'=16,'blk'=32] {'grp'}, dimensions={0}, use_global_device_ids=true | all-gather | bytes 69632 | tf_op jit(solution)/shard_map/all_gather | solution.py:17
  309.9 60.1 %all-gather.11.cloned.1.call-done = f32[256,8,8,128]{3,0,2,1:T(8,128)} async-done(((f32[16,8,8,128]{3,0,2,1:T(8,128)}), f32[256,8,8,128]{3,0,2,1:T(8,128)}) %all-gather.11.cloned.1.call-update) | async-done | bytes 8388624 | tf_op jit(solution)/shard_map/all_gather | solution.py:17
  370.0 1.1 slice.28
  371.1 0.2 copy.47
  371.3 6.9 %slice.31 = f32[240,8,8,128]{3,0,2,1:T(8,128)} slice(f32[256,8,8,128]{3,0,2,1:T(8,128)} %all-gather.11.cloned.1.call-done), slice={[16:256], [0:8], [0:8], [0:128]} | slice | bytes 15728640 | tf_op jit(solution)/shard_map/slice | solution.py:19
  378.2 28.2 %while.14 = (s32[]{:T(128)}, f32[16,8,8]{0,2,1:T(8,128)S(1)}, f32[16,8,8]{0,2,1:T(8,128)S(1)}, f32[16,8,8,128]{3,2,1,0:T(8,128)S(1)}, f32[15,16,8,8]{1,3,2,0:T(8...) while((s32[]{:T(128)}, f32[16,8,8]{0,2,1:T(8,128)S(1)}, ...), condition=%wide.region_5.6_spmd, body=%wide.region_4.5_spmd.sunk | while | flops 399362 | bytes 2678885 | solution.py:20
  378.2 1.1 constant_dynamic-slice_fusion.2
  379.3 0.1 copy.94
  379.5 0.5 fusion.45
  380.1 1.1 constant_dynamic-slice_fusion.2
  381.2 0.1 copy.94
  381.4 0.5 fusion.45
  382.0 1.1 constant_dynamic-slice_fusion.2
  383.1 0.1 copy.94
  383.3 0.5 fusion.45
  383.9 1.1 constant_dynamic-slice_fusion.2
  385.0 0.1 copy.94
  385.1 0.5 fusion.45
  385.7 1.1 constant_dynamic-slice_fusion.2
  386.8 0.1 copy.94
  387.0 0.5 fusion.45
  387.6 1.1 constant_dynamic-slice_fusion.2
  388.9 0.5 fusion.45
  389.5 1.1 constant_dynamic-slice_fusion.2
  390.8 0.5 fusion.45
  391.4 1.1 constant_dynamic-slice_fusion.2
  392.5 0.1 copy.94
  392.7 0.5 fusion.45
  393.3 1.1 constant_dynamic-slice_fusion.2
  394.6 0.5 fusion.45
  395.1 1.1 constant_dynamic-slice_fusion.2
  396.2 0.1 copy.94
  396.4 0.5 fusion.45
  397.0 1.1 constant_dynamic-slice_fusion.2
  398.1 0.1 copy.94
  398.3 0.5 fusion.45
  398.9 1.1 constant_dynamic-slice_fusion.2
  400.2 0.5 fusion.45
  400.8 1.1 constant_dynamic-slice_fusion.2
  401.9 0.1 copy.94
  402.1 0.5 fusion.45
  402.7 1.1 constant_dynamic-slice_fusion.2
  404.0 0.5 fusion.45
  404.5 1.1 constant_dynamic-slice_fusion.2
  405.8 0.5 fusion.45
  406.5 0.2 broadcast_divide_fusion
  406.7 1.1 copy.89
  (53 shorter events, 2.7 us)
Async XLA Ops:
  6.5 101.4 %all-gather.7.cloned.1.call-start = ((), (), s32[]{:S(2)}) async-start(), calls=%async_computation | async-start | bytes 8650752 | tf_op jit(solution)/shard_map/all_gather | solution.py:90
  8.4 191.9 %all-gather.9.cloned.1.call-start = ((), (), s32[]{:S(2)}) async-start(), calls=%async_computation.1 | async-start | bytes 8650752 | tf_op jit(solution)/shard_map/all_gather | solution.py:91
  10.2 359.8 %all-gather.11.cloned.1.call-start = ((), (), s32[]{:S(2)}) async-start(), calls=%async_computation.2 | async-start | bytes 8912896 | tf_op jit(solution)/shard_map/all_gather | solution.py:17
Sparse Core Ops, SparseCore 0:
  9.4 98.4 all-gather.6
  110.0 90.2 all-gather.8
  216.6 153.3 all-gather.10
where the time goes:
time: 417 us; the launch traced here: 414 us
  waiting for transfers between devices  162 us (39%)
  blocking collectives  158 us (38%)
  local copies, waits for them, and re-layouts  33.2 us (8%)
  matrix products  28 us (7%)
  other arithmetic  19.2 us (5%)
  between operations  13.3 us (3%)
    all_gather x2, blocking collectives, merged(): pieces = jax.tree.map(lambda part: lax.all_gather(part, axis), value)  84.2 us
    all_gather x1, waiting for transfers between devices, local(): lax.all_gather(prefix_values, 'blk', axis=0, tiled=True).reshape(-1, KV, HD)  80.8 us
    all_gather x1, waiting for transfers between devices, merged(): pieces = jax.tree.map(lambda part: lax.all_gather(part, axis), value)  60.1 us
    all_gather x1, blocking collectives, local(): lax.all_gather(draft_keys, 'blk', axis=0, tiled=True)  38.5 us
    all_gather x1, blocking collectives, local(): lax.all_gather(draft_values, 'blk', axis=0, tiled=True)  34.9 us
    all_gather x1, waiting for transfers between devices, local(): lax.all_gather(prefix_keys, 'blk', axis=0, tiled=True).reshape(-1, KV, HD)  21.3 us
    dynamic_slice x15, local copies, waits for them, and re-layouts, merged(): lax.scan(lambda subtotal, slab: (join(subtotal, slab), None), head, tail)  16.5 us
    dot_general x2, matrix products, absorb(): jnp.einsum('rkgp,pkd->rkgd', weights, value_rows.astype(jnp.float32), pre...  16.1 us
  transfers between devices with their start and end apart: 3, of which 3 were waited for; matrix products, arithmetic and copies ran while one was open for 6% of the time, Pallas kernels for 0%

commit v1 on v0

v1 whole, which is shorter than its diff:
```python
import math

import jax
import jax.numpy as jnp
from jax import lax
from jax.sharding import Mesh
from jax.sharding import PartitionSpec as P

H = 64
KV = 8
HD = 128


def split_product(weights, values):
    rounded = lax.reduce_precision(weights, exponent_bits=8, mantissa_bits=7)
    high = rounded.astype(jnp.bfloat16)
    low = (weights - rounded).astype(jnp.bfloat16)
    spec = "rgp,pd->rgd"
    return jnp.einsum(spec, high, values, preferred_element_type=jnp.float32) + jnp.einsum(
        spec, low, values, preferred_element_type=jnp.float32
    )


def local(queries, prefix_keys, prefix_values, draft_keys, draft_values, draft_offset):
    group_heads = H // KV
    rows = queries.shape[0]
    positions = prefix_keys.shape[0]
    ways = lax.axis_size("w")
    quarters = lax.axis_size("zq")
    quarter = lax.axis_index("zq")
    group = lax.axis_index("grp")
    inverse_root = 1.0 / math.sqrt(HD)

    query_heads = queries.reshape(rows, KV, group_heads * HD).transpose(1, 0, 2).reshape(KV, -1)
    key_heads = prefix_keys.reshape(positions, KV, HD).transpose(1, 0, 2).reshape(KV, -1)
    value_heads = prefix_values.reshape(positions, KV, HD).transpose(1, 0, 2).reshape(KV, -1)
    draft_key_heads = draft_keys.reshape(KV, HD)
    draft_value_heads = draft_values.reshape(KV, HD)
    send = jnp.concatenate(
        [query_heads, key_heads, draft_key_heads, value_heads, draft_value_heads], axis=1
    )
    got = lax.all_to_all(send, "w", 0, 0, tiled=True)

    query_size = rows * group_heads * HD
    key_size = positions * HD
    cut = [query_size, key_size, HD, key_size, HD]
    starts = [sum(cut[:n]) for n in range(len(cut))]
    query_block = got[:, : query_size].reshape(ways * rows, group_heads, HD)
    keys_here = jnp.concatenate(
        [
            got[:, starts[1] : starts[1] + key_size].reshape(ways * positions, HD),
            got[:, starts[2] : starts[2] + HD],
        ],
        axis=0,
    )
    values_here = jnp.concatenate(
        [
            got[:, starts[3] : starts[3] + key_size].reshape(ways * positions, HD),
            got[:, starts[4] : starts[4] + HD],
        ],
        axis=0,
    )
    local_keys = ways * positions
    keys_all = lax.all_gather(keys_here, "zq", axis=0)
    values_all = lax.all_gather(values_here, "zq", axis=0)
    prefix_k = keys_all[:, :local_keys].reshape(-1, HD)
    draft_k = keys_all[:, local_keys:].reshape(-1, HD)
    prefix_v = values_all[:, :local_keys].reshape(-1, HD)
    draft_v = values_all[:, local_keys:].reshape(-1, HD)

    block_rows = ways * rows
    scores_prefix = jnp.einsum(
        "rgd,pd->rgp", query_block, prefix_k, preferred_element_type=jnp.float32
    ) * inverse_root
    scores_draft = jnp.einsum(
        "rgd,jd->rgj", query_block, draft_k, preferred_element_type=jnp.float32
    ) * inverse_root

    query_first = quarter * block_rows
    query_index = query_first + lax.iota(jnp.int32, block_rows)
    drafts_per_group = quarters * ways
    key_index = group * drafts_per_group + lax.iota(jnp.int32, drafts_per_group)
    offsets = lax.dynamic_slice_in_dim(draft_offset, query_first, block_rows)
    visible = (key_index[None, :] <= query_index[:, None]) & (
        key_index[None, :] >= (query_index - offsets)[:, None]
    )
    visible = visible[:, None, :]
    masked_draft = jnp.where(visible, scores_draft, -jnp.inf)
    peak = jnp.maximum(jnp.max(scores_prefix, axis=2), jnp.max(masked_draft, axis=2))
    peak = lax.pmax(peak, "grp")

    weights_prefix = jnp.exp(scores_prefix - peak[..., None])
    weights_draft = jnp.where(visible, jnp.exp(masked_draft - peak[..., None]), 0.0)
    totals = jnp.sum(weights_prefix, axis=2) + jnp.sum(weights_draft, axis=2)
    summed = split_product(weights_prefix, prefix_v) + split_product(weights_draft, draft_v)
    summed, totals = lax.psum((summed, totals), "grp")
    attended = summed / totals[..., None]

    attended = attended.reshape(block_rows, 1, group_heads * HD)
    attended = lax.all_to_all(attended, "w", 0, 1, tiled=True)
    return attended.reshape(rows, H * HD)


def solution(mesh):
    groups, blocks = mesh.shape["grp"], mesh.shape["blk"]
    inner = Mesh(mesh.devices.reshape(groups, blocks // KV, KV), ("grp", "zq", "w"))
    rows = ("zq", "w")
    return jax.shard_map(
        local,
        mesh=inner,
        in_specs=(
            P(rows, None),
            P(("grp",) + rows, None),
            P(("grp",) + rows, None),
            P(("grp",) + rows, None),
            P(("grp",) + rows, None),
            P(),
        ),
        out_specs=P(rows, None),
        check_vma=False,
    )
```

time: 417 us -> 320 us (0.77)
  blocking collectives: 158 us -> 106 us
  local copies, waits for them, and re-layouts: 33.2 us -> 11.6 us
  waiting for transfers between devices: 162 us -> 149 us
  other arithmetic: 19.2 us -> 14.9 us
    all_gather x4 -> x0, blocking collectives: 158 us -> none  [the longest x2 84.2 us: merged(): pieces = jax.tree.map(lambda part: lax.all_gather(part, axis), value)]
    all_gather x3 -> x2, waiting for transfers between devices: 162 us -> 39.5 us  [the longest x1 39.5 us: local(): keys_all = lax.all_gather(keys_here, 'zq', axis=0)]
    psum x0 -> x1, waiting for transfers between devices: none -> 109 us  [local(): summed, totals = lax.psum((summed, totals), 'grp')]
    pmax x0 -> x1, blocking collectives: none -> 40.5 us  [local(): peak = lax.pmax(peak, 'grp')]
    psum x0 -> x1, blocking collectives: none -> 36.7 us  [local(): summed, totals = lax.psum((summed, totals), 'grp')]
    all_to_all x0 -> x2, blocking collectives: none -> 28.8 us  [the longest x1 16.2 us: local(): got = lax.all_to_all(send, 'w', 0, 0, tiled=True)]
    dynamic_slice x15 -> x0, local copies, waits for them, and re-layouts: 16.5 us -> none  [merged(): lax.scan(lambda subtotal, slab: (join(subtotal, slab), None), head, tail)]
    add x32 -> x2, other arithmetic: 8.38 us -> 0.01 us  [the longest x1 0.01 us: local(): totals = jnp.sum(weights_prefix, axis=2) + jnp.sum(weights_draft, axis=2)]
  transfers between devices with their start and end apart: 3 -> 3, of which waited for: 3 -> 2; matrix products, arithmetic and copies ran while one was open for 6% -> 7% of each run, Pallas kernels for 0% -> 0%
where the time goes in v1:
time: 320 us; the launch traced here: 318 us
  waiting for transfers between devices  149 us (47%)
  blocking collectives  106 us (33%)
  matrix products  23.9 us (7%)
  other arithmetic  14.9 us (5%)
  between operations  13.3 us (4%)
  local copies, waits for them, and re-layouts  11.6 us (4%)
    psum x1, waiting for transfers between devices, local(): summed, totals = lax.psum((summed, totals), 'grp')  109 us
    pmax x1, blocking collectives, local(): peak = lax.pmax(peak, 'grp')  40.5 us
    all_gather x1, waiting for transfers between devices, local(): keys_all = lax.all_gather(keys_here, 'zq', axis=0)  39.5 us
    psum x1, blocking collectives, local(): summed, totals = lax.psum((summed, totals), 'grp')  36.7 us
    all_to_all x1, blocking collectives, local(): got = lax.all_to_all(send, 'w', 0, 0, tiled=True)  16.2 us
    all_to_all x1, blocking collectives, local(): attended = lax.all_to_all(attended, 'w', 0, 1, tiled=True)  12.6 us
    dot_general x2, matrix products, split_product(): jnp.einsum(spec, high, values, preferred_element_type=jnp.float32)  8.91 us
    reduce_sum x2, other arithmetic, local(): totals = jnp.sum(weights_prefix, axis=2) + jnp.sum(weights_draft, axis=2)  8.66 us
  transfers between devices with their start and end apart: 3, of which 2 were waited for; matrix products, arithmetic and copies ran while one was open for 7% of the time, Pallas kernels for 0%

profile of v1, /device:TPU:6, one launch (start us, length us, event | category | flops | bytes accessed | tf_op | source)
XLA Modules:
  0.0 318.5 jit_solution(3505880730103507109)
XLA Ops:
  6.5 0.0 all-gather.5.cloned.1.call-start
  6.5 1.1 copy.29
  7.7 1.0 copy.30
  8.7 1.0 copy.31
  9.7 0.7 reduce
  10.4 0.7 reduce.1
  11.2 0.5 broadcast.43
  11.7 1.2 reduce.2
  12.9 0.2 reshape.136
  13.1 16.2 %all_to_all.27 = bf16[8,2,24704]{2,1,0:T(2,128)(2,1)S(1)} all-to-all(bf16[8,2,24704]{2,1,0:T(2,128)(2,1)S(1)} %reshape.136), channel_id=1, replica_groups=mesh['grp'=16,'zq'=4,'w'=8] {'w'}, dimensions={0} | all-to-all | bytes 1581056 | tf_op jit(solution)/shard_map/all_to_all | solution.py:42
  29.4 2.5 reshape.137
  31.8 0.1 copy.43
  31.9 0.1 fusion.27
  32.0 0.1 reshape.120
  32.1 0.7 pad_maximum_fusion
  32.9 0.0 all-gather.5.cloned.1.call-update
  32.9 0.0 all-gather.7.cloned.1.call-start
  32.9 0.1 reshape.123
  33.1 0.7 pad_maximum_fusion.1
  33.8 0.0 all-gather.7.cloned.1.call-update
  33.8 0.0 all-reduce.2.cloned.1.call-start
  33.9 0.8 dynamic-slice_subtract_fusion
  34.7 0.1 compare_and_fusion
  34.7 0.1 reshape.119
  34.9 39.5 %all-gather.5.cloned.1.call-done = bf16[4128,128]{1,0:T(8,128)(2,1)} async-done(((bf16[1032,128]{1,0:T(8,128)(2,1)}), bf16[4128,128]{1,0:T(8,128)(2,1)}) %all-gather.5.cloned.1.call-update) | async-done | bytes 1056784 | tf_op jit(solution)/shard_map/all_gather | solution.py:64
  74.3 1.3 slice.39
  75.6 0.9 fusion.29
  76.5 8.1 %multiply_reduce_fusion = (f32[128,8]{0,1:T(8,128)S(1)}, f32[128,8,4096]{2,0,1:T(8,128)}) fusion(bf16[4096,128,1]{1,0,2:T(8,128)(2,1)S(1)} %bitcast.60, bf16[128,8,128]{2,1,0:T(8,128)(2,1)S(1)} %reshape.119), kind=kOutput, calls=%fused_computation.4 | convolution fusion | flops 1082129408 | bytes 18092032 | tf_op jit(solution)/shard_map/rgd,pd->rgp/dot_general | solution.py:72
  84.6 40.5 %pmax.7 = f32[128,8]{0,1:T(8,128)S(1)} all-reduce(f32[128,8]{0,1:T(8,128)S(1)} %max.5), channel_id=1, replica_groups=mesh['grp'=16,'zq'=4,'w'=8] {'grp'}, use_global_device_ids=true, to_apply=%region_2.3 | all-reduce | flops 1024 | bytes 8192 | tf_op jit(solution)/shard_map/pmax | solution.py:90
  125.1 0.0 all-gather.7.cloned.1.call-done
  125.1 0.0 copy-start
  125.1 1.4 slice.43
  126.6 1.2 fusion.16
  127.8 7.7 %fusion.2 = f32[128,8,128]{2,0,1:T(8,128)S(1)} fusion(bf16[4096,128,1]{1,0,2:T(8,128)(2,1)S(1)} %bitcast.69, f32[128,8,4096]{2,0,1:T(8,128)} %get-tuple-element.11, f32[128,8]{0,1:T(8,128)S(1)} %pmax.7), kind=kOutput, calls=%fused_computation.6 | convolution fusion | flops 1090519040 | bytes 18354176 | tf_op jit(solution)/shard_map/rgp,pd->rgd/dot_general | solution.py:19
  135.5 0.5 copy-done
  136.0 4.3 %fusion.6 = f32[128,8,128]{2,0,1:T(8,128)S(1)} fusion(f32[128,8,128]{2,0,1:T(8,128)S(1)} %fusion.2, bf16[4096,128,1]{1,0,2:T(8,128)(2,1)S(1)} %bitcast.70, f32[128,8,4096]{2,0,1:T(8,128)S(1)} %copy-done, f32[128,8]{0,1:T(8,128)S(1)} %pmax.7), kind=kOutput, calls=%fused_computation.10 | convolution fusion | flops 1094844416 | bytes 18878464 | tf_op jit(solution)/shard_map/rgp,pd->rgd/dot_general | solution.py:19
  140.3 1.8 fusion.5
  142.1 0.0 all-reduce.2.cloned.1.call-update
  142.1 8.6 %fusion.1 = f32[128,8]{0,1:T(8,128)S(1)} fusion(f32[128,8,4096]{2,0,1:T(8,128)} %get-tuple-element.11, f32[128,8]{0,1:T(8,128)S(1)} %pmax.7), kind=kLoop, calls=%fused_computation.5 | loop fusion | flops 12581888 | bytes 16785408 | tf_op jit(solution)/shard_map/reduce_sum | solution.py:94
  150.8 36.7 %psum.15 = f32[128,8]{0,1:T(8,128)S(1)} all-reduce(f32[128,8]{0,1:T(8,128)S(1)} %add.47), channel_id=1, replica_groups=mesh['grp'=16,'zq'=4,'w'=8] {'grp'}, use_global_device_ids=true, to_apply=%region_6.7 | all-reduce | flops 1024 | bytes 8192 | tf_op jit(solution)/shard_map/psum | solution.py:96
  187.4 109.1 %all-reduce.2.cloned.1.call-done = f32[128,8,128]{2,0,1:T(8,128)} async-done(((f32[128,8,128]{2,0,1:T(8,128)}), f32[128,8,128]{2,0,1:T(8,128)}) %all-reduce.2.cloned.1.call-update) | async-done | bytes 524304 | tf_op jit(solution)/shard_map/psum | solution.py:96
  296.6 1.2 broadcast_divide_fusion
  297.8 0.2 copy.24
  298.0 0.4 copy.25
  298.4 12.6 %all_to_all.28 = f32[128,1,1024]{2,1,0:T(1,128)S(1)} all-to-all(f32[128,1,1024]{2,1,0:T(1,128)S(1)} %copy.25), channel_id=1, replica_groups=mesh['grp'=16,'zq'=4,'w'=8] {'w'}, dimensions={0} | all-to-all | bytes 1048576 | tf_op jit(solution)/shard_map/all_to_all | solution.py:100
  311.0 0.1 copy.28
  311.1 0.8 copy.32
  (10 shorter events, 0.1 us)
Async XLA Ops:
  6.5 67.8 %all-gather.5.cloned.1.call-start = ((), (), s32[]{:S(2)}) async-start(), calls=%async_computation.3 | async-start | bytes 1320960 | tf_op jit(solution)/shard_map/all_gather | solution.py:64
  32.9 92.2 %all-gather.7.cloned.1.call-start = ((), (), s32[]{:S(2)}) async-start(), calls=%async_computation.4 | async-start | bytes 1320960 | tf_op jit(solution)/shard_map/all_gather | solution.py:65
  33.8 262.7 %all-reduce.2.cloned.1.call-start = ((), (), s32[]{:S(2)}) async-start(), calls=%async_computation.2 | async-start | bytes 1048576 | tf_op jit(solution)/shard_map/psum | solution.py:96
  125.1 10.9 %copy-start = (f32[128,8,4096]{2,0,1:T(8,128)S(1)}, f32[128,8,4096]{2,0,1:T(8,128)}, u32[]{:S(2)}) copy-start(f32[128,8,4096]{2,0,1:T(8,128)} %get-tuple-element.11) | copy-start | bytes 50331652
Sparse Core Ops, SparseCore 0:
  33.0 41.2 all-gather.4
  76.4 36.4 all-gather.6
  142.2 154.2 all-reduce.1

commit v2 on v1

--- a/solution.py
+++ b/solution.py
@@ -87,14 +87,34 @@
     visible = visible[:, None, :]
     masked_draft = jnp.where(visible, scores_draft, -jnp.inf)
     peak = jnp.maximum(jnp.max(scores_prefix, axis=2), jnp.max(masked_draft, axis=2))
-    peak = lax.pmax(peak, "grp")
 
     weights_prefix = jnp.exp(scores_prefix - peak[..., None])
     weights_draft = jnp.where(visible, jnp.exp(masked_draft - peak[..., None]), 0.0)
     totals = jnp.sum(weights_prefix, axis=2) + jnp.sum(weights_draft, axis=2)
     summed = split_product(weights_prefix, prefix_v) + split_product(weights_draft, draft_v)
-    summed, totals = lax.psum((summed, totals), "grp")
-    attended = summed / totals[..., None]
+
+    groups = lax.axis_size("grp")
+    slice_rows = block_rows // groups
+    packed = jnp.concatenate(
+        [
+            summed.reshape(groups, -1),
+            peak.reshape(groups, -1),
+            totals.reshape(groups, -1),
+        ],
+        axis=1,
+    )
+    parts = lax.all_to_all(packed, "grp", 0, 0, tiled=True)
+    sum_size = slice_rows * group_heads * HD
+    head_size = slice_rows * group_heads
+    part_sums = parts[:, :sum_size].reshape(groups, slice_rows, group_heads, HD)
+    part_peaks = parts[:, sum_size : sum_size + head_size].reshape(groups, slice_rows, group_heads)
+    part_totals = parts[:, sum_size + head_size :].reshape(groups, slice_rows, group_heads)
+    joined = jnp.max(part_peaks, axis=0)
+    scales = jnp.exp(part_peaks - joined[None])
+    merged_totals = jnp.sum(part_totals * scales, axis=0)
+    merged_sums = jnp.sum(part_sums * scales[..., None], axis=0)
+    attended = (merged_sums / merged_totals[..., None]).reshape(slice_rows, group_heads * HD)
+    attended = lax.all_gather(attended, "grp", axis=0, tiled=True)
 
     attended = attended.reshape(block_rows, 1, group_heads * HD)
     attended = lax.all_to_all(attended, "w", 0, 1, tiled=True)

time: 320 us -> 241 us (0.75)
  waiting for transfers between devices: 149 us -> 67.8 us
  blocking collectives: 106 us -> 97.4 us
  other arithmetic: 14.9 us -> 19.7 us
  local copies, waits for them, and re-layouts: 11.6 us -> 15.6 us
    psum x1 -> x0, waiting for transfers between devices: 109 us -> none  [local(): summed, totals = lax.psum((summed, totals), 'grp')]
    all_gather x0 -> x1, blocking collectives: none -> 41.5 us  [local(): attended = lax.all_gather(attended, 'grp', axis=0, tiled=True)]
    pmax x1 -> x0, blocking collectives: 40.5 us -> none  [local(): peak = lax.pmax(peak, 'grp')]
    psum x1 -> x0, blocking collectives: 36.7 us -> none  [local(): summed, totals = lax.psum((summed, totals), 'grp')]
    all_gather x1, waiting for transfers between devices: 0.02 us -> 28.3 us  [local(): values_all = lax.all_gather(values_here, 'zq', axis=0)]
    all_to_all x0 -> x1, blocking collectives: none -> 26.5 us  [local(): parts = lax.all_to_all(packed, 'grp', 0, 0, tiled=True)]
    reduce_sum x0 -> x2, other arithmetic: none -> 4.3 us  [the longest x1 3.34 us: local(): merged_sums = jnp.sum(part_sums * scales[..., None], axis=0)]
    all_to_all x0 -> x2, local copies, waits for them, and re-layouts: none -> 3.72 us  [local(): parts = lax.all_to_all(packed, 'grp', 0, 0, tiled=True)]
  transfers between devices with their start and end apart: 3 -> 2, of which waited for: 2 -> 2; matrix products, arithmetic and copies ran while one was open for 7% -> 5% of each run, Pallas kernels for 0% -> 0%
where the time goes in v2:
time: 241 us; the launch traced here: 240 us
  blocking collectives  97.4 us (40%)
  waiting for transfers between devices  67.8 us (28%)
  matrix products  26.1 us (11%)
  other arithmetic  19.7 us (8%)
  local copies, waits for them, and re-layouts  15.6 us (6%)
  between operations  13.7 us (6%)
    all_gather x1, blocking collectives, local(): attended = lax.all_gather(attended, 'grp', axis=0, tiled=True)  41.5 us
    all_gather x1, waiting for transfers between devices, local(): keys_all = lax.all_gather(keys_here, 'zq', axis=0)  39.5 us
    all_gather x1, waiting for transfers between devices, local(): values_all = lax.all_gather(values_here, 'zq', axis=0)  28.3 us
    all_to_all x1, blocking collectives, local(): parts = lax.all_to_all(packed, 'grp', 0, 0, tiled=True)  26.5 us
    all_to_all x1, blocking collectives, local(): got = lax.all_to_all(send, 'w', 0, 0, tiled=True)  16.2 us
    all_to_all x1, blocking collectives, local(): attended = lax.all_to_all(attended, 'w', 0, 1, tiled=True)  13.2 us
    dot_general x2, matrix products, split_product(): jnp.einsum(spec, low, values, preferred_element_type=jnp.float32)  8.93 us
    reduce_sum x2, other arithmetic, local(): totals = jnp.sum(weights_prefix, axis=2) + jnp.sum(weights_draft, axis=2)  8.66 us
  transfers between devices with their start and end apart: 2, of which 2 were waited for; matrix products, arithmetic and copies ran while one was open for 5% of the time, Pallas kernels for 0%

profile of v2, /device:TPU:6, one launch (start us, length us, event | category | flops | bytes accessed | tf_op | source)
XLA Modules:
  0.0 240.4 jit_solution(10505051737952480475)
XLA Ops:
  6.5 0.0 all-gather.5.cloned.1.call-start
  6.5 1.1 copy.46
  7.7 1.0 copy.47
  8.7 1.0 copy.48
  9.7 0.7 reduce.3
  10.4 0.7 reduce.4
  11.2 0.5 broadcast.49
  11.7 1.2 reduce.5
  12.9 0.2 reshape.179
  13.1 16.2 %all_to_all.39 = bf16[8,2,24704]{2,1,0:T(2,128)(2,1)S(1)} all-to-all(bf16[8,2,24704]{2,1,0:T(2,128)(2,1)S(1)} %reshape.179), channel_id=1, replica_groups=mesh['grp'=16,'zq'=4,'w'=8] {'w'}, dimensions={0} | all-to-all | bytes 1581056 | tf_op jit(solution)/shard_map/all_to_all | solution.py:42
  29.4 2.5 %reshape.180 = bf16[8,1,49408]{2,1,0:T(2,128)(2,1)S(1)} reshape(bf16[8,2,24704]{2,1,0:T(2,128)(2,1)S(1)} %all_to_all.39) | data formatting | bytes 1581056
  31.8 0.1 copy.60
  31.9 0.1 fusion.30
  32.0 0.1 reshape.161
  32.1 0.7 pad_maximum_fusion
  32.9 0.0 all-gather.5.cloned.1.call-update
  32.9 0.0 all-gather.7.cloned.1.call-start
  32.9 0.1 reshape.164
  33.1 0.7 pad_maximum_fusion.1
  33.8 0.0 all-gather.7.cloned.1.call-update
  33.8 0.8 dynamic-slice_subtract_fusion
  34.6 0.1 compare_and_fusion
  34.7 0.1 reshape.160
  34.8 39.5 %all-gather.5.cloned.1.call-done = bf16[4128,128]{1,0:T(8,128)(2,1)} async-done(((bf16[1032,128]{1,0:T(8,128)(2,1)}), bf16[4128,128]{1,0:T(8,128)(2,1)}) %all-gather.5.cloned.1.call-update) | async-done | bytes 1056784 | tf_op jit(solution)/shard_map/all_gather | solution.py:64
  74.3 1.3 slice.51
  75.6 0.9 fusion.32
  76.5 8.1 %multiply_reduce_fusion = (f32[128,8]{0,1:T(8,128)S(1)}, f32[128,8,4096]{2,0,1:T(8,128)}) fusion(bf16[4096,128,1]{1,0,2:T(8,128)(2,1)S(1)} %bitcast.73, bf16[128,8,128]{2,1,0:T(8,128)(2,1)S(1)} %reshape.160), kind=kOutput, calls=%fused_computation.4 | convolution fusion | flops 1082129408 | bytes 18092032 | tf_op jit(solution)/shard_map/rgd,pd->rgp/dot_general | solution.py:72
  84.6 28.3 %all-gather.7.cloned.1.call-done = bf16[4128,128]{1,0:T(8,128)(2,1)} async-done(((bf16[1032,128]{1,0:T(8,128)(2,1)}), bf16[4128,128]{1,0:T(8,128)(2,1)}) %all-gather.7.cloned.1.call-update) | async-done | bytes 1056784 | tf_op jit(solution)/shard_map/all_gather | solution.py:65
  112.9 1.0 fusion.17
  113.9 1.3 slice.55
  115.2 0.1 copy.38
  115.3 8.6 %fusion.1 = f32[128,8]{0,1:T(8,128)S(1)} fusion(f32[128,8,4096]{2,0,1:T(8,128)} %get-tuple-element.11, f32[128,8]{0,1:T(8,128)S(1)} %max.11), kind=kLoop, calls=%fused_computation.5 | loop fusion | flops 12581888 | bytes 16785408 | tf_op jit(solution)/shard_map/reduce_sum | solution.py:93
  123.9 0.1 copy.39
  124.0 0.1 add.48
  124.1 7.3 %fusion.2 = f32[128,8,128]{2,0,1:T(8,128)S(1)} fusion(bf16[4096,128,1]{1,0,2:T(8,128)(2,1)S(1)} %bitcast.82, f32[128,8,4096]{2,0,1:T(8,128)} %get-tuple-element.11, f32[128,8]{0,1:T(8,128)S(1)} %max.11), kind=kOutput, calls=%fused_computation.6 | convolution fusion | flops 1090519040 | bytes 18354176 | tf_op jit(solution)/shard_map/rgp,pd->rgd/dot_general | solution.py:19
  131.4 8.0 %fusion.7 = f32[128,8,128]{2,0,1:T(8,128)S(1)} fusion(f32[128,8,128]{2,0,1:T(8,128)S(1)} %fusion.2, bf16[4096,128,1]{1,0,2:T(8,128)(2,1)S(1)} %bitcast.83, f32[128,8,4096]{2,0,1:T(8,128)} %get-tuple-element.11, f32[128,8]{0,1:T(8,128)S(1)} %max.11), kind=kOutput, calls=%fused_computation.12 | convolution fusion | flops 1094844416 | bytes 18878464 | tf_op jit(solution)/shard_map/rgp,pd->rgd/dot_general | solution.py:19
  139.4 1.0 fusion.6
  140.3 0.3 copy.37
  140.7 0.1 reshape.167
  140.8 0.1 max.12
  140.8 0.1 concatenate.15
  140.9 0.5 copy.40
  141.5 26.5 %all_to_all.40 = f32[16,1,8320]{2,1,0:T(1,128)S(1)} all-to-all(f32[16,1,8320]{2,1,0:T(1,128)S(1)} %copy.40), channel_id=1, replica_groups=mesh['grp'=16,'zq'=4,'w'=8] {'grp'}, dimensions={0} | all-to-all | bytes 1064960 | tf_op jit(solution)/shard_map/all_to_all | solution.py:106
  168.0 3.2 %copy.41 = f32[16,1,8320]{0,2,1:T(8,128)} copy(f32[16,1,8320]{2,1,0:T(1,128)S(1)} %all_to_all.40) | data formatting | bytes 1064960 | tf_op jit(solution)/shard_map/all_to_all | solution.py:106
  171.1 0.9 slice_reduce_fusion
  172.0 1.0 fusion.24
  173.0 0.1 sub.51
  173.0 0.1 div.13
  173.1 0.1 copy.42
  173.2 0.9 fusion.25
  174.1 3.3 %fusion.5 = f32[8192]{0:T(1024)S(1)} fusion(f32[16,8320]{0,1:T(8,128)} %bitcast.72, f32[16,8,8]{0,2,1:T(8,128)S(1)} %fusion.25), kind=kLoop, calls=%fused_computation.9 | loop fusion | flops 253952 | bytes 561152 | tf_op jit(solution)/shard_map/reduce_sum | solution.py:115
  177.4 0.1 bitcast_divide_fusion
  177.5 41.5 %all_gather.19 = f32[128,1024]{1,0:T(8,128)S(1)} all-gather(f32[8,1024]{1,0:T(8,128)S(1)} %bitcast_divide_fusion), channel_id=1, replica_groups=mesh['grp'=16,'zq'=4,'w'=8] {'grp'}, dimensions={0}, use_global_device_ids=true | all-gather | bytes 557056 | tf_op jit(solution)/shard_map/all_gather | solution.py:117
  219.0 0.4 reshape.169
  219.4 13.2 %all_to_all.41 = f32[128,1,1024]{2,1,0:T(1,128)S(1)} all-to-all(f32[128,1,1024]{2,1,0:T(1,128)S(1)} %reshape.169), channel_id=1, replica_groups=mesh['grp'=16,'zq'=4,'w'=8] {'w'}, dimensions={0} | all-to-all | bytes 1048576 | tf_op jit(solution)/shard_map/all_to_all | solution.py:120
  232.6 0.1 copy.45
  232.7 0.8 copy.49
  (11 shorter events, 0.1 us)
Async XLA Ops:
  6.5 67.8 %all-gather.5.cloned.1.call-start = ((), (), s32[]{:S(2)}) async-start(), calls=%async_computation.3 | async-start | bytes 1320960 | tf_op jit(solution)/shard_map/all_gather | solution.py:64
  32.9 80.0 %all-gather.7.cloned.1.call-start = ((), (), s32[]{:S(2)}) async-start(), calls=%async_computation.4 | async-start | bytes 1320960 | tf_op jit(solution)/shard_map/all_gather | solution.py:65
Sparse Core Ops, SparseCore 0:
  33.0 41.2 all-gather.4
  76.4 36.4 all-gather.6

commit v3 on v2

--- a/solution.py
+++ b/solution.py
@@ -32,41 +32,32 @@
     inverse_root = 1.0 / math.sqrt(HD)
 
     query_heads = queries.reshape(rows, KV, group_heads * HD).transpose(1, 0, 2).reshape(KV, -1)
-    key_heads = prefix_keys.reshape(positions, KV, HD).transpose(1, 0, 2).reshape(KV, -1)
-    value_heads = prefix_values.reshape(positions, KV, HD).transpose(1, 0, 2).reshape(KV, -1)
-    draft_key_heads = draft_keys.reshape(KV, HD)
-    draft_value_heads = draft_values.reshape(KV, HD)
+    key_heads = jnp.concatenate(
+        [prefix_keys.reshape(positions, KV, HD).transpose(1, 0, 2), draft_keys.reshape(KV, 1, HD)],
+        axis=1,
+    ).reshape(KV, -1)
+    value_heads = jnp.concatenate(
+        [prefix_values.reshape(positions, KV, HD).transpose(1, 0, 2), draft_values.reshape(KV, 1, HD)],
+        axis=1,
+    ).reshape(KV, -1)
+    own_quarter = (lax.iota(jnp.int32, quarters) == quarter)[:, None, None]
+    query_send = jnp.where(own_quarter, query_heads[None], jnp.zeros_like(query_heads)[None])
+    kv_send = jnp.concatenate([key_heads, value_heads], axis=1)
     send = jnp.concatenate(
-        [query_heads, key_heads, draft_key_heads, value_heads, draft_value_heads], axis=1
-    )
-    got = lax.all_to_all(send, "w", 0, 0, tiled=True)
+        [query_send, jnp.broadcast_to(kv_send[None], (quarters,) + kv_send.shape)], axis=2
+    ).reshape(quarters * KV, -1)
+    got = lax.all_to_all(send, ("zq", "w"), 0, 0, tiled=True)
 
     query_size = rows * group_heads * HD
-    key_size = positions * HD
-    cut = [query_size, key_size, HD, key_size, HD]
-    starts = [sum(cut[:n]) for n in range(len(cut))]
-    query_block = got[:, : query_size].reshape(ways * rows, group_heads, HD)
-    keys_here = jnp.concatenate(
-        [
-            got[:, starts[1] : starts[1] + key_size].reshape(ways * positions, HD),
-            got[:, starts[2] : starts[2] + HD],
-        ],
-        axis=0,
-    )
-    values_here = jnp.concatenate(
-        [
-            got[:, starts[3] : starts[3] + key_size].reshape(ways * positions, HD),
-            got[:, starts[4] : starts[4] + HD],
-        ],
-        axis=0,
-    )
-    local_keys = ways * positions
-    keys_all = lax.all_gather(keys_here, "zq", axis=0)
-    values_all = lax.all_gather(values_here, "zq", axis=0)
-    prefix_k = keys_all[:, :local_keys].reshape(-1, HD)
-    draft_k = keys_all[:, local_keys:].reshape(-1, HD)
-    prefix_v = values_all[:, :local_keys].reshape(-1, HD)
-    draft_v = values_all[:, local_keys:].reshape(-1, HD)
+    key_size = (positions + 1) * HD
+    query_block = lax.dynamic_slice_in_dim(got[:, :query_size], quarter * ways, ways, axis=0)
+    query_block = query_block.reshape(ways * rows, group_heads, HD)
+    keys_all = got[:, query_size : query_size + key_size].reshape(quarters * ways, positions + 1, HD)
+    values_all = got[:, query_size + key_size :].reshape(quarters * ways, positions + 1, HD)
+    prefix_k = keys_all[:, :positions].reshape(-1, HD)
+    draft_k = keys_all[:, positions]
+    prefix_v = values_all[:, :positions].reshape(-1, HD)
+    draft_v = values_all[:, positions]
 
     block_rows = ways * rows
     scores_prefix = jnp.einsum(
@@ -114,7 +105,8 @@
     merged_totals = jnp.sum(part_totals * scales, axis=0)
     merged_sums = jnp.sum(part_sums * scales[..., None], axis=0)
     attended = (merged_sums / merged_totals[..., None]).reshape(slice_rows, group_heads * HD)
-    attended = lax.all_gather(attended, "grp", axis=0, tiled=True)
+    attended = jnp.broadcast_to(attended[None], (groups,) + attended.shape)
+    attended = lax.all_to_all(attended, "grp", 0, 0, tiled=True)
 
     attended = attended.reshape(block_rows, 1, group_heads * HD)
     attended = lax.all_to_all(attended, "w", 0, 1, tiled=True)

time: 241 us -> 229 us (0.950)
  blocking collectives: 97.4 us -> 59.3 us
  local copies, waits for them, and re-layouts: 15.6 us -> 37.5 us
  between operations: 13.7 us -> 0.27 us
  starting transfers between devices: 0.04 us -> 11.9 us
  waiting for transfers between devices: 67.8 us -> 71.5 us
    all_to_all x0 -> x1, waiting for transfers between devices: none -> 71.5 us  [local(): got = lax.all_to_all(send, ('zq', 'w'), 0, 0, tiled=True)]
    all_gather x2 -> x0, waiting for transfers between devices: 67.8 us -> none  [the longest x1 39.5 us: local(): keys_all = lax.all_gather(keys_here, 'zq', axis=0)]
    all_gather x1 -> x0, blocking collectives: 41.5 us -> none  [local(): attended = lax.all_gather(attended, 'grp', axis=0, tiled=True)]
    unnamed x12 -> x8, local copies, waits for them, and re-layouts: 6.85 us -> 27.6 us
    all_to_all x0 -> x1, starting transfers between devices: none -> 11.9 us  [local(): got = lax.all_to_all(send, ('zq', 'w'), 0, 0, tiled=True)]
    all_to_all x1 -> x2, other arithmetic: 1.23 us -> 3.99 us  [local(): got = lax.all_to_all(send, ('zq', 'w'), 0, 0, tiled=True)]
    all_to_all x1, blocking collectives: 16.2 us -> 18.9 us  [local(): attended = lax.all_to_all(attended, 'grp', 0, 0, tiled=True)]
  transfers between devices with their start and end apart: 2 -> 1, of which waited for: 2 -> 1; matrix products, arithmetic and copies ran while one was open for 5% -> 0% of each run, Pallas kernels for 0% -> 0%
where the time goes in v3:
time: 229 us; the launch traced here: 226 us
  waiting for transfers between devices  71.5 us (31%)
  blocking collectives  59.3 us (26%)
  local copies, waits for them, and re-layouts  37.5 us (16%)
  matrix products  24.2 us (11%)
  other arithmetic  21.3 us (9%)
  starting transfers between devices  11.9 us (5%)
    all_to_all x1, waiting for transfers between devices, local(): got = lax.all_to_all(send, ('zq', 'w'), 0, 0, tiled=True)  71.5 us
    unnamed x8, local copies, waits for them, and re-layouts  27.6 us
    all_to_all x1, blocking collectives, local(): parts = lax.all_to_all(packed, 'grp', 0, 0, tiled=True)  27.1 us
    all_to_all x1, blocking collectives, local(): attended = lax.all_to_all(attended, 'grp', 0, 0, tiled=True)  18.9 us
    all_to_all x1, blocking collectives, local(): attended = lax.all_to_all(attended, 'w', 0, 1, tiled=True)  13.2 us
    all_to_all x1, starting transfers between devices, local(): got = lax.all_to_all(send, ('zq', 'w'), 0, 0, tiled=True)  11.9 us
    reduce_sum x2, other arithmetic, local(): totals = jnp.sum(weights_prefix, axis=2) + jnp.sum(weights_draft, axis=2)  8.66 us
    dot_general x2, matrix products, split_product(): jnp.einsum(spec, low, values, preferred_element_type=jnp.float32)  8.41 us
  transfers between devices with their start and end apart: 1, of which 1 were waited for; matrix products, arithmetic and copies ran while one was open for 0% of the time, Pallas kernels for 0%

profile of v3, /device:TPU:6, one launch (start us, length us, event | category | flops | bytes accessed | tf_op | source)
XLA Modules:
  0.0 226.0 jit_solution(1543386949448938268)
XLA Ops:
  0.0 0.1 broadcast_in_dim.72
  0.1 0.1 broadcast_in_dim.73
  0.2 0.7 reduce.3
  0.9 0.7 reduce.4
  1.6 1.1 copy.58
  2.7 1.0 copy.59
  3.7 1.0 copy.60
  4.7 0.1 maximum_bitcast_fusion.1
  4.8 0.1 broadcast_bitcast_fusion
  4.9 0.1 bitcast_select_fusion
  5.1 0.2 maximum_bitcast_fusion
  5.3 0.5 broadcast.63
  5.8 3.8 %reduce.5 = bf16[32,49408]{1,0:T(8,128)(2,1)} reduce(bf16[32,1,49408]{2,0,1:T(8,128)(2,1)S(1)} %maximum_bitcast_fusion, bf16[]{:T(256)} %broadcast.63), dimensions={1}, to_apply=%copy.42.reduce_sub_computation | reduce | bytes 6324226 | tf_op jit(solution)/shard_map/all_to_all | solution.py:49
  9.6 4.6 %reshape.185 = bf16[32,2,24704]{2,1,0:T(2,128)(2,1)} reshape(bf16[32,49408]{1,0:T(8,128)(2,1)} %reduce.5) | data formatting | bytes 6324224
  14.2 11.9 %all-to-all-start = ((bf16[32,2,24704]{2,1,0:T(2,128)(2,1)}), bf16[32,2,24704]{2,1,0:T(2,128)(2,1)S(1)}, u32[]{:S(2)}, u32[]{:S(2)}) async-start(bf16[32,2,24704]{2,1,0:T(2,128)(2,1)} %reshape.185), calls=%async_computation | async-start | bytes 6324224 | tf_op jit(solution)/shard_map/all_to_all | solution.py:49
  26.2 0.8 dynamic-slice_subtract_fusion
  26.9 0.1 compare_and_fusion
  27.0 71.5 %all-to-all-done = bf16[32,2,24704]{2,1,0:T(2,128)(2,1)S(1)} async-done(((bf16[32,2,24704]{2,1,0:T(2,128)(2,1)}), bf16[32,2,24704]{2,1,0:T(2,128)(2,1)S(1)}, u32[]{:S(2)}, u32[]{:S(2)}) %all-to-all-start) | async-done | bytes 3162144 | tf_op jit(solution)/shard_map/all_to_all | solution.py:49
  98.5 15.9 %reshape.186 = bf16[32,1,49408]{2,1,0:T(2,128)(2,1)} reshape(bf16[32,2,24704]{2,1,0:T(2,128)(2,1)S(1)} %all-to-all-done) | data formatting | bytes 6324224
  114.4 3.1 %copy.79 = bf16[32,1,49408]{2,0,1:T(8,128)(2,1)S(1)} copy(bf16[32,1,49408]{2,1,0:T(2,128)(2,1)} %reshape.186) | data formatting | bytes 6324224
  117.5 1.1 slice.40
  118.6 0.1 fusion.30
  118.7 0.5 reshape.171
  119.3 0.1 slice.42
  119.4 0.5 reshape.173
  120.0 0.1 slice.45
  120.1 1.0 constant_dynamic-slice_fusion
  121.1 0.1 reshape.170
  121.2 8.1 %multiply_reduce_fusion = (f32[128,8]{0,1:T(8,128)S(1)}, f32[128,8,4096]{2,0,1:T(8,128)}) fusion(bf16[4096,128,1]{1,0,2:T(8,128)(2,1)S(1)} %bitcast.74, bf16[128,8,128]{2,1,0:T(8,128)(2,1)S(1)} %reshape.170), kind=kOutput, calls=%fused_computation.4 | convolution fusion | flops 1082129408 | bytes 18092032 | tf_op jit(solution)/shard_map/rgd,pd->rgp/dot_general | solution.py:63
  129.3 0.2 fusion.31
  129.5 0.1 copy.48
  129.7 8.6 %fusion.1 = f32[128,8]{0,1:T(8,128)S(1)} fusion(f32[128,8,4096]{2,0,1:T(8,128)} %get-tuple-element.8, f32[128,8]{0,1:T(8,128)S(1)} %max.11), kind=kLoop, calls=%fused_computation.5 | loop fusion | flops 12581888 | bytes 16785408 | tf_op jit(solution)/shard_map/reduce_sum | solution.py:84
  138.3 0.1 copy.49
  138.4 0.1 add.52
  138.5 0.1 max.12
  138.6 0.3 fusion.17
  138.8 7.3 %fusion.2 = f32[128,8,128]{2,0,1:T(8,128)S(1)} fusion(bf16[4096,128,1]{1,0,2:T(8,128)(2,1)S(1)} %bitcast.78, f32[128,8,4096]{2,0,1:T(8,128)} %get-tuple-element.8, f32[128,8]{0,1:T(8,128)S(1)} %max.11), kind=kOutput, calls=%fused_computation.6 | convolution fusion | flops 1090519040 | bytes 18354176 | tf_op jit(solution)/shard_map/rgp,pd->rgd/dot_general | solution.py:19
  146.1 8.1 %fusion.7 = f32[128,8,128]{2,0,1:T(8,128)S(1)} fusion(f32[128,8,128]{2,0,1:T(8,128)S(1)} %fusion.2, bf16[4096,128,1]{1,0,2:T(8,128)(2,1)S(1)} %bitcast.79, f32[128,8,4096]{2,0,1:T(8,128)} %get-tuple-element.8, f32[128,8]{0,1:T(8,128)S(1)} %max.11), kind=kOutput, calls=%fused_computation.14 | convolution fusion | flops 1094844416 | bytes 18878464 | tf_op jit(solution)/shard_map/rgp,pd->rgd/dot_general | solution.py:19
  154.2 0.3 fusion.6
  154.5 0.3 copy.47
  154.9 0.1 reshape.175
  155.0 0.1 concatenate.23
  155.0 0.5 copy.50
  155.6 27.1 %all_to_all.44 = f32[16,1,8320]{2,1,0:T(1,128)S(1)} all-to-all(f32[16,1,8320]{2,1,0:T(1,128)S(1)} %copy.50), channel_id=1, replica_groups=mesh['grp'=16,'zq'=4,'w'=8] {'grp'}, dimensions={0} | all-to-all | bytes 1064960 | tf_op jit(solution)/shard_map/all_to_all | solution.py:97
  182.7 3.2 %copy.51 = f32[16,1,8320]{0,2,1:T(8,128)} copy(f32[16,1,8320]{2,1,0:T(1,128)S(1)} %all_to_all.44) | data formatting | bytes 1064960 | tf_op jit(solution)/shard_map/all_to_all | solution.py:97
  185.9 0.9 slice_reduce_fusion
  186.8 1.0 fusion.24
  187.7 0.1 sub.51
  187.8 0.1 div.16
  187.9 0.1 copy.52
  188.0 0.9 fusion.25
  188.8 3.3 %fusion.5 = f32[8192]{0:T(1024)S(1)} fusion(f32[16,8320]{0,1:T(8,128)} %bitcast.71, f32[16,8,8]{0,2,1:T(8,128)S(1)} %fusion.25), kind=kLoop, calls=%fused_computation.9 | loop fusion | flops 253952 | bytes 561152 | tf_op jit(solution)/shard_map/reduce_sum | solution.py:106
  192.2 0.1 bitcast_divide_fusion
  192.3 18.9 %all_to_all.45 = f32[16,8,1024]{2,1,0:T(8,128)S(1)} all-to-all(f32[16,8,1024]{2,1,0:T(8,128)S(1)} %broadcast_in_dim.83), channel_id=1, replica_groups=mesh['grp'=16,'zq'=4,'w'=8] {'grp'}, dimensions={0} | all-to-all | bytes 1048576 | tf_op jit(solution)/shard_map/all_to_all | solution.py:109
  211.2 0.6 reshape.177
  211.9 13.2 %all_to_all.46 = f32[128,1,1024]{2,1,0:T(1,128)S(1)} all-to-all(f32[128,1,1024]{2,1,0:T(1,128)S(1)} %reshape.177), channel_id=1, replica_groups=mesh['grp'=16,'zq'=4,'w'=8] {'w'}, dimensions={0} | all-to-all | bytes 1048576 | tf_op jit(solution)/shard_map/all_to_all | solution.py:112
  225.1 0.1 copy.55
  225.2 0.8 copy.61
  (10 shorter events, 0.2 us)
Async XLA Ops:
  14.2 84.3 %all-to-all-start = ((bf16[32,2,24704]{2,1,0:T(2,128)(2,1)}), bf16[32,2,24704]{2,1,0:T(2,128)(2,1)S(1)}, u32[]{:S(2)}, u32[]{:S(2)}) async-start(bf16[32,2,24704]{2,1,0:T(2,128)(2,1)} %reshape.185), calls=%async_computation | async-start | bytes 6324224 | tf_op jit(solution)/shard_map/all_to_all | solution.py:49

commit v4 on v2

--- a/solution.py
+++ b/solution.py
@@ -114,7 +114,8 @@
     merged_totals = jnp.sum(part_totals * scales, axis=0)
     merged_sums = jnp.sum(part_sums * scales[..., None], axis=0)
     attended = (merged_sums / merged_totals[..., None]).reshape(slice_rows, group_heads * HD)
-    attended = lax.all_gather(attended, "grp", axis=0, tiled=True)
+    attended = jnp.broadcast_to(attended[None], (groups,) + attended.shape)
+    attended = lax.all_to_all(attended, "grp", 0, 0, tiled=True)
 
     attended = attended.reshape(block_rows, 1, group_heads * HD)
     attended = lax.all_to_all(attended, "w", 0, 1, tiled=True)

time: 241 us -> 221 us (0.917)
  blocking collectives: 97.4 us -> 74.8 us
    all_gather x1 -> x0, blocking collectives: 41.5 us -> none  [local(): attended = lax.all_gather(attended, 'grp', axis=0, tiled=True)]
    all_to_all x0 -> x1, blocking collectives: none -> 18.7 us  [local(): attended = lax.all_to_all(attended, 'grp', 0, 0, tiled=True)]
  transfers between devices with their start and end apart: 2 -> 2, of which waited for: 2 -> 2; matrix products, arithmetic and copies ran while one was open for 5% -> 6% of each run, Pallas kernels for 0% -> 0%
where the time goes in v4:
time: 221 us; the launch traced here: 218 us
  blocking collectives  74.8 us (34%)
  waiting for transfers between devices  67.8 us (31%)
  matrix products  26.1 us (12%)
  other arithmetic  19.7 us (9%)
  local copies, waits for them, and re-layouts  15.9 us (7%)
  between operations  13.7 us (6%)
    all_gather x1, waiting for transfers between devices, local(): keys_all = lax.all_gather(keys_here, 'zq', axis=0)  39.5 us
    all_gather x1, waiting for transfers between devices, local(): values_all = lax.all_gather(values_here, 'zq', axis=0)  28.3 us
    all_to_all x1, blocking collectives, local(): parts = lax.all_to_all(packed, 'grp', 0, 0, tiled=True)  26.5 us
    all_to_all x1, blocking collectives, local(): attended = lax.all_to_all(attended, 'grp', 0, 0, tiled=True)  18.7 us
    all_to_all x1, blocking collectives, local(): got = lax.all_to_all(send, 'w', 0, 0, tiled=True)  16.2 us
    all_to_all x1, blocking collectives, local(): attended = lax.all_to_all(attended, 'w', 0, 1, tiled=True)  13.4 us
    dot_general x2, matrix products, split_product(): jnp.einsum(spec, low, values, preferred_element_type=jnp.float32)  8.93 us
    reduce_sum x2, other arithmetic, local(): totals = jnp.sum(weights_prefix, axis=2) + jnp.sum(weights_draft, axis=2)  8.66 us
  transfers between devices with their start and end apart: 2, of which 2 were waited for; matrix products, arithmetic and copies ran while one was open for 6% of the time, Pallas kernels for 0%

profile of v4, /device:TPU:6, one launch (start us, length us, event | category | flops | bytes accessed | tf_op | source)
XLA Modules:
  0.0 218.1 jit_solution(10301714281055539871)
XLA Ops:
  6.5 0.0 all-gather.5.cloned.1.call-start
  6.5 1.1 copy.46
  7.7 1.0 copy.47
  8.7 1.0 copy.48
  9.7 0.7 reduce.3
  10.4 0.7 reduce.4
  11.2 0.5 broadcast.50
  11.7 1.2 reduce.5
  12.9 0.2 reshape.187
  13.1 16.2 %all_to_all.44 = bf16[8,2,24704]{2,1,0:T(2,128)(2,1)S(1)} all-to-all(bf16[8,2,24704]{2,1,0:T(2,128)(2,1)S(1)} %reshape.187), channel_id=1, replica_groups=mesh['grp'=16,'zq'=4,'w'=8] {'w'}, dimensions={0} | all-to-all | bytes 1581056 | tf_op jit(solution)/shard_map/all_to_all | solution.py:42
  29.4 2.5 %reshape.188 = bf16[8,1,49408]{2,1,0:T(2,128)(2,1)S(1)} reshape(bf16[8,2,24704]{2,1,0:T(2,128)(2,1)S(1)} %all_to_all.44) | data formatting | bytes 1581056
  31.8 0.1 copy.60
  31.9 0.1 fusion.30
  32.0 0.1 reshape.169
  32.1 0.7 pad_maximum_fusion
  32.9 0.0 all-gather.5.cloned.1.call-update
  32.9 0.0 all-gather.7.cloned.1.call-start
  32.9 0.1 reshape.172
  33.1 0.7 pad_maximum_fusion.1
  33.8 0.0 all-gather.7.cloned.1.call-update
  33.8 0.8 dynamic-slice_subtract_fusion
  34.6 0.1 compare_and_fusion
  34.7 0.1 reshape.168
  34.8 39.5 %all-gather.5.cloned.1.call-done = bf16[4128,128]{1,0:T(8,128)(2,1)} async-done(((bf16[1032,128]{1,0:T(8,128)(2,1)}), bf16[4128,128]{1,0:T(8,128)(2,1)}) %all-gather.5.cloned.1.call-update) | async-done | bytes 1056784 | tf_op jit(solution)/shard_map/all_gather | solution.py:64
  74.3 1.3 slice.51
  75.6 0.9 fusion.32
  76.5 8.1 %multiply_reduce_fusion = (f32[128,8]{0,1:T(8,128)S(1)}, f32[128,8,4096]{2,0,1:T(8,128)}) fusion(bf16[4096,128,1]{1,0,2:T(8,128)(2,1)S(1)} %bitcast.73, bf16[128,8,128]{2,1,0:T(8,128)(2,1)S(1)} %reshape.168), kind=kOutput, calls=%fused_computation.4 | convolution fusion | flops 1082129408 | bytes 18092032 | tf_op jit(solution)/shard_map/rgd,pd->rgp/dot_general | solution.py:72
  84.6 28.3 %all-gather.7.cloned.1.call-done = bf16[4128,128]{1,0:T(8,128)(2,1)} async-done(((bf16[1032,128]{1,0:T(8,128)(2,1)}), bf16[4128,128]{1,0:T(8,128)(2,1)}) %all-gather.7.cloned.1.call-update) | async-done | bytes 1056784 | tf_op jit(solution)/shard_map/all_gather | solution.py:65
  112.9 1.0 fusion.17
  113.9 1.3 slice.55
  115.2 0.1 copy.38
  115.3 8.6 %fusion.1 = f32[128,8]{0,1:T(8,128)S(1)} fusion(f32[128,8,4096]{2,0,1:T(8,128)} %get-tuple-element.11, f32[128,8]{0,1:T(8,128)S(1)} %max.11), kind=kLoop, calls=%fused_computation.5 | loop fusion | flops 12581888 | bytes 16785408 | tf_op jit(solution)/shard_map/reduce_sum | solution.py:93
  123.9 0.1 copy.39
  124.1 0.1 add.48
  124.1 7.3 %fusion.2 = f32[128,8,128]{2,0,1:T(8,128)S(1)} fusion(bf16[4096,128,1]{1,0,2:T(8,128)(2,1)S(1)} %bitcast.82, f32[128,8,4096]{2,0,1:T(8,128)} %get-tuple-element.11, f32[128,8]{0,1:T(8,128)S(1)} %max.11), kind=kOutput, calls=%fused_computation.6 | convolution fusion | flops 1090519040 | bytes 18354176 | tf_op jit(solution)/shard_map/rgp,pd->rgd/dot_general | solution.py:19
  131.4 8.0 %fusion.7 = f32[128,8,128]{2,0,1:T(8,128)S(1)} fusion(f32[128,8,128]{2,0,1:T(8,128)S(1)} %fusion.2, bf16[4096,128,1]{1,0,2:T(8,128)(2,1)S(1)} %bitcast.83, f32[128,8,4096]{2,0,1:T(8,128)} %get-tuple-element.11, f32[128,8]{0,1:T(8,128)S(1)} %max.11), kind=kOutput, calls=%fused_computation.12 | convolution fusion | flops 1094844416 | bytes 18878464 | tf_op jit(solution)/shard_map/rgp,pd->rgd/dot_general | solution.py:19
  139.4 1.0 fusion.6
  140.3 0.3 copy.37
  140.7 0.1 reshape.175
  140.8 0.1 max.12
  140.8 0.1 concatenate.15
  140.9 0.5 copy.40
  141.5 26.5 %all_to_all.45 = f32[16,1,8320]{2,1,0:T(1,128)S(1)} all-to-all(f32[16,1,8320]{2,1,0:T(1,128)S(1)} %copy.40), channel_id=1, replica_groups=mesh['grp'=16,'zq'=4,'w'=8] {'grp'}, dimensions={0} | all-to-all | bytes 1064960 | tf_op jit(solution)/shard_map/all_to_all | solution.py:106
  168.0 3.2 %copy.41 = f32[16,1,8320]{0,2,1:T(8,128)} copy(f32[16,1,8320]{2,1,0:T(1,128)S(1)} %all_to_all.45) | data formatting | bytes 1064960 | tf_op jit(solution)/shard_map/all_to_all | solution.py:106
  171.1 0.9 slice_reduce_fusion
  172.0 1.0 fusion.24
  173.0 0.1 sub.51
  173.0 0.1 div.16
  173.1 0.1 copy.42
  173.2 0.9 fusion.25
  174.1 3.3 %fusion.5 = f32[8192]{0:T(1024)S(1)} fusion(f32[16,8320]{0,1:T(8,128)} %bitcast.72, f32[16,8,8]{0,2,1:T(8,128)S(1)} %fusion.25), kind=kLoop, calls=%fused_computation.9 | loop fusion | flops 253952 | bytes 561152 | tf_op jit(solution)/shard_map/reduce_sum | solution.py:115
  177.4 0.1 bitcast_divide_fusion
  177.6 18.7 %all_to_all.46 = f32[16,8,1024]{2,1,0:T(8,128)S(1)} all-to-all(f32[16,8,1024]{2,1,0:T(8,128)S(1)} %broadcast_in_dim.36), channel_id=1, replica_groups=mesh['grp'=16,'zq'=4,'w'=8] {'grp'}, dimensions={0} | all-to-all | bytes 1048576 | tf_op jit(solution)/shard_map/all_to_all | solution.py:118
  196.3 0.6 reshape.177
  196.9 13.4 %all_to_all.47 = f32[128,1,1024]{2,1,0:T(1,128)S(1)} all-to-all(f32[128,1,1024]{2,1,0:T(1,128)S(1)} %reshape.177), channel_id=1, replica_groups=mesh['grp'=16,'zq'=4,'w'=8] {'w'}, dimensions={0} | all-to-all | bytes 1048576 | tf_op jit(solution)/shard_map/all_to_all | solution.py:121
  210.3 0.1 copy.45
  210.4 0.8 copy.49
  (12 shorter events, 0.2 us)
Async XLA Ops:
  6.5 67.8 %all-gather.5.cloned.1.call-start = ((), (), s32[]{:S(2)}) async-start(), calls=%async_computation.4 | async-start | bytes 1320960 | tf_op jit(solution)/shard_map/all_gather | solution.py:64
  32.9 80.0 %all-gather.7.cloned.1.call-start = ((), (), s32[]{:S(2)}) async-start(), calls=%async_computation.5 | async-start | bytes 1320960 | tf_op jit(solution)/shard_map/all_gather | solution.py:65
Sparse Core Ops, SparseCore 0:
  33.0 41.2 all-gather.4
  76.4 36.4 all-gather.6

commit v5 on v4

--- a/solution.py
+++ b/solution.py
@@ -61,8 +61,8 @@
         axis=0,
     )
     local_keys = ways * positions
-    keys_all = lax.all_gather(keys_here, "zq", axis=0)
-    values_all = lax.all_gather(values_here, "zq", axis=0)
+    both_all = lax.all_gather(jnp.stack([keys_here, values_here]), "zq", axis=0)
+    keys_all, values_all = both_all[:, 0], both_all[:, 1]
     prefix_k = keys_all[:, :local_keys].reshape(-1, HD)
     draft_k = keys_all[:, local_keys:].reshape(-1, HD)
     prefix_v = values_all[:, :local_keys].reshape(-1, HD)

time: 221 us -> 206 us (0.932)
  waiting for transfers between devices: 67.8 us -> 56.5 us
    all_gather x2 -> x1, waiting for transfers between devices: 67.8 us -> 56.5 us  [local(): both_all = lax.all_gather(jnp.stack([keys_here, values_here]), 'zq', axis=0)]
  transfers between devices with their start and end apart: 2 -> 1, of which waited for: 2 -> 1; matrix products, arithmetic and copies ran while one was open for 6% -> 0% of each run, Pallas kernels for 0% -> 0%
where the time goes in v5:
time: 206 us; the launch traced here: 204 us
  blocking collectives  75.4 us (37%)
  waiting for transfers between devices  56.5 us (27%)
  matrix products  24.2 us (12%)
  other arithmetic  19.1 us (9%)
  local copies, waits for them, and re-layouts  15.1 us (7%)
  between operations  13.7 us (7%)
    all_gather x1, waiting for transfers between devices, local(): both_all = lax.all_gather(jnp.stack([keys_here, values_here]), 'zq', axis=0)  56.5 us
    all_to_all x1, blocking collectives, local(): parts = lax.all_to_all(packed, 'grp', 0, 0, tiled=True)  26.5 us
    all_to_all x1, blocking collectives, local(): attended = lax.all_to_all(attended, 'grp', 0, 0, tiled=True)  18.8 us
    all_to_all x1, blocking collectives, local(): got = lax.all_to_all(send, 'w', 0, 0, tiled=True)  16.2 us
    all_to_all x1, blocking collectives, local(): attended = lax.all_to_all(attended, 'w', 0, 1, tiled=True)  13.9 us
    reduce_sum x2, other arithmetic, local(): totals = jnp.sum(weights_prefix, axis=2) + jnp.sum(weights_draft, axis=2)  8.66 us
    dot_general x2, matrix products, split_product(): jnp.einsum(spec, low, values, preferred_element_type=jnp.float32)  8.43 us
    dot_general x1, matrix products, local(): jnp.einsum('rgd,pd->rgp', query_block, prefix_k, preferred_element_type=j...  8.06 us
  transfers between devices with their start and end apart: 1, of which 1 were waited for; matrix products, arithmetic and copies ran while one was open for 0% of the time, Pallas kernels for 0%

profile of v5, /device:TPU:6, one launch (start us, length us, event | category | flops | bytes accessed | tf_op | source)
XLA Modules:
  0.0 204.1 jit_solution(7967593883240150405)
XLA Ops:
  6.5 0.0 all-gather.3.cloned.1.call-start
  6.5 1.1 copy.46
  7.7 1.0 copy.47
  8.7 1.0 copy.48
  9.7 0.7 reduce.3
  10.4 0.7 reduce.4
  11.2 0.5 broadcast.50
  11.7 1.2 reduce.5
  12.9 0.2 reshape.186
  13.1 16.2 %all_to_all.44 = bf16[8,2,24704]{2,1,0:T(2,128)(2,1)S(1)} all-to-all(bf16[8,2,24704]{2,1,0:T(2,128)(2,1)S(1)} %reshape.186), channel_id=1, replica_groups=mesh['grp'=16,'zq'=4,'w'=8] {'w'}, dimensions={0} | all-to-all | bytes 1581056 | tf_op jit(solution)/shard_map/all_to_all | solution.py:42
  29.4 2.5 %reshape.187 = bf16[8,1,49408]{2,1,0:T(2,128)(2,1)S(1)} reshape(bf16[8,2,24704]{2,1,0:T(2,128)(2,1)S(1)} %all_to_all.44) | data formatting | bytes 1581056
  31.8 0.1 copy.60
  31.9 0.1 fusion.30
  32.0 0.1 reshape.169
  32.1 0.1 reshape.170
  32.3 0.8 pad_maximum_fusion
  33.2 0.0 all-gather.3.cloned.1.call-update
  33.2 0.8 dynamic-slice_subtract_fusion
  34.0 0.1 compare_and_fusion
  34.0 0.1 reshape.168
  34.2 56.5 %all-gather.3.cloned.1.call-done = bf16[8,1032,128]{2,1,0:T(8,128)(2,1)} async-done(((bf16[2,1032,128]{2,1,0:T(8,128)(2,1)}), bf16[8,1032,128]{2,1,0:T(8,128)(2,1)}) %all-gather.3.cloned.1.call-update) | async-done | bytes 2113552 | tf_op jit(solution)/shard_map/all_gather | solution.py:64
  90.7 1.7 slice_bitcast_fusion.1
  92.4 0.1 slice.62
  92.4 0.2 fusion.32
  92.7 8.1 %multiply_reduce_fusion = (f32[128,8]{0,1:T(8,128)S(1)}, f32[128,8,4096]{2,0,1:T(8,128)}) fusion(bf16[4096,128,1]{1,0,2:T(8,128)(2,1)S(1)} %bitcast.80, bf16[128,8,128]{2,1,0:T(8,128)(2,1)S(1)} %reshape.168), kind=kOutput, calls=%fused_computation.4 | convolution fusion | flops 1082129408 | bytes 18092032 | tf_op jit(solution)/shard_map/rgd,pd->rgp/dot_general | solution.py:72
  100.8 0.3 fusion.17
  101.0 0.1 slice.65
  101.1 0.1 copy.38
  101.2 8.6 %fusion.1 = f32[128,8]{0,1:T(8,128)S(1)} fusion(f32[128,8,4096]{2,0,1:T(8,128)} %get-tuple-element.13, f32[128,8]{0,1:T(8,128)S(1)} %max.11), kind=kLoop, calls=%fused_computation.5 | loop fusion | flops 12581888 | bytes 16785408 | tf_op jit(solution)/shard_map/reduce_sum | solution.py:93
  109.8 0.1 copy.39
  110.0 0.1 add.48
  110.0 7.3 %fusion.2 = f32[128,8,128]{2,0,1:T(8,128)S(1)} fusion(bf16[4096,128,1]{1,0,2:T(8,128)(2,1)S(1)} %bitcast.87, f32[128,8,4096]{2,0,1:T(8,128)} %get-tuple-element.13, f32[128,8]{0,1:T(8,128)S(1)} %max.11), kind=kOutput, calls=%fused_computation.6 | convolution fusion | flops 1090519040 | bytes 18354176 | tf_op jit(solution)/shard_map/rgp,pd->rgd/dot_general | solution.py:19
  117.3 8.1 %fusion.7 = f32[128,8,128]{2,0,1:T(8,128)S(1)} fusion(f32[128,8,128]{2,0,1:T(8,128)S(1)} %fusion.2, bf16[4096,128,1]{1,0,2:T(8,128)(2,1)S(1)} %bitcast.88, f32[128,8,4096]{2,0,1:T(8,128)} %get-tuple-element.13, f32[128,8]{0,1:T(8,128)S(1)} %max.11), kind=kOutput, calls=%fused_computation.12 | convolution fusion | flops 1094844416 | bytes 18878464 | tf_op jit(solution)/shard_map/rgp,pd->rgd/dot_general | solution.py:19
  125.5 0.3 fusion.6
  125.8 0.3 copy.37
  126.1 0.1 reshape.175
  126.2 0.1 max.12
  126.3 0.1 concatenate.15
  126.3 0.5 copy.40
  126.9 26.5 %all_to_all.45 = f32[16,1,8320]{2,1,0:T(1,128)S(1)} all-to-all(f32[16,1,8320]{2,1,0:T(1,128)S(1)} %copy.40), channel_id=1, replica_groups=mesh['grp'=16,'zq'=4,'w'=8] {'grp'}, dimensions={0} | all-to-all | bytes 1064960 | tf_op jit(solution)/shard_map/all_to_all | solution.py:106
  153.4 3.2 %copy.41 = f32[16,1,8320]{0,2,1:T(8,128)} copy(f32[16,1,8320]{2,1,0:T(1,128)S(1)} %all_to_all.45) | data formatting | bytes 1064960 | tf_op jit(solution)/shard_map/all_to_all | solution.py:106
  156.6 0.9 slice_reduce_fusion
  157.4 1.0 fusion.24
  158.4 0.1 sub.51
  158.5 0.1 div.16
  158.6 0.1 copy.42
  158.6 0.9 fusion.25
  159.5 3.3 %fusion.5 = f32[8192]{0:T(1024)S(1)} fusion(f32[16,8320]{0,1:T(8,128)} %bitcast.79, f32[16,8,8]{0,2,1:T(8,128)S(1)} %fusion.25), kind=kLoop, calls=%fused_computation.9 | loop fusion | flops 253952 | bytes 561152 | tf_op jit(solution)/shard_map/reduce_sum | solution.py:115
  162.9 0.1 bitcast_divide_fusion
  163.0 18.8 %all_to_all.46 = f32[16,8,1024]{2,1,0:T(8,128)S(1)} all-to-all(f32[16,8,1024]{2,1,0:T(8,128)S(1)} %broadcast_in_dim.36), channel_id=1, replica_groups=mesh['grp'=16,'zq'=4,'w'=8] {'grp'}, dimensions={0} | all-to-all | bytes 1048576 | tf_op jit(solution)/shard_map/all_to_all | solution.py:118
  181.8 0.6 reshape.177
  182.5 13.9 %all_to_all.47 = f32[128,1,1024]{2,1,0:T(1,128)S(1)} all-to-all(f32[128,1,1024]{2,1,0:T(1,128)S(1)} %reshape.177), channel_id=1, replica_groups=mesh['grp'=16,'zq'=4,'w'=8] {'w'}, dimensions={0} | all-to-all | bytes 1048576 | tf_op jit(solution)/shard_map/all_to_all | solution.py:121
  196.3 0.1 copy.45
  196.4 0.8 copy.49
  (13 shorter events, 0.2 us)
Async XLA Ops:
  6.5 84.1 %all-gather.3.cloned.1.call-start = ((), (), s32[]{:S(2)}) async-start(), calls=%async_computation.4 | async-start | bytes 2641920 | tf_op jit(solution)/shard_map/all_gather | solution.py:64
Sparse Core Ops, SparseCore 0:
  33.3 57.3 all-gather.2

commit v6 on v5

--- a/solution.py
+++ b/solution.py
@@ -1,8 +1,11 @@
+import functools
 import math
 
 import jax
 import jax.numpy as jnp
 from jax import lax
+from jax.experimental import pallas as pl
+from jax.experimental.pallas import tpu as pltpu
 from jax.sharding import Mesh
 from jax.sharding import PartitionSpec as P
 
@@ -19,6 +22,56 @@
     return jnp.einsum(spec, high, values, preferred_element_type=jnp.float32) + jnp.einsum(
         spec, low, values, preferred_element_type=jnp.float32
     )
+
+
+def attend_kernel(inverse_root, query_ref, key_ref, value_ref, sum_ref, peak_ref, total_ref):
+    scores = lax.dot_general(
+        query_ref[...],
+        key_ref[...],
+        (((1,), (1,)), ((), ())),
+        preferred_element_type=jnp.float32,
+    ) * inverse_root
+    peak = jnp.max(scores, axis=1, keepdims=True)
+    weights = jnp.exp(scores - peak)
+    total_ref[...] = jnp.sum(weights, axis=1, keepdims=True)
+    peak_ref[...] = peak
+    high = weights.astype(jnp.bfloat16)
+    low = (weights - high.astype(jnp.float32)).astype(jnp.bfloat16)
+    values = value_ref[...]
+    sum_ref[...] = jnp.dot(high, values, preferred_element_type=jnp.float32) + jnp.dot(
+        low, values, preferred_element_type=jnp.float32
+    )
+
+
+def attend_prefix(query_rows, keys, values, inverse_root):
+    count, width = query_rows.shape
+    length = keys.shape[0]
+    tile = 256
+    return pl.pallas_call(
+        functools.partial(attend_kernel, inverse_root),
+        grid=(count // tile,),
+        in_specs=[
+            pl.BlockSpec((tile, width), lambda i: (i, 0)),
+            pl.BlockSpec((length, width), lambda i: (0, 0)),
+            pl.BlockSpec((length, width), lambda i: (0, 0)),
+        ],
+        out_specs=[
+            pl.BlockSpec((tile, width), lambda i: (i, 0)),
+            pl.BlockSpec((tile, 1), lambda i: (i, 0)),
+            pl.BlockSpec((tile, 1), lambda i: (i, 0)),
+        ],
+        out_shape=[
+            jax.ShapeDtypeStruct((count, width), jnp.float32),
+            jax.ShapeDtypeStruct((count, 1), jnp.float32),
+            jax.ShapeDtypeStruct((count, 1), jnp.float32),
+        ],
+        compiler_params=pltpu.CompilerParams(vmem_limit_bytes=48 * 1024 * 1024),
+        cost_estimate=pl.CostEstimate(
+            flops=6 * count * length * width,
+            transcendentals=count * length,
+            bytes_accessed=2 * count * width + 4 * length * width + 4 * count * (width + 2),
+        ),
+    )(query_rows, keys, values)
 
 
 def local(queries, prefix_keys, prefix_values, draft_keys, draft_values, draft_offset):
@@ -69,9 +122,11 @@
     draft_v = values_all[:, local_keys:].reshape(-1, HD)
 
     block_rows = ways * rows
-    scores_prefix = jnp.einsum(
-        "rgd,pd->rgp", query_block, prefix_k, preferred_element_type=jnp.float32
-    ) * inverse_root
+    query_rows = query_block.reshape(block_rows * group_heads, HD)
+    prefix_sum, prefix_peak, prefix_total = attend_prefix(query_rows, prefix_k, prefix_v, inverse_root)
+    prefix_sum = prefix_sum.reshape(block_rows, group_heads, HD)
+    prefix_peak = prefix_peak.reshape(block_rows, group_heads)
+    prefix_total = prefix_total.reshape(block_rows, group_heads)
     scores_draft = jnp.einsum(
         "rgd,jd->rgj", query_block, draft_k, preferred_element_type=jnp.float32
     ) * inverse_root
@@ -86,12 +141,11 @@
     )
     visible = visible[:, None, :]
     masked_draft = jnp.where(visible, scores_draft, -jnp.inf)
-    peak = jnp.maximum(jnp.max(scores_prefix, axis=2), jnp.max(masked_draft, axis=2))
-
-    weights_prefix = jnp.exp(scores_prefix - peak[..., None])
+    peak = jnp.maximum(prefix_peak, jnp.max(masked_draft, axis=2))
+    prefix_scale = jnp.exp(prefix_peak - peak)
     weights_draft = jnp.where(visible, jnp.exp(masked_draft - peak[..., None]), 0.0)
-    totals = jnp.sum(weights_prefix, axis=2) + jnp.sum(weights_draft, axis=2)
-    summed = split_product(weights_prefix, prefix_v) + split_product(weights_draft, draft_v)
+    totals = prefix_total * prefix_scale + jnp.sum(weights_draft, axis=2)
+    summed = prefix_sum * prefix_scale[..., None] + split_product(weights_draft, draft_v)
 
     groups = lax.axis_size("grp")
     slice_rows = block_rows // groups

time: 206 us -> 185 us (0.90)
  matrix products: 24.2 us -> 1.56 us
  Pallas kernels: 0 us -> 11 us
  other arithmetic: 19.1 us -> 9.58 us
    pallas_call x0 -> x1, Pallas kernels: none -> 11 us  [attend_prefix(): pl.pallas_call(functools.partial(attend_kernel, inverse_root), grid=(coun...]
    reduce_sum x2 -> x1, other arithmetic: 8.66 us -> 0.04 us  [local(): totals = prefix_total * prefix_scale + jnp.sum(weights_draft, axis=2)]
    dot_general x2 -> x1, matrix products: 8.43 us -> 0.36 us  [split_product(): jnp.einsum(spec, low, values, preferred_element_type=jnp.float32)]
    dot_general x1 -> x0, matrix products: 8.06 us -> none  [local(): jnp.einsum('rgd,pd->rgp', query_block, prefix_k, preferred_element_type=j...]
    dot_general x2 -> x1, matrix products: 7.54 us -> 0.27 us  [split_product(): jnp.einsum(spec, high, values, preferred_element_type=jnp.float32)]
    unnamed x12 -> x20, local copies, waits for them, and re-layouts: 6.85 us -> 6.79 us
  transfers between devices with their start and end apart: 1 -> 1, of which waited for: 1 -> 1; matrix products, arithmetic and copies ran while one was open for 0% -> 1% of each run, Pallas kernels for 0% -> 0%
where the time goes in v6:
time: 185 us; the launch traced here: 183 us
  blocking collectives  75.4 us (41%)
  waiting for transfers between devices  56.4 us (30%)
  local copies, waits for them, and re-layouts  15.4 us (8%)
  between operations  13.7 us (7%)
  Pallas kernels  11 us (6%)
  other arithmetic  9.58 us (5%)
    all_gather x1, waiting for transfers between devices, local(): both_all = lax.all_gather(jnp.stack([keys_here, values_here]), 'zq', axis=0)  56.4 us
    all_to_all x1, blocking collectives, local(): parts = lax.all_to_all(packed, 'grp', 0, 0, tiled=True)  26.5 us
    all_to_all x1, blocking collectives, local(): attended = lax.all_to_all(attended, 'grp', 0, 0, tiled=True)  18.8 us
    all_to_all x1, blocking collectives, local(): got = lax.all_to_all(send, 'w', 0, 0, tiled=True)  16.2 us
    all_to_all x1, blocking collectives, local(): attended = lax.all_to_all(attended, 'w', 0, 1, tiled=True)  13.9 us
    pallas_call x1, Pallas kernels, attend_prefix(): pl.pallas_call(functools.partial(attend_kernel, inverse_root), grid=(coun...  11 us
    unnamed x20, local copies, waits for them, and re-layouts  6.79 us
    all_to_all x2, local copies, waits for them, and re-layouts, local(): parts = lax.all_to_all(packed, 'grp', 0, 0, tiled=True)  3.72 us
  transfers between devices with their start and end apart: 1, of which 1 were waited for; matrix products, arithmetic and copies ran while one was open for 1% of the time, Pallas kernels for 0%

profile of v6, /device:TPU:6, one launch (start us, length us, event | category | flops | bytes accessed | tf_op | source)
XLA Modules:
  0.0 183.1 jit_solution(2510911099637329757)
XLA Ops:
  6.5 0.0 copy-start.1
  6.5 0.0 copy-start.2
  6.5 0.0 copy-start.3
  6.5 0.0 all-gather.3.cloned.1.call-start
  6.5 1.1 copy.53
  7.7 1.0 copy.54
  8.7 0.0 copy-done.1
  8.8 0.0 copy-done.2
  8.8 0.0 copy-done.3
  8.9 0.5 broadcast.53
  9.4 1.2 reduce.8
  10.7 0.2 reshape.214
  10.9 16.2 %all_to_all.44 = bf16[8,2,24704]{2,1,0:T(2,128)(2,1)S(1)} all-to-all(bf16[8,2,24704]{2,1,0:T(2,128)(2,1)S(1)} %reshape.214), channel_id=1, replica_groups=mesh['grp'=16,'zq'=4,'w'=8] {'w'}, dimensions={0} | all-to-all | bytes 1581056 | tf_op jit(solution)/shard_map/all_to_all | solution.py:95
  27.1 2.5 %reshape.215 = bf16[8,1,49408]{2,1,0:T(2,128)(2,1)S(1)} reshape(bf16[8,2,24704]{2,1,0:T(2,128)(2,1)S(1)} %all_to_all.44) | data formatting | bytes 1581056
  29.6 0.1 copy.66
  29.7 0.1 fusion.18
  29.8 0.1 reshape.191
  29.9 0.1 reshape.192
  30.1 0.8 pad_maximum_fusion
  30.9 0.0 all-gather.3.cloned.1.call-update
  31.0 0.8 dynamic-slice_subtract_fusion
  31.7 0.1 compare_and_fusion
  31.8 0.1 reshape.197
  31.9 0.1 reshape_reshape.3.query_ref
  32.1 56.4 %all-gather.3.cloned.1.call-done = bf16[8,1032,128]{2,1,0:T(8,128)(2,1)} async-done(((bf16[2,1032,128]{2,1,0:T(8,128)(2,1)}), bf16[8,1032,128]{2,1,0:T(8,128)(2,1)}) %all-gather.3.cloned.1.call-update) | async-done | bytes 2113552 | tf_op jit(solution)/shard_map/all_gather | solution.py:117
  88.4 1.7 slice_bitcast_fusion
  90.1 0.0 copy-start
  90.1 0.1 slice.64
  90.2 0.1 slice.62
  90.3 0.8 copy-done
  91.1 11.0 %shard_map.64 = (f32[1024,128]{1,0:T(8,128)S(1)}, f32[1024,1]{1,0:T(8,128)S(1)}, f32[1024,1]{1,0:T(8,128)S(1)}) custom-call(bf16[1024,128]{1,0:T(8,128)(2,1)S(1)} %reshape_reshape.3.query_ref, bf16[4096,128]{1,0:T(8,128)(2,1)S(1)} %bitcast.71, bf16[4096,128]{1,0:T(8,128)(2,1)S(1)} %bitcast.70), custom_call_target="tpu_custom_call" | custom-call | flops 3221225472 | bytes 2891776 | tf_op jit(solution)/shard_map/pallas_call | solution.py:50
  102.1 0.2 reduce.5
  102.3 0.1 reshape.196
  102.4 0.1 reshape.201
  102.6 0.9 fusion.20
  103.5 0.1 copy.45
  103.6 0.3 fusion.7
  103.9 0.1 copy.46
  104.0 0.1 reduce_sum.32
  104.1 0.1 reduce_max.21
  104.2 0.2 reduce.7
  104.4 0.1 reshape.202
  104.5 0.4 fusion.1
  104.8 0.3 copy.44
  105.1 0.1 reshape.200
  105.3 0.1 concatenate.15
  105.3 0.5 copy.47
  105.9 26.5 %all_to_all.45 = f32[16,1,8320]{2,1,0:T(1,128)S(1)} all-to-all(f32[16,1,8320]{2,1,0:T(1,128)S(1)} %copy.47), channel_id=1, replica_groups=mesh['grp'=16,'zq'=4,'w'=8] {'grp'}, dimensions={0} | all-to-all | bytes 1064960 | tf_op jit(solution)/shard_map/all_to_all | solution.py:160
  132.4 3.2 %copy.48 = f32[16,1,8320]{0,2,1:T(8,128)} copy(f32[16,1,8320]{2,1,0:T(1,128)S(1)} %all_to_all.45) | data formatting | bytes 1064960 | tf_op jit(solution)/shard_map/all_to_all | solution.py:160
  135.6 0.9 slice_reduce_fusion
  136.4 1.0 fusion.14
  137.4 0.1 sub.49
  137.5 0.1 div.16
  137.6 0.1 copy.49
  137.7 0.9 fusion.15
  138.5 3.3 %fusion = f32[8192]{0:T(1024)S(1)} fusion(f32[16,8320]{0,1:T(8,128)} %bitcast.76, f32[16,8,8]{0,2,1:T(8,128)S(1)} %fusion.15), kind=kLoop, calls=%fused_computation.1 | loop fusion | flops 253952 | bytes 561152 | tf_op jit(solution)/shard_map/reduce_sum | solution.py:169
  141.9 0.1 bitcast_divide_fusion
  142.0 18.8 %all_to_all.46 = f32[16,8,1024]{2,1,0:T(8,128)S(1)} all-to-all(f32[16,8,1024]{2,1,0:T(8,128)S(1)} %broadcast_in_dim.36), channel_id=1, replica_groups=mesh['grp'=16,'zq'=4,'w'=8] {'grp'}, dimensions={0} | all-to-all | bytes 1048576 | tf_op jit(solution)/shard_map/all_to_all | solution.py:172
  160.8 0.6 reshape.204
  161.4 13.9 %all_to_all.47 = f32[128,1,1024]{2,1,0:T(1,128)S(1)} all-to-all(f32[128,1,1024]{2,1,0:T(1,128)S(1)} %reshape.204), channel_id=1, replica_groups=mesh['grp'=16,'zq'=4,'w'=8] {'w'}, dimensions={0} | all-to-all | bytes 1048576 | tf_op jit(solution)/shard_map/all_to_all | solution.py:175
  175.3 0.1 copy.52
  175.4 0.8 copy.56
  (17 shorter events, 0.4 us)
Async XLA Ops:
  6.5 2.2 %copy-start.1 = (bf16[128,1024]{1,0:T(8,128)(2,1)S(1)}, bf16[128,1024]{1,0:T(8,128)(2,1)}, u32[]{:S(2)}) copy-start(bf16[128,1024]{1,0:T(8,128)(2,1)} %param.8) | copy-start | bytes 786436
  6.5 2.2 %copy-start.2 = (bf16[1,1024]{1,0:T(2,128)(2,1)S(1)}, bf16[1,1024]{1,0:T(2,128)(2,1)}, u32[]{:S(2)}) copy-start(bf16[1,1024]{1,0:T(2,128)(2,1)} %param.9) | copy-start | bytes 6148
  6.5 2.3 %copy-start.3 = (bf16[1,1024]{1,0:T(2,128)(2,1)S(1)}, bf16[1,1024]{1,0:T(2,128)(2,1)}, u32[]{:S(2)}) copy-start(bf16[1,1024]{1,0:T(2,128)(2,1)} %param.10) | copy-start | bytes 6148
  6.5 81.9 %all-gather.3.cloned.1.call-start = ((), (), s32[]{:S(2)}) async-start(), calls=%async_computation.4 | async-start | bytes 2641920 | tf_op jit(solution)/shard_map/all_gather | solution.py:117
  90.1 1.0 copy-start
Sparse Core Ops, SparseCore 0:
  31.1 57.3 all-gather.2

commit v7 on v6

--- a/solution.py
+++ b/solution.py
@@ -114,12 +114,18 @@
         axis=0,
     )
     local_keys = ways * positions
-    both_all = lax.all_gather(jnp.stack([keys_here, values_here]), "zq", axis=0)
+    both_here = jnp.stack([keys_here, values_here])
+    blocks = [both_here] + [
+        lax.ppermute(both_here, "zq", [(i, (i + shift) % quarters) for i in range(quarters)])
+        for shift in range(1, quarters)
+    ]
+    both_all = jnp.stack(blocks)
     keys_all, values_all = both_all[:, 0], both_all[:, 1]
     prefix_k = keys_all[:, :local_keys].reshape(-1, HD)
     draft_k = keys_all[:, local_keys:].reshape(-1, HD)
     prefix_v = values_all[:, :local_keys].reshape(-1, HD)
     draft_v = values_all[:, local_keys:].reshape(-1, HD)
+    source_quarter = (quarter - lax.iota(jnp.int32, quarters)) % quarters
 
     block_rows = ways * rows
     query_rows = query_block.reshape(block_rows * group_heads, HD)
@@ -134,7 +140,8 @@
     query_first = quarter * block_rows
     query_index = query_first + lax.iota(jnp.int32, block_rows)
     drafts_per_group = quarters * ways
-    key_index = group * drafts_per_group + lax.iota(jnp.int32, drafts_per_group)
+    draft_source = (source_quarter[:, None] * ways + lax.iota(jnp.int32, ways)[None, :]).reshape(-1)
+    key_index = group * drafts_per_group + draft_source
     offsets = lax.dynamic_slice_in_dim(draft_offset, query_first, block_rows)
     visible = (key_index[None, :] <= query_index[:, None]) & (
         key_index[None, :] >= (query_index - offsets)[:, None]

time: 185 us -> 172 us (0.930)
  starting transfers between devices: 0.01 us -> 22 us
  waiting for transfers between devices: 56.4 us -> 39.2 us
  between operations: 13.7 us -> 0.34 us
  blocking collectives: 75.4 us -> 69.5 us
    all_gather x1 -> x0, waiting for transfers between devices: 56.4 us -> none  [local(): both_all = lax.all_gather(jnp.stack([keys_here, values_here]), 'zq', axis=0)]
    ppermute x0 -> x3, waiting for transfers between devices: none -> 28.1 us  [local(): lax.ppermute(both_here, 'zq', [(i, (i + shift) % quarters) for i in range...]
    ppermute x0 -> x3, starting transfers between devices: none -> 16.9 us  [local(): lax.ppermute(both_here, 'zq', [(i, (i + shift) % quarters) for i in range...]
    all_to_all x1 -> x0, blocking collectives: 16.2 us -> none  [local(): got = lax.all_to_all(send, 'w', 0, 0, tiled=True)]
    all_to_all x0 -> x1, waiting for transfers between devices: none -> 11.1 us  [local(): got = lax.all_to_all(send, 'w', 0, 0, tiled=True)]
    all_to_all x1, blocking collectives: 13.9 us -> 25 us  [local(): attended = lax.all_to_all(attended, 'w', 0, 1, tiled=True)]
    all_to_all x0 -> x1, starting transfers between devices: none -> 5.11 us  [local(): got = lax.all_to_all(send, 'w', 0, 0, tiled=True)]
    unnamed x20 -> x18, local copies, waits for them, and re-layouts: 6.79 us -> 8.58 us
  transfers between devices with their start and end apart: 1 -> 4, of which waited for: 1 -> 3; matrix products, arithmetic and copies ran while one was open for 1% -> 1% of each run, Pallas kernels for 0% -> 0%
where the time goes in v7:
time: 172 us; the launch traced here: 170 us
  blocking collectives  69.5 us (40%)
  waiting for transfers between devices  39.2 us (23%)
  starting transfers between devices  22 us (13%)
  local copies, waits for them, and re-layouts  16.5 us (10%)
  Pallas kernels  11 us (6%)
  other arithmetic  9.84 us (6%)
    ppermute x3, waiting for transfers between devices, local(): lax.ppermute(both_here, 'zq', [(i, (i + shift) % quarters) for i in range...  28.1 us
    all_to_all x1, blocking collectives, local(): parts = lax.all_to_all(packed, 'grp', 0, 0, tiled=True)  26 us
    all_to_all x1, blocking collectives, local(): attended = lax.all_to_all(attended, 'w', 0, 1, tiled=True)  25 us
    all_to_all x1, blocking collectives, local(): attended = lax.all_to_all(attended, 'grp', 0, 0, tiled=True)  18.5 us
    ppermute x3, starting transfers between devices, local(): lax.ppermute(both_here, 'zq', [(i, (i + shift) % quarters) for i in range...  16.9 us
    all_to_all x1, waiting for transfers between devices, local(): got = lax.all_to_all(send, 'w', 0, 0, tiled=True)  11.1 us
    pallas_call x1, Pallas kernels, attend_prefix(): pl.pallas_call(functools.partial(attend_kernel, inverse_root), grid=(coun...  11 us
    unnamed x18, local copies, waits for them, and re-layouts  8.58 us
  transfers between devices with their start and end apart: 4, of which 3 were waited for; matrix products, arithmetic and copies ran while one was open for 1% of the time, Pallas kernels for 0%

profile of v7, /device:TPU:6, one launch (start us, length us, event | category | flops | bytes accessed | tf_op | source)
XLA Modules:
  0.0 169.9 jit_solution(1924300903730462577)
XLA Ops:
  0.0 1.1 copy.68
  1.1 1.0 copy.69
  2.1 1.0 copy.70
  3.1 0.7 reduce.3
  4.0 0.5 broadcast.98
  4.5 1.2 reduce.8
  5.7 1.1 reshape.242
  6.8 5.1 %all-to-all-start = ((bf16[8,2,24704]{2,1,0:T(2,128)(2,1)}), bf16[8,2,24704]{2,1,0:T(2,128)(2,1)S(1)}, u32[]{:S(2)}, u32[]{:S(2)}) async-start(bf16[8,2,24704]{2,1,0:T(2,128)(2,1)} %reshape.242), calls=%async_computation | async-start | bytes 1581056 | tf_op jit(solution)/shard_map/all_to_all | solution.py:95
  11.9 11.1 %all-to-all-done = bf16[8,2,24704]{2,1,0:T(2,128)(2,1)S(1)} async-done(((bf16[8,2,24704]{2,1,0:T(2,128)(2,1)}), bf16[8,2,24704]{2,1,0:T(2,128)(2,1)S(1)}, u32[]{:S(2)}, u32[]{:S(2)}) %all-to-all-start) | async-done | bytes 790560 | tf_op jit(solution)/shard_map/all_to_all | solution.py:95
  23.1 2.5 %reshape.243 = bf16[8,1,49408]{2,1,0:T(2,128)(2,1)S(1)} reshape(bf16[8,2,24704]{2,1,0:T(2,128)(2,1)S(1)} %all-to-all-done) | data formatting | bytes 1581056
  25.5 0.1 copy.81
  25.6 0.1 fusion.21
  25.7 0.1 reshape.220
  25.8 0.1 reshape.221
  26.0 0.1 fusion.20
  26.1 10.1 %collective-permute-start.2 = (bf16[2,1032,128]{2,1,0:T(8,128)(2,1)S(1)}, bf16[2,1032,128]{2,1,0:T(8,128)(2,1)S(1)}, u32[]{:S(2)}, u32[]{:S(2)}) collective-permute-start(bf16[2,1032,128]{2,1,0:T(8,128)(2,1)S(1)} %get-tuple-element.23), channel_id=1, source_target_pairs={{0,24},{8,0},{16,8},{24,16},{1,25},{9,1},{17,9},{25,17},{2,26},{10... | collective-permute-start | bytes 1585160 | tf_op jit(solution)/shard_map/ppermute | solution.py:119
  36.2 1.9 %collective-permute-start.1 = (bf16[2,1032,128]{2,1,0:T(8,128)(2,1)S(1)}, bf16[2,1032,128]{2,1,0:T(8,128)(2,1)S(1)}, u32[]{:S(2)}, u32[]{:S(2)}) collective-permute-start(bf16[2,1032,128]{2,1,0:T(8,128)(2,1)S(1)} %get-tuple-element.23), channel_id=1, source_target_pairs={{0,16},{8,24},{16,0},{24,8},{1,17},{9,25},{17,1},{25,9},{2,18},{10... | collective-permute-start | bytes 1585160 | tf_op jit(solution)/shard_map/ppermute | solution.py:119
  38.2 4.8 %collective-permute-start = (bf16[2,1032,128]{2,1,0:T(8,128)(2,1)S(1)}, bf16[2,1032,128]{2,1,0:T(8,128)(2,1)S(1)}, u32[]{:S(2)}, u32[]{:S(2)}) collective-permute-start(bf16[2,1032,128]{2,1,0:T(8,128)(2,1)S(1)} %get-tuple-element.23), channel_id=1, source_target_pairs={{0,8},{8,16},{16,24},{24,0},{1,9},{9,17},{17,25},{25,1},{2,10},{10... | collective-permute-start | bytes 1585160 | tf_op jit(solution)/shard_map/ppermute | solution.py:119
  43.0 0.1 add_add_fusion
  43.1 0.1 add.71
  43.1 0.8 dynamic-slice_subtract_fusion
  43.9 0.1 compare_and_fusion
  44.0 0.8 reshape.226
  44.8 0.1 reshape_reshape.3.query_ref
  44.9 23.9 %collective-permute-done.2 = bf16[2,1032,128]{2,1,0:T(8,128)(2,1)S(1)} collective-permute-done((bf16[2,1032,128]{2,1,0:T(8,128)(2,1)S(1)}, bf16[2,1032,128]{2,1,0:T(8,128)(2,1)S(1)}, u32[]{:S(2)}, u32[]{:S(2)}) %collective-permute-start.2) | collective-permute-done | bytes 528416 | tf_op jit(solution)/shard_map/ppermute | solution.py:119
  68.8 0.0 collective-permute-done.1
  68.8 4.2 %collective-permute-done = bf16[2,1032,128]{2,1,0:T(8,128)(2,1)S(1)} collective-permute-done((bf16[2,1032,128]{2,1,0:T(8,128)(2,1)S(1)}, bf16[2,1032,128]{2,1,0:T(8,128)(2,1)S(1)}, u32[]{:S(2)}, u32[]{:S(2)}) %collective-permute-start) | collective-permute-done | bytes 528416 | tf_op jit(solution)/shard_map/ppermute | solution.py:119
  73.0 0.3 pad_maximum_fusion
  73.3 0.1 slice_bitcast_fusion
  73.5 0.1 slice.62
  73.5 0.1 slice.64
  73.6 0.8 copy-done
  74.5 11.0 %shard_map.64 = (f32[1024,128]{1,0:T(8,128)S(1)}, f32[1024,1]{1,0:T(8,128)S(1)}, f32[1024,1]{1,0:T(8,128)S(1)}) custom-call(bf16[1024,128]{1,0:T(8,128)(2,1)S(1)} %reshape_reshape.3.query_ref, bf16[4096,128]{1,0:T(8,128)(2,1)S(1)} %bitcast.80, bf16[4096,128]{1,0:T(8,128)(2,1)S(1)} %bitcast.81), custom_call_target="tpu_custom_call" | custom-call | flops 3221225472 | bytes 2891776 | tf_op jit(solution)/shard_map/pallas_call | solution.py:50
  85.5 0.2 reduce.5
  85.7 0.1 reshape.225
  85.8 0.9 fusion.23
  86.8 0.3 fusion.7
  87.1 0.1 reshape.230
  87.2 0.1 copy.60
  87.3 0.4 fusion.1
  87.6 0.3 copy.59
  87.9 0.1 reshape.229
  88.0 0.1 copy.61
  88.1 0.1 reduce_sum.32
  88.2 0.2 reduce.7
  88.4 0.1 reshape.231
  88.5 0.1 reduce_max.21
  88.6 0.1 concatenate.15
  88.7 0.5 copy.62
  89.3 26.0 %all_to_all.44 = f32[16,1,8320]{2,1,0:T(1,128)S(1)} all-to-all(f32[16,1,8320]{2,1,0:T(1,128)S(1)} %copy.62), channel_id=1, replica_groups=mesh['grp'=16,'zq'=4,'w'=8] {'grp'}, dimensions={0} | all-to-all | bytes 1064960 | tf_op jit(solution)/shard_map/all_to_all | solution.py:167
  115.3 3.2 %copy.63 = f32[16,1,8320]{0,2,1:T(8,128)} copy(f32[16,1,8320]{2,1,0:T(1,128)S(1)} %all_to_all.44) | data formatting | bytes 1064960 | tf_op jit(solution)/shard_map/all_to_all | solution.py:167
  118.5 0.9 slice_reduce_fusion
  119.3 0.1 sub.61
  119.4 1.0 fusion.14
  120.4 0.8 fusion.15
  121.2 3.3 %fusion = f32[8192]{0:T(1024)S(1)} fusion(f32[16,8320]{0,1:T(8,128)} %bitcast.86, f32[16,8,8]{0,2,1:T(8,128)S(1)} %fusion.15), kind=kLoop, calls=%fused_computation.1 | loop fusion | flops 253952 | bytes 561152 | tf_op jit(solution)/shard_map/reduce_sum | solution.py:176
  124.6 0.1 div.16
  124.7 0.1 copy.64
  124.8 0.1 bitcast_divide_fusion
  124.9 18.5 %all_to_all.45 = f32[16,8,1024]{2,1,0:T(8,128)S(1)} all-to-all(f32[16,8,1024]{2,1,0:T(8,128)S(1)} %broadcast_in_dim.38), channel_id=1, replica_groups=mesh['grp'=16,'zq'=4,'w'=8] {'grp'}, dimensions={0} | all-to-all | bytes 1048576 | tf_op jit(solution)/shard_map/all_to_all | solution.py:179
  143.4 0.6 reshape.233
  144.0 25.0 %all_to_all.46 = f32[128,1,1024]{2,1,0:T(1,128)S(1)} all-to-all(f32[128,1,1024]{2,1,0:T(1,128)S(1)} %reshape.233), channel_id=1, replica_groups=mesh['grp'=16,'zq'=4,'w'=8] {'w'}, dimensions={0} | all-to-all | bytes 1048576 | tf_op jit(solution)/shard_map/all_to_all | solution.py:182
  169.0 0.1 copy.67
  169.1 0.8 copy.71
  (20 shorter events, 0.3 us)
Async XLA Ops:
  0.0 3.9 %copy-start.2 = (bf16[1,1024]{1,0:T(2,128)(2,1)S(1)}, bf16[1,1024]{1,0:T(2,128)(2,1)}, u32[]{:S(2)}) copy-start(bf16[1,1024]{1,0:T(2,128)(2,1)} %param.10) | copy-start | bytes 6148
  6.8 16.2 %all-to-all-start = ((bf16[8,2,24704]{2,1,0:T(2,128)(2,1)}), bf16[8,2,24704]{2,1,0:T(2,128)(2,1)S(1)}, u32[]{:S(2)}, u32[]{:S(2)}) async-start(bf16[8,2,24704]{2,1,0:T(2,128)(2,1)} %reshape.242), calls=%async_computation | async-start | bytes 1581056 | tf_op jit(solution)/shard_map/all_to_all | solution.py:95
  26.1 42.7 %collective-permute-start.2 = (bf16[2,1032,128]{2,1,0:T(8,128)(2,1)S(1)}, bf16[2,1032,128]{2,1,0:T(8,128)(2,1)S(1)}, u32[]{:S(2)}, u32[]{:S(2)}) collective-permute-start(bf16[2,1032,128]{2,1,0:T(8,128)(2,1)S(1)} %get-tuple-element.23), channel_id=1, source_target_pairs={{0,24},{8,0},{16,8},{24,16},{1,25},{9,1},{17,9},{25,17},{2,26},{10... | collective-permute-start | bytes 1585160 | tf_op jit(solution)/shard_map/ppermute | solution.py:119
  36.2 32.6 %collective-permute-start.1 = (bf16[2,1032,128]{2,1,0:T(8,128)(2,1)S(1)}, bf16[2,1032,128]{2,1,0:T(8,128)(2,1)S(1)}, u32[]{:S(2)}, u32[]{:S(2)}) collective-permute-start(bf16[2,1032,128]{2,1,0:T(8,128)(2,1)S(1)} %get-tuple-element.23), channel_id=1, source_target_pairs={{0,16},{8,24},{16,0},{24,8},{1,17},{9,25},{17,1},{25,9},{2,18},{10... | collective-permute-start | bytes 1585160 | tf_op jit(solution)/shard_map/ppermute | solution.py:119
  38.2 34.9 %collective-permute-start = (bf16[2,1032,128]{2,1,0:T(8,128)(2,1)S(1)}, bf16[2,1032,128]{2,1,0:T(8,128)(2,1)S(1)}, u32[]{:S(2)}, u32[]{:S(2)}) collective-permute-start(bf16[2,1032,128]{2,1,0:T(8,128)(2,1)S(1)} %get-tuple-element.23), channel_id=1, source_target_pairs={{0,8},{8,16},{16,24},{24,0},{1,9},{9,17},{17,25},{25,1},{2,10},{10... | collective-permute-start | bytes 1585160 | tf_op jit(solution)/shard_map/ppermute | solution.py:119
  73.5 1.0 copy-start
  74.5 11.4 %copy-start.1 = (bf16[128,8,128]{2,1,0:T(8,128)(2,1)S(1)}, bf16[128,8,128]{2,1,0:T(8,128)(2,1)}, u32[]{:S(2)}) copy-start(bf16[128,8,128]{2,1,0:T(8,128)(2,1)} %reshape.226) | copy-start | bytes 786436

commit v8 on v7

--- a/solution.py
+++ b/solution.py
@@ -155,31 +155,25 @@
     summed = prefix_sum * prefix_scale[..., None] + split_product(weights_draft, draft_v)
 
     groups = lax.axis_size("grp")
-    slice_rows = block_rows // groups
+    def by_destination(part):
+        part = part.reshape((ways, groups) + part.shape[1:])
+        return part.transpose((1, 0) + tuple(range(2, part.ndim))).reshape(groups * ways, -1)
     packed = jnp.concatenate(
-        [
-            summed.reshape(groups, -1),
-            peak.reshape(groups, -1),
-            totals.reshape(groups, -1),
-        ],
-        axis=1,
+        [by_destination(summed), by_destination(peak), by_destination(totals)], axis=1
     )
-    parts = lax.all_to_all(packed, "grp", 0, 0, tiled=True)
-    sum_size = slice_rows * group_heads * HD
-    head_size = slice_rows * group_heads
-    part_sums = parts[:, :sum_size].reshape(groups, slice_rows, group_heads, HD)
-    part_peaks = parts[:, sum_size : sum_size + head_size].reshape(groups, slice_rows, group_heads)
-    part_totals = parts[:, sum_size + head_size :].reshape(groups, slice_rows, group_heads)
+    parts = lax.all_to_all(packed, ("grp", "w"), 0, 0, tiled=True)
+    sum_size = group_heads * HD
+    parts = parts.reshape(groups, KV, -1)
+    part_sums = parts[:, :, :sum_size].reshape(groups, KV, group_heads, HD)
+    part_peaks = parts[:, :, sum_size : sum_size + group_heads]
+    part_totals = parts[:, :, sum_size + group_heads :]
     joined = jnp.max(part_peaks, axis=0)
     scales = jnp.exp(part_peaks - joined[None])
     merged_totals = jnp.sum(part_totals * scales, axis=0)
     merged_sums = jnp.sum(part_sums * scales[..., None], axis=0)
-    attended = (merged_sums / merged_totals[..., None]).reshape(slice_rows, group_heads * HD)
+    attended = (merged_sums / merged_totals[..., None]).reshape(1, H * HD)
     attended = jnp.broadcast_to(attended[None], (groups,) + attended.shape)
     attended = lax.all_to_all(attended, "grp", 0, 0, tiled=True)
-
-    attended = attended.reshape(block_rows, 1, group_heads * HD)
-    attended = lax.all_to_all(attended, "w", 0, 1, tiled=True)
     return attended.reshape(rows, H * HD)
 
 

time: 172 us -> 155 us (0.901)
  blocking collectives: 69.5 us -> 62.9 us
  other arithmetic: 9.84 us -> 3.46 us
  local copies, waits for them, and re-layouts: 16.5 us -> 12.2 us
    all_to_all x2 -> x1, blocking collectives: 51 us -> 42.5 us  [local(): parts = lax.all_to_all(packed, ('grp', 'w'), 0, 0, tiled=True)]
    reduce_sum x1, other arithmetic: 3.34 us -> 0.21 us  [local(): merged_sums = jnp.sum(part_sums * scales[..., None], axis=0)]
    all_to_all x2 -> x1, local copies, waits for them, and re-layouts: 3.72 us -> 0.61 us  [local(): parts = lax.all_to_all(packed, ('grp', 'w'), 0, 0, tiled=True)]
    all_to_all x1, blocking collectives: 18.5 us -> 20.3 us  [local(): attended = lax.all_to_all(attended, 'grp', 0, 0, tiled=True)]
    unnamed x18 -> x23, local copies, waits for them, and re-layouts: 8.58 us -> 7.98 us
where the time goes in v8:
time: 155 us; the launch traced here: 153 us
  blocking collectives  62.9 us (41%)
  waiting for transfers between devices  39.2 us (25%)
  starting transfers between devices  22 us (14%)
  local copies, waits for them, and re-layouts  12.2 us (8%)
  Pallas kernels  11 us (7%)
  other arithmetic  3.46 us (2%)
    all_to_all x1, blocking collectives, local(): parts = lax.all_to_all(packed, ('grp', 'w'), 0, 0, tiled=True)  42.5 us
    ppermute x3, waiting for transfers between devices, local(): lax.ppermute(both_here, 'zq', [(i, (i + shift) % quarters) for i in range...  28.1 us
    all_to_all x1, blocking collectives, local(): attended = lax.all_to_all(attended, 'grp', 0, 0, tiled=True)  20.3 us
    ppermute x3, starting transfers between devices, local(): lax.ppermute(both_here, 'zq', [(i, (i + shift) % quarters) for i in range...  16.9 us
    all_to_all x1, waiting for transfers between devices, local(): got = lax.all_to_all(send, 'w', 0, 0, tiled=True)  11.1 us
    pallas_call x1, Pallas kernels, attend_prefix(): pl.pallas_call(functools.partial(attend_kernel, inverse_root), grid=(coun...  11 us
    unnamed x23, local copies, waits for them, and re-layouts  7.98 us
    all_to_all x1, starting transfers between devices, local(): got = lax.all_to_all(send, 'w', 0, 0, tiled=True)  5.11 us
  transfers between devices with their start and end apart: 4, of which 3 were waited for; matrix products, arithmetic and copies ran while one was open for 1% of the time, Pallas kernels for 0%

profile of v8, /device:TPU:6, one launch (start us, length us, event | category | flops | bytes accessed | tf_op | source)
XLA Modules:
  0.0 152.6 jit_solution(2407182460385380406)
XLA Ops:
  0.0 0.0 copy-start.1
  0.0 0.0 copy-start.3
  0.0 0.0 copy-start.4
  0.0 1.1 copy.69
  1.2 1.0 copy.70
  2.2 0.0 copy-done.1
  2.2 0.0 copy-done.3
  2.3 0.0 copy-done.4
  2.4 0.5 broadcast.96
  2.9 1.2 reduce.6
  4.1 1.1 reshape.240
  5.2 5.1 %all-to-all-start = ((bf16[8,2,24704]{2,1,0:T(2,128)(2,1)}), bf16[8,2,24704]{2,1,0:T(2,128)(2,1)S(1)}, u32[]{:S(2)}, u32[]{:S(2)}) async-start(bf16[8,2,24704]{2,1,0:T(2,128)(2,1)} %reshape.240), calls=%async_computation | async-start | bytes 1581056 | tf_op jit(solution)/shard_map/all_to_all | solution.py:95
  10.4 11.1 %all-to-all-done = bf16[8,2,24704]{2,1,0:T(2,128)(2,1)S(1)} async-done(((bf16[8,2,24704]{2,1,0:T(2,128)(2,1)}), bf16[8,2,24704]{2,1,0:T(2,128)(2,1)S(1)}, u32[]{:S(2)}, u32[]{:S(2)}) %all-to-all-start) | async-done | bytes 790560 | tf_op jit(solution)/shard_map/all_to_all | solution.py:95
  21.5 2.5 %reshape.241 = bf16[8,1,49408]{2,1,0:T(2,128)(2,1)S(1)} reshape(bf16[8,2,24704]{2,1,0:T(2,128)(2,1)S(1)} %all-to-all-done) | data formatting | bytes 1581056
  23.9 0.1 copy.89
  24.1 0.1 fusion.20
  24.1 0.1 reshape.216
  24.3 0.1 reshape.217
  24.4 0.1 fusion.19
  24.5 10.1 %collective-permute-start.2 = (bf16[2,1032,128]{2,1,0:T(8,128)(2,1)S(1)}, bf16[2,1032,128]{2,1,0:T(8,128)(2,1)S(1)}, u32[]{:S(2)}, u32[]{:S(2)}) collective-permute-start(bf16[2,1032,128]{2,1,0:T(8,128)(2,1)S(1)} %get-tuple-element.23), channel_id=1, source_target_pairs={{0,24},{8,0},{16,8},{24,16},{1,25},{9,1},{17,9},{25,17},{2,26},{10... | collective-permute-start | bytes 1585160 | tf_op jit(solution)/shard_map/ppermute | solution.py:119
  34.7 1.9 %collective-permute-start.1 = (bf16[2,1032,128]{2,1,0:T(8,128)(2,1)S(1)}, bf16[2,1032,128]{2,1,0:T(8,128)(2,1)S(1)}, u32[]{:S(2)}, u32[]{:S(2)}) collective-permute-start(bf16[2,1032,128]{2,1,0:T(8,128)(2,1)S(1)} %get-tuple-element.23), channel_id=1, source_target_pairs={{0,16},{8,24},{16,0},{24,8},{1,17},{9,25},{17,1},{25,9},{2,18},{10... | collective-permute-start | bytes 1585160 | tf_op jit(solution)/shard_map/ppermute | solution.py:119
  36.6 4.8 %collective-permute-start = (bf16[2,1032,128]{2,1,0:T(8,128)(2,1)S(1)}, bf16[2,1032,128]{2,1,0:T(8,128)(2,1)S(1)}, u32[]{:S(2)}, u32[]{:S(2)}) collective-permute-start(bf16[2,1032,128]{2,1,0:T(8,128)(2,1)S(1)} %get-tuple-element.23), channel_id=1, source_target_pairs={{0,8},{8,16},{16,24},{24,0},{1,9},{9,17},{17,25},{25,1},{2,10},{10... | collective-permute-start | bytes 1585160 | tf_op jit(solution)/shard_map/ppermute | solution.py:119
  41.4 0.1 add_add_fusion
  41.5 0.1 add.71
  41.6 0.8 dynamic-slice_subtract_fusion
  42.3 0.1 compare_and_fusion
  42.4 0.8 reshape.222
  43.2 0.1 reshape_reshape.3.query_ref
  43.3 23.9 %collective-permute-done.2 = bf16[2,1032,128]{2,1,0:T(8,128)(2,1)S(1)} collective-permute-done((bf16[2,1032,128]{2,1,0:T(8,128)(2,1)S(1)}, bf16[2,1032,128]{2,1,0:T(8,128)(2,1)S(1)}, u32[]{:S(2)}, u32[]{:S(2)}) %collective-permute-start.2) | collective-permute-done | bytes 528416 | tf_op jit(solution)/shard_map/ppermute | solution.py:119
  67.2 0.0 collective-permute-done.1
  67.2 4.2 %collective-permute-done = bf16[2,1032,128]{2,1,0:T(8,128)(2,1)S(1)} collective-permute-done((bf16[2,1032,128]{2,1,0:T(8,128)(2,1)S(1)}, bf16[2,1032,128]{2,1,0:T(8,128)(2,1)S(1)}, u32[]{:S(2)}, u32[]{:S(2)}) %collective-permute-start) | collective-permute-done | bytes 528416 | tf_op jit(solution)/shard_map/ppermute | solution.py:119
  71.5 0.3 pad_maximum_fusion
  71.7 0.1 slice_bitcast_fusion
  71.9 0.0 copy-start
  71.9 0.1 slice.62
  72.0 0.1 slice.64
  72.0 0.8 copy-done
  72.9 0.0 copy-start.2
  72.9 11.0 %shard_map.64 = (f32[1024,128]{1,0:T(8,128)S(1)}, f32[1024,1]{1,0:T(8,128)S(1)}, f32[1024,1]{1,0:T(8,128)S(1)}) custom-call(bf16[1024,128]{1,0:T(8,128)(2,1)S(1)} %reshape_reshape.3.query_ref, bf16[4096,128]{1,0:T(8,128)(2,1)S(1)} %bitcast.96, bf16[4096,128]{1,0:T(8,128)(2,1)S(1)} %bitcast.97), custom_call_target="tpu_custom_call" | custom-call | flops 3221225472 | bytes 2891776 | tf_op jit(solution)/shard_map/pallas_call | solution.py:50
  83.9 0.2 reduce.3
  84.1 0.1 reshape.221
  84.2 0.0 copy-done.2
  84.2 0.9 fusion.22
  85.2 0.3 fusion.7
  85.5 0.1 reshape.227
  85.6 0.1 copy.60
  85.7 0.4 fusion
  86.1 0.3 copy.93
  86.4 0.1 copy.91
  86.5 0.1 copy.62
  86.6 0.2 reduce.5
  86.8 0.1 reshape.229
  87.0 0.1 concatenate.15
  87.1 0.6 copy.58
  87.7 42.5 %all_to_all.26 = f32[128,1,1040]{2,1,0:T(1,128)S(1)} all-to-all(f32[128,1,1040]{2,1,0:T(1,128)S(1)} %copy.58), channel_id=1, replica_groups=mesh['grp'=16,'zq'=4,'w'=8] {'grp','w'}, dimensions={0} | all-to-all | bytes 1064960 | tf_op jit(solution)/shard_map/all_to_all | solution.py:164
  130.3 0.1 fusion.8
  130.4 0.1 copy.59
  130.4 0.2 fusion.2
  130.7 0.1 bitcast_divide_fusion
  130.7 0.4 broadcast_in_dim.38
  131.1 20.3 %all_to_all.27 = f32[16,1,8192]{2,1,0:T(1,128)S(1)} all-to-all(f32[16,1,8192]{2,1,0:T(1,128)S(1)} %broadcast_in_dim.38), channel_id=1, replica_groups=mesh['grp'=16,'zq'=4,'w'=8] {'grp'}, dimensions={0} | all-to-all | bytes 1048576 | tf_op jit(solution)/shard_map/all_to_all | solution.py:176
  151.5 1.1 copy.92
  (19 shorter events, 0.4 us)
Async XLA Ops:
  0.0 2.2 %copy-start.1 = (bf16[128,1024]{1,0:T(8,128)(2,1)S(1)}, bf16[128,1024]{1,0:T(8,128)(2,1)}, u32[]{:S(2)}) copy-start(bf16[128,1024]{1,0:T(8,128)(2,1)} %param.8) | copy-start | bytes 786436
  0.0 2.2 %copy-start.3 = (bf16[1,1024]{1,0:T(2,128)(2,1)S(1)}, bf16[1,1024]{1,0:T(2,128)(2,1)}, u32[]{:S(2)}) copy-start(bf16[1,1024]{1,0:T(2,128)(2,1)} %param.9) | copy-start | bytes 6148
  0.0 2.3 %copy-start.4 = (bf16[1,1024]{1,0:T(2,128)(2,1)S(1)}, bf16[1,1024]{1,0:T(2,128)(2,1)}, u32[]{:S(2)}) copy-start(bf16[1,1024]{1,0:T(2,128)(2,1)} %param.10) | copy-start | bytes 6148
  5.2 16.2 %all-to-all-start = ((bf16[8,2,24704]{2,1,0:T(2,128)(2,1)}), bf16[8,2,24704]{2,1,0:T(2,128)(2,1)S(1)}, u32[]{:S(2)}, u32[]{:S(2)}) async-start(bf16[8,2,24704]{2,1,0:T(2,128)(2,1)} %reshape.240), calls=%async_computation | async-start | bytes 1581056 | tf_op jit(solution)/shard_map/all_to_all | solution.py:95
  24.5 42.7 %collective-permute-start.2 = (bf16[2,1032,128]{2,1,0:T(8,128)(2,1)S(1)}, bf16[2,1032,128]{2,1,0:T(8,128)(2,1)S(1)}, u32[]{:S(2)}, u32[]{:S(2)}) collective-permute-start(bf16[2,1032,128]{2,1,0:T(8,128)(2,1)S(1)} %get-tuple-element.23), channel_id=1, source_target_pairs={{0,24},{8,0},{16,8},{24,16},{1,25},{9,1},{17,9},{25,17},{2,26},{10... | collective-permute-start | bytes 1585160 | tf_op jit(solution)/shard_map/ppermute | solution.py:119
  34.7 32.6 %collective-permute-start.1 = (bf16[2,1032,128]{2,1,0:T(8,128)(2,1)S(1)}, bf16[2,1032,128]{2,1,0:T(8,128)(2,1)S(1)}, u32[]{:S(2)}, u32[]{:S(2)}) collective-permute-start(bf16[2,1032,128]{2,1,0:T(8,128)(2,1)S(1)} %get-tuple-element.23), channel_id=1, source_target_pairs={{0,16},{8,24},{16,0},{24,8},{1,17},{9,25},{17,1},{25,9},{2,18},{10... | collective-permute-start | bytes 1585160 | tf_op jit(solution)/shard_map/ppermute | solution.py:119
  36.6 34.9 %collective-permute-start = (bf16[2,1032,128]{2,1,0:T(8,128)(2,1)S(1)}, bf16[2,1032,128]{2,1,0:T(8,128)(2,1)S(1)}, u32[]{:S(2)}, u32[]{:S(2)}) collective-permute-start(bf16[2,1032,128]{2,1,0:T(8,128)(2,1)S(1)} %get-tuple-element.23), channel_id=1, source_target_pairs={{0,8},{8,16},{16,24},{24,0},{1,9},{9,17},{17,25},{25,1},{2,10},{10... | collective-permute-start | bytes 1585160 | tf_op jit(solution)/shard_map/ppermute | solution.py:119
  71.9 1.0 copy-start
  72.9 11.4 %copy-start.2 = (bf16[128,8,128]{2,1,0:T(8,128)(2,1)S(1)}, bf16[128,8,128]{2,1,0:T(8,128)(2,1)}, u32[]{:S(2)}) copy-start(bf16[128,8,128]{2,1,0:T(8,128)(2,1)} %reshape.222) | copy-start | bytes 786436

commit v9 on v8

--- a/solution.py
+++ b/solution.py
@@ -137,12 +137,14 @@
         "rgd,jd->rgj", query_block, draft_k, preferred_element_type=jnp.float32
     ) * inverse_root
 
-    query_first = quarter * block_rows
-    query_index = query_first + lax.iota(jnp.int32, block_rows)
+    block_index = lax.iota(jnp.int32, block_rows)
+    query_index = ((block_index // rows) * quarters + quarter) * rows + block_index % rows
     drafts_per_group = quarters * ways
-    draft_source = (source_quarter[:, None] * ways + lax.iota(jnp.int32, ways)[None, :]).reshape(-1)
+    draft_source = (lax.iota(jnp.int32, ways)[None, :] * quarters + source_quarter[:, None]).reshape(-1)
     key_index = group * drafts_per_group + draft_source
-    offsets = lax.dynamic_slice_in_dim(draft_offset, query_first, block_rows)
+    offsets = lax.dynamic_slice_in_dim(
+        draft_offset.reshape(ways, quarters, rows), quarter, 1, axis=1
+    ).reshape(block_rows)
     visible = (key_index[None, :] <= query_index[:, None]) & (
         key_index[None, :] >= (query_index - offsets)[:, None]
     )
@@ -179,8 +181,8 @@
 
 def solution(mesh):
     groups, blocks = mesh.shape["grp"], mesh.shape["blk"]
-    inner = Mesh(mesh.devices.reshape(groups, blocks // KV, KV), ("grp", "zq", "w"))
-    rows = ("zq", "w")
+    inner = Mesh(mesh.devices.reshape(groups, KV, blocks // KV), ("grp", "w", "zq"))
+    rows = ("w", "zq")
     return jax.shard_map(
         local,
         mesh=inner,

time: 155 us -> 140 us (0.903)
  the two profiles are of different devices: /device:TPU:6 before, /device:TPU:8 now
where the time goes in v9:
time: 140 us
  blocking collectives  52.1 us (37%)
  waiting for transfers between devices  42 us (30%)
  starting transfers between devices  17.8 us (13%)
  local copies, waits for them, and re-layouts  12.4 us (9%)
  Pallas kernels  11 us (8%)
  other arithmetic  2.71 us (2%)
  matrix products  1.55 us (1%)
    all_to_all x1, blocking collectives, local(): parts = lax.all_to_all(packed, ('grp', 'w'), 0, 0, tiled=True)  33.8 us
    all_to_all x1, waiting for transfers between devices, local(): got = lax.all_to_all(send, 'w', 0, 0, tiled=True)  23.2 us
    ppermute x3, waiting for transfers between devices, local(): lax.ppermute(both_here, 'zq', [(i, (i + shift) % quarters) for i in range...  18.9 us
    all_to_all x1, blocking collectives, local(): attended = lax.all_to_all(attended, 'grp', 0, 0, tiled=True)  18.3 us
    pallas_call x1, Pallas kernels, attend_prefix(): pl.pallas_call(functools.partial(attend_kernel, inverse_root), grid=(coun...  11 us
    all_to_all x1, starting transfers between devices, local(): got = lax.all_to_all(send, 'w', 0, 0, tiled=True)  10.3 us
    unnamed x25, local copies, waits for them, and re-layouts  7.98 us
    ppermute x3, starting transfers between devices, local(): lax.ppermute(both_here, 'zq', [(i, (i + shift) % quarters) for i in range...  7.45 us
  transfers between devices with their start and end apart: 4, of which 4 were waited for; matrix products, arithmetic and copies ran while one was open for 1% of the time, Pallas kernels for 0%

profile of v9, /device:TPU:8, one launch (start us, length us, event | category | flops | bytes accessed | tf_op | source)
XLA Modules:
  0.0 139.9 jit_solution(4535627276078589380)
XLA Ops:
  0.0 0.0 copy-start.1
  0.0 0.0 copy-start.3
  0.0 0.0 copy-start.4
  0.0 1.1 copy.69
  1.2 1.0 copy.70
  2.2 0.0 copy-done.1
  2.2 0.0 copy-done.3
  2.3 0.0 copy-done.4
  2.4 0.5 broadcast.198
  2.9 1.2 reduce.10
  4.1 1.1 reshape.285
  5.2 10.3 %all-to-all-start = ((bf16[8,2,24704]{2,1,0:T(2,128)(2,1)}), bf16[8,2,24704]{2,1,0:T(2,128)(2,1)S(1)}, u32[]{:S(2)}, u32[]{:S(2)}) async-start(bf16[8,2,24704]{2,1,0:T(2,128)(2,1)} %reshape.285), calls=%async_computation | async-start | bytes 1581056 | tf_op jit(solution)/shard_map/all_to_all | solution.py:95
  15.6 23.2 %all-to-all-done = bf16[8,2,24704]{2,1,0:T(2,128)(2,1)S(1)} async-done(((bf16[8,2,24704]{2,1,0:T(2,128)(2,1)}), bf16[8,2,24704]{2,1,0:T(2,128)(2,1)S(1)}, u32[]{:S(2)}, u32[]{:S(2)}) %all-to-all-start) | async-done | bytes 790560 | tf_op jit(solution)/shard_map/all_to_all | solution.py:95
  38.8 2.5 %reshape.286 = bf16[8,1,49408]{2,1,0:T(2,128)(2,1)S(1)} reshape(bf16[8,2,24704]{2,1,0:T(2,128)(2,1)S(1)} %all-to-all-done) | data formatting | bytes 1581056
  41.2 0.1 copy.89
  41.3 0.1 fusion.24
  41.4 0.1 reshape.252
  41.5 0.0 copy-start.5
  41.5 0.1 reshape.253
  41.7 0.1 fusion.23
  41.8 3.0 %collective-permute-start.2 = (bf16[2,1032,128]{2,1,0:T(8,128)(2,1)S(1)}, bf16[2,1032,128]{2,1,0:T(8,128)(2,1)S(1)}, u32[]{:S(2)}, u32[]{:S(2)}) collective-permute-start(bf16[2,1032,128]{2,1,0:T(8,128)(2,1)S(1)} %get-tuple-element.23), channel_id=1, source_target_pairs={{0,3},{1,0},{2,1},{3,2},{4,7},{5,4},{6,5},{7,6},{8,11},{9,8},{10,9... | collective-permute-start | bytes 1585160 | tf_op jit(solution)/shard_map/ppermute | solution.py:119
  44.8 2.4 %collective-permute-start.1 = (bf16[2,1032,128]{2,1,0:T(8,128)(2,1)S(1)}, bf16[2,1032,128]{2,1,0:T(8,128)(2,1)S(1)}, u32[]{:S(2)}, u32[]{:S(2)}) collective-permute-start(bf16[2,1032,128]{2,1,0:T(8,128)(2,1)S(1)} %get-tuple-element.23), channel_id=1, source_target_pairs={{0,2},{1,3},{2,0},{3,1},{4,6},{5,7},{6,4},{7,5},{8,10},{9,11},{10,... | collective-permute-start | bytes 1585160 | tf_op jit(solution)/shard_map/ppermute | solution.py:119
  47.3 2.0 %collective-permute-start = (bf16[2,1032,128]{2,1,0:T(8,128)(2,1)S(1)}, bf16[2,1032,128]{2,1,0:T(8,128)(2,1)S(1)}, u32[]{:S(2)}, u32[]{:S(2)}) collective-permute-start(bf16[2,1032,128]{2,1,0:T(8,128)(2,1)S(1)} %get-tuple-element.23), channel_id=1, source_target_pairs={{0,1},{1,2},{2,3},{3,0},{4,5},{5,6},{6,7},{7,4},{8,9},{9,10},{10,1... | collective-permute-start | bytes 1585160 | tf_op jit(solution)/shard_map/ppermute | solution.py:119
  49.3 0.1 add_add_fusion
  49.3 0.0 copy-done.5
  49.3 0.1 reshape.258
  49.5 0.1 reshape.259
  49.5 0.1 add.105
  49.6 0.1 compare_and_fusion
  49.7 0.8 reshape.260
  50.5 0.1 reshape_reshape.3.query_ref
  50.7 4.6 %collective-permute-done.2 = bf16[2,1032,128]{2,1,0:T(8,128)(2,1)S(1)} collective-permute-done((bf16[2,1032,128]{2,1,0:T(8,128)(2,1)S(1)}, bf16[2,1032,128]{2,1,0:T(8,128)(2,1)S(1)}, u32[]{:S(2)}, u32[]{:S(2)}) %collective-permute-start.2) | collective-permute-done | bytes 528416 | tf_op jit(solution)/shard_map/ppermute | solution.py:119
  55.3 12.3 %collective-permute-done.1 = bf16[2,1032,128]{2,1,0:T(8,128)(2,1)S(1)} collective-permute-done((bf16[2,1032,128]{2,1,0:T(8,128)(2,1)S(1)}, bf16[2,1032,128]{2,1,0:T(8,128)(2,1)S(1)}, u32[]{:S(2)}, u32[]{:S(2)}) %collective-permute-start.1) | collective-permute-done | bytes 528416 | tf_op jit(solution)/shard_map/ppermute | solution.py:119
  67.6 1.9 %collective-permute-done = bf16[2,1032,128]{2,1,0:T(8,128)(2,1)S(1)} collective-permute-done((bf16[2,1032,128]{2,1,0:T(8,128)(2,1)S(1)}, bf16[2,1032,128]{2,1,0:T(8,128)(2,1)S(1)}, u32[]{:S(2)}, u32[]{:S(2)}) %collective-permute-start) | collective-permute-done | bytes 528416 | tf_op jit(solution)/shard_map/ppermute | solution.py:119
  69.5 0.3 pad_maximum_fusion
  69.8 0.1 slice_bitcast_fusion
  69.9 0.0 copy-start
  70.0 0.1 slice.62
  70.0 0.1 slice.64
  70.1 0.8 copy-done
  70.9 11.0 %shard_map.64 = (f32[1024,128]{1,0:T(8,128)S(1)}, f32[1024,1]{1,0:T(8,128)S(1)}, f32[1024,1]{1,0:T(8,128)S(1)}) custom-call(bf16[1024,128]{1,0:T(8,128)(2,1)S(1)} %reshape_reshape.3.query_ref, bf16[4096,128]{1,0:T(8,128)(2,1)S(1)} %bitcast.96, bf16[4096,128]{1,0:T(8,128)(2,1)S(1)} %bitcast.97), custom_call_target="tpu_custom_call" | custom-call | flops 3221225472 | bytes 2891776 | tf_op jit(solution)/shard_map/pallas_call | solution.py:50
  81.9 0.2 reduce.3
  82.2 0.1 reshape.257
  82.3 0.0 copy-done.2
  82.3 0.9 fusion.26
  83.2 0.3 fusion.7
  83.6 0.1 reshape.265
  83.7 0.1 copy.60
  83.8 0.4 fusion
  84.1 0.3 copy.93
  84.4 0.1 copy.91
  84.5 0.1 copy.62
  84.6 0.2 reduce.6
  84.9 0.1 reshape.267
  85.0 0.1 concatenate.15
  85.1 0.6 copy.58
  85.8 33.8 %all_to_all.26 = f32[128,1,1040]{2,1,0:T(1,128)S(1)} all-to-all(f32[128,1,1040]{2,1,0:T(1,128)S(1)} %copy.58), channel_id=1, replica_groups=mesh['grp'=16,'w'=8,'zq'=4] {'grp','w'}, dimensions={0} | all-to-all | bytes 1064960 | tf_op jit(solution)/shard_map/all_to_all | solution.py:166
  119.6 0.1 fusion.8
  119.7 0.1 copy.59
  119.8 0.2 fusion.2
  120.0 0.1 bitcast_divide_fusion
  120.1 0.4 broadcast_in_dim.38
  120.5 18.3 %all_to_all.27 = f32[16,1,8192]{2,1,0:T(1,128)S(1)} all-to-all(f32[16,1,8192]{2,1,0:T(1,128)S(1)} %broadcast_in_dim.38), channel_id=1, replica_groups=mesh['grp'=16,'w'=8,'zq'=4] {'grp'}, dimensions={0} | all-to-all | bytes 1048576 | tf_op jit(solution)/shard_map/all_to_all | solution.py:178
  138.8 1.1 copy.92
  (23 shorter events, 0.5 us)
Async XLA Ops:
  0.0 2.2 %copy-start.1 = (bf16[128,1024]{1,0:T(8,128)(2,1)S(1)}, bf16[128,1024]{1,0:T(8,128)(2,1)}, u32[]{:S(2)}) copy-start(bf16[128,1024]{1,0:T(8,128)(2,1)} %param.8) | copy-start | bytes 786436
  0.0 2.2 %copy-start.3 = (bf16[1,1024]{1,0:T(2,128)(2,1)S(1)}, bf16[1,1024]{1,0:T(2,128)(2,1)}, u32[]{:S(2)}) copy-start(bf16[1,1024]{1,0:T(2,128)(2,1)} %param.9) | copy-start | bytes 6148
  0.0 2.3 %copy-start.4 = (bf16[1,1024]{1,0:T(2,128)(2,1)S(1)}, bf16[1,1024]{1,0:T(2,128)(2,1)}, u32[]{:S(2)}) copy-start(bf16[1,1024]{1,0:T(2,128)(2,1)} %param.10) | copy-start | bytes 6148
  5.2 33.5 %all-to-all-start = ((bf16[8,2,24704]{2,1,0:T(2,128)(2,1)}), bf16[8,2,24704]{2,1,0:T(2,128)(2,1)S(1)}, u32[]{:S(2)}, u32[]{:S(2)}) async-start(bf16[8,2,24704]{2,1,0:T(2,128)(2,1)} %reshape.285), calls=%async_computation | async-start | bytes 1581056 | tf_op jit(solution)/shard_map/all_to_all | solution.py:95
  41.5 7.8 %copy-start.5 = (s32[512]{0:T(512)S(1)}, s32[512]{0:T(512)}, u32[]{:S(2)}) copy-start(s32[512]{0:T(512)} %param.11) | copy-start | bytes 6148
  41.8 13.5 %collective-permute-start.2 = (bf16[2,1032,128]{2,1,0:T(8,128)(2,1)S(1)}, bf16[2,1032,128]{2,1,0:T(8,128)(2,1)S(1)}, u32[]{:S(2)}, u32[]{:S(2)}) collective-permute-start(bf16[2,1032,128]{2,1,0:T(8,128)(2,1)S(1)} %get-tuple-element.23), channel_id=1, source_target_pairs={{0,3},{1,0},{2,1},{3,2},{4,7},{5,4},{6,5},{7,6},{8,11},{9,8},{10,9... | collective-permute-start | bytes 1585160 | tf_op jit(solution)/shard_map/ppermute | solution.py:119
  44.8 22.8 %collective-permute-start.1 = (bf16[2,1032,128]{2,1,0:T(8,128)(2,1)S(1)}, bf16[2,1032,128]{2,1,0:T(8,128)(2,1)S(1)}, u32[]{:S(2)}, u32[]{:S(2)}) collective-permute-start(bf16[2,1032,128]{2,1,0:T(8,128)(2,1)S(1)} %get-tuple-element.23), channel_id=1, source_target_pairs={{0,2},{1,3},{2,0},{3,1},{4,6},{5,7},{6,4},{7,5},{8,10},{9,11},{10,... | collective-permute-start | bytes 1585160 | tf_op jit(solution)/shard_map/ppermute | solution.py:119
  47.3 22.2 %collective-permute-start = (bf16[2,1032,128]{2,1,0:T(8,128)(2,1)S(1)}, bf16[2,1032,128]{2,1,0:T(8,128)(2,1)S(1)}, u32[]{:S(2)}, u32[]{:S(2)}) collective-permute-start(bf16[2,1032,128]{2,1,0:T(8,128)(2,1)S(1)} %get-tuple-element.23), channel_id=1, source_target_pairs={{0,1},{1,2},{2,3},{3,0},{4,5},{5,6},{6,7},{7,4},{8,9},{9,10},{10,1... | collective-permute-start | bytes 1585160 | tf_op jit(solution)/shard_map/ppermute | solution.py:119
  69.9 1.0 copy-start
  70.9 11.4 %copy-start.2 = (bf16[128,8,128]{2,1,0:T(8,128)(2,1)S(1)}, bf16[128,8,128]{2,1,0:T(8,128)(2,1)}, u32[]{:S(2)}) copy-start(bf16[128,8,128]{2,1,0:T(8,128)(2,1)} %reshape.260) | copy-start | bytes 786436

commit v10 on v9

--- a/solution.py
+++ b/solution.py
@@ -119,17 +119,20 @@
         lax.ppermute(both_here, "zq", [(i, (i + shift) % quarters) for i in range(quarters)])
         for shift in range(1, quarters)
     ]
-    both_all = jnp.stack(blocks)
-    keys_all, values_all = both_all[:, 0], both_all[:, 1]
-    prefix_k = keys_all[:, :local_keys].reshape(-1, HD)
-    draft_k = keys_all[:, local_keys:].reshape(-1, HD)
-    prefix_v = values_all[:, :local_keys].reshape(-1, HD)
-    draft_v = values_all[:, local_keys:].reshape(-1, HD)
+    draft_k = jnp.concatenate([block[0, local_keys:] for block in blocks], axis=0)
+    draft_v = jnp.concatenate([block[1, local_keys:] for block in blocks], axis=0)
     source_quarter = (quarter - lax.iota(jnp.int32, quarters)) % quarters
 
     block_rows = ways * rows
     query_rows = query_block.reshape(block_rows * group_heads, HD)
-    prefix_sum, prefix_peak, prefix_total = attend_prefix(query_rows, prefix_k, prefix_v, inverse_root)
+    pieces = [
+        attend_prefix(query_rows, block[0, :local_keys], block[1, :local_keys], inverse_root)
+        for block in blocks
+    ]
+    prefix_peak = functools.reduce(jnp.maximum, [piece[1] for piece in pieces])
+    piece_scales = [jnp.exp(piece[1] - prefix_peak) for piece in pieces]
+    prefix_total = sum(piece[2] * scale for piece, scale in zip(pieces, piece_scales))
+    prefix_sum = sum(piece[0] * scale for piece, scale in zip(pieces, piece_scales))
     prefix_sum = prefix_sum.reshape(block_rows, group_heads, HD)
     prefix_peak = prefix_peak.reshape(block_rows, group_heads)
     prefix_total = prefix_total.reshape(block_rows, group_heads)

time: 140 us -> 136 us (0.971)
  the two profiles are of different devices: /device:TPU:8 before, /device:TPU:6 now
where the time goes in v10:
time: 136 us; the launch traced here: 134 us
  blocking collectives  45.6 us (34%)
  waiting for transfers between devices  33.9 us (25%)
  starting transfers between devices  18.6 us (14%)
  local copies, waits for them, and re-layouts  15.2 us (11%)
  Pallas kernels  14 us (10%)
  other arithmetic  5.19 us (4%)
    all_to_all x1, blocking collectives, local(): parts = lax.all_to_all(packed, ('grp', 'w'), 0, 0, tiled=True)  29.9 us
    all_to_all x1, waiting for transfers between devices, local(): got = lax.all_to_all(send, 'w', 0, 0, tiled=True)  22.7 us
    all_to_all x1, blocking collectives, local(): attended = lax.all_to_all(attended, 'grp', 0, 0, tiled=True)  15.7 us
    pallas_call x4, Pallas kernels, attend_prefix(): pl.pallas_call(functools.partial(attend_kernel, inverse_root), grid=(coun...  14 us
    ppermute x3, waiting for transfers between devices, local(): lax.ppermute(both_here, 'zq', [(i, (i + shift) % quarters) for i in range...  11.1 us
    all_to_all x1, starting transfers between devices, local(): got = lax.all_to_all(send, 'w', 0, 0, tiled=True)  10.3 us
    unnamed x21, local copies, waits for them, and re-layouts  9.56 us
    ppermute x3, starting transfers between devices, local(): lax.ppermute(both_here, 'zq', [(i, (i + shift) % quarters) for i in range...  8.29 us
  transfers between devices with their start and end apart: 4, of which 2 were waited for; matrix products, arithmetic and copies ran while one was open for 1% of the time, Pallas kernels for 8%

profile of v10, /device:TPU:6, one launch (start us, length us, event | category | flops | bytes accessed | tf_op | source)
XLA Modules:
  0.0 133.7 jit_solution(6648033863686410455)
XLA Ops:
  0.0 0.7 reduce.1
  0.7 0.7 reduce.2
  1.4 1.1 copy.71
  2.5 1.0 copy.72
  3.5 1.0 copy.73
  4.6 0.5 broadcast.202
  5.1 1.2 reduce.20
  6.4 0.0 copy-start.3
  6.4 1.1 reshape.273
  7.5 10.3 %all-to-all-start = ((bf16[8,2,24704]{2,1,0:T(2,128)(2,1)}), bf16[8,2,24704]{2,1,0:T(2,128)(2,1)S(1)}, u32[]{:S(2)}, u32[]{:S(2)}) async-start(bf16[8,2,24704]{2,1,0:T(2,128)(2,1)} %reshape.273), calls=%async_computation | async-start | bytes 1581056 | tf_op jit(solution)/shard_map/all_to_all | solution.py:95
  17.8 0.1 add_add_fusion
  17.9 0.1 add.126
  18.0 0.1 reshape.244
  18.1 0.1 reshape.245
  18.2 0.1 compare_and_fusion
  18.3 22.7 %all-to-all-done = bf16[8,2,24704]{2,1,0:T(2,128)(2,1)S(1)} async-done(((bf16[8,2,24704]{2,1,0:T(2,128)(2,1)}), bf16[8,2,24704]{2,1,0:T(2,128)(2,1)S(1)}, u32[]{:S(2)}, u32[]{:S(2)}) %all-to-all-start) | async-done | bytes 790560 | tf_op jit(solution)/shard_map/all_to_all | solution.py:95
  41.0 2.5 %reshape.274 = bf16[8,1,49408]{2,1,0:T(2,128)(2,1)S(1)} reshape(bf16[8,2,24704]{2,1,0:T(2,128)(2,1)S(1)} %all-to-all-done) | data formatting | bytes 1581056
  43.5 0.1 copy.91
  43.6 0.1 fusion.36
  43.6 0.1 reshape.240
  43.8 0.1 reshape.241
  44.0 0.1 pad_maximum_fusion
  44.0 1.9 %collective-permute-start = (bf16[2,1032,128]{2,1,0:T(8,128)(2,1)S(1)}, bf16[2,1032,128]{2,1,0:T(8,128)(2,1)S(1)}, u32[]{:S(2)}, u32[]{:S(2)}) collective-permute-start(bf16[2,1032,128]{2,1,0:T(8,128)(2,1)S(1)} %pad_maximum_fusion), channel_id=1, source_target_pairs={{0,1},{1,2},{2,3},{3,0},{4,5},{5,6},{6,7},{7,4},{8,9},{9,10},{10,1... | collective-permute-start | bytes 1585160 | tf_op jit(solution)/shard_map/ppermute | solution.py:119
  46.0 0.1 reshape_reshape.3.query_ref
  46.1 0.8 reshape.246
  47.0 3.6 %collective-permute-start.2 = (bf16[2,1032,128]{2,1,0:T(8,128)(2,1)S(1)}, bf16[2,1032,128]{2,1,0:T(8,128)(2,1)S(1)}, u32[]{:S(2)}, u32[]{:S(2)}) collective-permute-start(bf16[2,1032,128]{2,1,0:T(8,128)(2,1)S(1)} %pad_maximum_fusion), channel_id=1, source_target_pairs={{0,3},{1,0},{2,1},{3,2},{4,7},{5,4},{6,5},{7,6},{8,11},{9,8},{10,9... | collective-permute-start | bytes 1585160 | tf_op jit(solution)/shard_map/ppermute | solution.py:119
  50.6 2.7 %collective-permute-start.1 = (bf16[2,1032,128]{2,1,0:T(8,128)(2,1)S(1)}, bf16[2,1032,128]{2,1,0:T(8,128)(2,1)S(1)}, u32[]{:S(2)}, u32[]{:S(2)}) collective-permute-start(bf16[2,1032,128]{2,1,0:T(8,128)(2,1)S(1)} %pad_maximum_fusion), channel_id=1, source_target_pairs={{0,2},{1,3},{2,0},{3,1},{4,6},{5,7},{6,4},{7,5},{8,10},{9,11},{10,... | collective-permute-start | bytes 1585160 | tf_op jit(solution)/shard_map/ppermute | solution.py:119
  53.3 3.5 %shard_map.64 = (f32[1024,128]{1,0:T(8,128)S(1)}, f32[1024,1]{1,0:T(8,128)S(1)}, f32[1024,1]{1,0:T(8,128)S(1)}) custom-call(bf16[1024,128]{1,0:T(8,128)(2,1)S(1)} %reshape_reshape.3.query_ref, bf16[1024,128]{1,0:T(8,128)(2,1)S(1)} %slice_bitcast_fusion.7.key_ref, bf16[1024,128]{1,0:T(8,128)(2,1)S(1)} %slice_bitcast_fusion.6.value_ref), custom_call_target="tpu_custom_call" | custom-call | flops 805306368 | bytes 1318912 | tf_op jit(solution)/shard_map/pallas_call | solution.py:50
  56.9 0.0 collective-permute-done
  56.9 3.5 %shard_map.65 = (f32[1024,128]{1,0:T(8,128)S(1)}, f32[1024,1]{1,0:T(8,128)S(1)}, f32[1024,1]{1,0:T(8,128)S(1)}) custom-call(bf16[1024,128]{1,0:T(8,128)(2,1)S(1)} %reshape_reshape.3.query_ref, bf16[1024,128]{1,0:T(8,128)(2,1)S(1)} %get-tuple-element.51.key_ref, bf16[1024,128]{1,0:T(8,128)(2,1)S(1)} %get-tuple-element.50.value_ref), custom_call_target="tpu_custom_call" | custom-call | flops 805306368 | bytes 1318912 | tf_op jit(solution)/shard_map/pallas_call | solution.py:50
  60.4 11.1 %collective-permute-done.1 = bf16[2,1032,128]{2,1,0:T(8,128)(2,1)S(1)} collective-permute-done((bf16[2,1032,128]{2,1,0:T(8,128)(2,1)S(1)}, bf16[2,1032,128]{2,1,0:T(8,128)(2,1)S(1)}, u32[]{:S(2)}, u32[]{:S(2)}) %collective-permute-start.1) | collective-permute-done | bytes 528416 | tf_op jit(solution)/shard_map/ppermute | solution.py:119
  71.6 0.7 copy-done.1
  72.4 3.5 %shard_map.66 = (f32[1024,128]{1,0:T(8,128)S(1)}, f32[1024,1]{1,0:T(8,128)S(1)}, f32[1024,1]{1,0:T(8,128)S(1)}) custom-call(bf16[1024,128]{1,0:T(8,128)(2,1)S(1)} %reshape_reshape.3.query_ref, bf16[1024,128]{1,0:T(8,128)(2,1)S(1)} %get-tuple-element.53.key_ref, bf16[1024,128]{1,0:T(8,128)(2,1)S(1)} %get-tuple-element.52.value_ref), custom_call_target="tpu_custom_call" | custom-call | flops 805306368 | bytes 1318912 | tf_op jit(solution)/shard_map/pallas_call | solution.py:50
  75.9 0.0 collective-permute-done.2
  75.9 0.0 copy-start
  75.9 0.8 copy-done
  76.7 3.5 %shard_map.67 = (f32[1024,128]{1,0:T(8,128)S(1)}, f32[1024,1]{1,0:T(8,128)S(1)}, f32[1024,1]{1,0:T(8,128)S(1)}) custom-call(bf16[1024,128]{1,0:T(8,128)(2,1)S(1)} %reshape_reshape.3.query_ref, bf16[1024,128]{1,0:T(8,128)(2,1)S(1)} %get-tuple-element.55.key_ref, bf16[1024,128]{1,0:T(8,128)(2,1)S(1)} %get-tuple-element.54.value_ref), custom_call_target="tpu_custom_call" | custom-call | flops 805306368 | bytes 1318912 | tf_op jit(solution)/shard_map/pallas_call | solution.py:50
  80.2 0.0 copy-start.2
  80.2 1.2 add_reduce_fusion
  81.4 0.1 reshape.249
  81.4 0.1 reshape.243
  81.5 0.7 slice_bitcast_fusion.8
  82.2 0.7 slice_bitcast_fusion.9
  82.9 0.0 copy-done.2
  82.9 0.2 fusion.38
  83.1 0.1 copy.62
  83.2 0.1 reshape.251
  83.4 0.1 fusion.9
  83.4 0.1 copy.64
  83.6 0.3 fusion.11
  83.9 0.6 add_bitcast_fusion
  84.5 0.4 fusion
  84.9 0.3 copy.95
  85.2 0.1 copy.93
  85.3 0.1 concatenate.23
  85.4 0.6 copy.60
  86.0 29.9 %all_to_all.26 = f32[128,1,1040]{2,1,0:T(1,128)S(1)} all-to-all(f32[128,1,1040]{2,1,0:T(1,128)S(1)} %copy.60), channel_id=1, replica_groups=mesh['grp'=16,'w'=8,'zq'=4] {'grp','w'}, dimensions={0} | all-to-all | bytes 1064960 | tf_op jit(solution)/shard_map/all_to_all | solution.py:169
  116.0 0.1 fusion.12
  116.1 0.1 copy.61
  116.2 0.2 fusion.2
  116.4 0.1 bitcast_divide_fusion
  116.5 0.4 broadcast_in_dim.38
  116.9 15.7 %all_to_all.27 = f32[16,1,8192]{2,1,0:T(1,128)S(1)} all-to-all(f32[16,1,8192]{2,1,0:T(1,128)S(1)} %broadcast_in_dim.38), channel_id=1, replica_groups=mesh['grp'=16,'w'=8,'zq'=4] {'grp'}, dimensions={0} | all-to-all | bytes 1048576 | tf_op jit(solution)/shard_map/all_to_all | solution.py:181
  132.6 1.1 copy.94
  (28 shorter events, 0.5 us)
Async XLA Ops:
  6.4 11.6 %copy-start.3 = (s32[512]{0:T(512)S(1)}, s32[512]{0:T(512)}, u32[]{:S(2)}) copy-start(s32[512]{0:T(512)} %param.11) | copy-start | bytes 6148
  7.5 33.5 %all-to-all-start = ((bf16[8,2,24704]{2,1,0:T(2,128)(2,1)}), bf16[8,2,24704]{2,1,0:T(2,128)(2,1)S(1)}, u32[]{:S(2)}, u32[]{:S(2)}) async-start(bf16[8,2,24704]{2,1,0:T(2,128)(2,1)} %reshape.273), calls=%async_computation | async-start | bytes 1581056 | tf_op jit(solution)/shard_map/all_to_all | solution.py:95
  44.0 12.8 %collective-permute-start = (bf16[2,1032,128]{2,1,0:T(8,128)(2,1)S(1)}, bf16[2,1032,128]{2,1,0:T(8,128)(2,1)S(1)}, u32[]{:S(2)}, u32[]{:S(2)}) collective-permute-start(bf16[2,1032,128]{2,1,0:T(8,128)(2,1)S(1)} %pad_maximum_fusion), channel_id=1, source_target_pairs={{0,1},{1,2},{2,3},{3,0},{4,5},{5,6},{6,7},{7,4},{8,9},{9,10},{10,1... | collective-permute-start | bytes 1585160 | tf_op jit(solution)/shard_map/ppermute | solution.py:119
  47.0 28.9 %collective-permute-start.2 = (bf16[2,1032,128]{2,1,0:T(8,128)(2,1)S(1)}, bf16[2,1032,128]{2,1,0:T(8,128)(2,1)S(1)}, u32[]{:S(2)}, u32[]{:S(2)}) collective-permute-start(bf16[2,1032,128]{2,1,0:T(8,128)(2,1)S(1)} %pad_maximum_fusion), channel_id=1, source_target_pairs={{0,3},{1,0},{2,1},{3,2},{4,7},{5,4},{6,5},{7,6},{8,11},{9,8},{10,9... | collective-permute-start | bytes 1585160 | tf_op jit(solution)/shard_map/ppermute | solution.py:119
  50.6 21.0 %collective-permute-start.1 = (bf16[2,1032,128]{2,1,0:T(8,128)(2,1)S(1)}, bf16[2,1032,128]{2,1,0:T(8,128)(2,1)S(1)}, u32[]{:S(2)}, u32[]{:S(2)}) collective-permute-start(bf16[2,1032,128]{2,1,0:T(8,128)(2,1)S(1)} %pad_maximum_fusion), channel_id=1, source_target_pairs={{0,2},{1,3},{2,0},{3,1},{4,6},{5,7},{6,4},{7,5},{8,10},{9,11},{10,... | collective-permute-start | bytes 1585160 | tf_op jit(solution)/shard_map/ppermute | solution.py:119
  71.6 0.8 copy-start.1
  75.9 0.8 copy-start
  80.2 2.7 %copy-start.2 = (bf16[128,8,128]{2,1,0:T(8,128)(2,1)S(1)}, bf16[128,8,128]{2,1,0:T(8,128)(2,1)}, u32[]{:S(2)}) copy-start(bf16[128,8,128]{2,1,0:T(8,128)(2,1)} %reshape.246) | copy-start | bytes 786436

commit v11 on v10

--- a/solution.py
+++ b/solution.py
@@ -89,32 +89,31 @@
     value_heads = prefix_values.reshape(positions, KV, HD).transpose(1, 0, 2).reshape(KV, -1)
     draft_key_heads = draft_keys.reshape(KV, HD)
     draft_value_heads = draft_values.reshape(KV, HD)
-    send = jnp.concatenate(
-        [query_heads, key_heads, draft_key_heads, value_heads, draft_value_heads], axis=1
-    )
+    send = jnp.concatenate([key_heads, draft_key_heads, value_heads, draft_value_heads], axis=1)
     got = lax.all_to_all(send, "w", 0, 0, tiled=True)
 
-    query_size = rows * group_heads * HD
     key_size = positions * HD
-    cut = [query_size, key_size, HD, key_size, HD]
+    cut = [key_size, HD, key_size, HD]
     starts = [sum(cut[:n]) for n in range(len(cut))]
-    query_block = got[:, : query_size].reshape(ways * rows, group_heads, HD)
     keys_here = jnp.concatenate(
         [
-            got[:, starts[1] : starts[1] + key_size].reshape(ways * positions, HD),
-            got[:, starts[2] : starts[2] + HD],
+            got[:, starts[0] : starts[0] + key_size].reshape(ways * positions, HD),
+            got[:, starts[1] : starts[1] + HD],
         ],
         axis=0,
     )
     values_here = jnp.concatenate(
         [
-            got[:, starts[3] : starts[3] + key_size].reshape(ways * positions, HD),
-            got[:, starts[4] : starts[4] + HD],
+            got[:, starts[2] : starts[2] + key_size].reshape(ways * positions, HD),
+            got[:, starts[3] : starts[3] + HD],
         ],
         axis=0,
     )
+    both_here = jnp.stack([keys_here, values_here])
+    query_heads, both_here = lax.optimization_barrier((query_heads, both_here))
+    query_block = lax.all_to_all(query_heads, "w", 0, 0, tiled=True)
+    query_block = query_block.reshape(ways * rows, group_heads, HD)
     local_keys = ways * positions
-    both_here = jnp.stack([keys_here, values_here])
     blocks = [both_here] + [
         lax.ppermute(both_here, "zq", [(i, (i + shift) % quarters) for i in range(quarters)])
         for shift in range(1, quarters)

time: 136 us -> 143 us (1.051)
  blocking collectives: 45.6 us -> 52.5 us
  waiting for transfers between devices: 33.9 us -> 30.1 us
  starting transfers between devices: 18.6 us -> 21.2 us
  other arithmetic: 5.19 us -> 7.37 us
    all_to_all x0 -> x1, waiting for transfers between devices: none -> 13.1 us  [local(): query_block = lax.all_to_all(query_heads, 'w', 0, 0, tiled=True)]
    ppermute x3, waiting for transfers between devices: 11.1 us -> 0.01 us  [local(): lax.ppermute(both_here, 'zq', [(i, (i + shift) % quarters) for i in range...]
    all_to_all x1, waiting for transfers between devices: 22.7 us -> 16.9 us  [local(): got = lax.all_to_all(send, 'w', 0, 0, tiled=True)]
    all_to_all x1, blocking collectives: 29.9 us -> 34.2 us  [local(): parts = lax.all_to_all(packed, ('grp', 'w'), 0, 0, tiled=True)]
    all_to_all x0 -> x1, starting transfers between devices: none -> 3.41 us  [local(): query_block = lax.all_to_all(query_heads, 'w', 0, 0, tiled=True)]
    unnamed x21 -> x17, local copies, waits for them, and re-layouts: 9.56 us -> 6.53 us
    all_to_all x1, blocking collectives: 15.7 us -> 18.3 us  [local(): attended = lax.all_to_all(attended, 'grp', 0, 0, tiled=True)]
    all_to_all x0 -> x2, other arithmetic: none -> 2.37 us  [local(): query_block = lax.all_to_all(query_heads, 'w', 0, 0, tiled=True)]
  transfers between devices with their start and end apart: 4 -> 5, of which waited for: 2 -> 2; matrix products, arithmetic and copies ran while one was open for 1% -> 4% of each run, Pallas kernels for 8% -> 7%
where the time goes in v11:
time: 143 us; the launch traced here: 141 us
  blocking collectives  52.5 us (37%)
  waiting for transfers between devices  30.1 us (21%)
  starting transfers between devices  21.2 us (15%)
  local copies, waits for them, and re-layouts  14.2 us (10%)
  Pallas kernels  14 us (10%)
  other arithmetic  7.37 us (5%)
    all_to_all x1, blocking collectives, local(): parts = lax.all_to_all(packed, ('grp', 'w'), 0, 0, tiled=True)  34.2 us
    all_to_all x1, blocking collectives, local(): attended = lax.all_to_all(attended, 'grp', 0, 0, tiled=True)  18.3 us
    all_to_all x1, waiting for transfers between devices, local(): got = lax.all_to_all(send, 'w', 0, 0, tiled=True)  16.9 us
    pallas_call x4, Pallas kernels, attend_prefix(): pl.pallas_call(functools.partial(attend_kernel, inverse_root), grid=(coun...  14 us
    all_to_all x1, waiting for transfers between devices, local(): query_block = lax.all_to_all(query_heads, 'w', 0, 0, tiled=True)  13.1 us
    all_to_all x1, starting transfers between devices, local(): got = lax.all_to_all(send, 'w', 0, 0, tiled=True)  10.4 us
    ppermute x3, starting transfers between devices, local(): lax.ppermute(both_here, 'zq', [(i, (i + shift) % quarters) for i in range...  7.39 us
    unnamed x17, local copies, waits for them, and re-layouts  6.53 us
  transfers between devices with their start and end apart: 5, of which 2 were waited for; matrix products, arithmetic and copies ran while one was open for 4% of the time, Pallas kernels for 7%

profile of v11, /device:TPU:6, one launch (start us, length us, event | category | flops | bytes accessed | tf_op | source)
XLA Modules:
  0.0 140.6 jit_solution(9593931617467099763)
XLA Ops:
  0.0 1.0 copy.60
  1.0 0.7 reduce.2
  1.7 0.7 reduce.1
  2.4 1.0 copy.59
  3.5 0.5 broadcast.204
  4.0 1.0 reduce.22
  5.0 0.0 copy-start
  5.0 0.9 reshape.279
  6.0 10.4 %all-to-all-start = ((bf16[8,2,16512]{2,1,0:T(2,128)(2,1)}), bf16[8,2,16512]{2,1,0:T(2,128)(2,1)S(1)}, u32[]{:S(2)}, u32[]{:S(2)}) async-start(bf16[8,2,16512]{2,1,0:T(2,128)(2,1)} %reshape.279), calls=%async_computation | async-start | bytes 1056768 | tf_op jit(solution)/shard_map/all_to_all | solution.py:93
  16.4 0.2 copy.58
  16.6 0.1 reshape.248
  16.7 0.1 reshape.249
  16.8 0.1 add_add_fusion
  16.9 0.1 add.126
  17.0 0.1 compare_and_fusion
  17.0 16.9 %all-to-all-done = bf16[8,2,16512]{2,1,0:T(2,128)(2,1)S(1)} async-done(((bf16[8,2,16512]{2,1,0:T(2,128)(2,1)}), bf16[8,2,16512]{2,1,0:T(2,128)(2,1)S(1)}, u32[]{:S(2)}, u32[]{:S(2)}) %all-to-all-start) | async-done | bytes 528416 | tf_op jit(solution)/shard_map/all_to_all | solution.py:93
  34.0 1.0 reshape.280
  35.0 0.1 copy.79
  35.1 0.1 reshape.244
  35.2 0.1 reshape.245
  35.4 0.1 pad_maximum_fusion
  35.5 2.4 %collective-permute-start.2 = (bf16[2,1032,128]{2,1,0:T(8,128)(2,1)S(1)}, bf16[2,1032,128]{2,1,0:T(8,128)(2,1)S(1)}, u32[]{:S(2)}, u32[]{:S(2)}) collective-permute-start(bf16[2,1032,128]{2,1,0:T(8,128)(2,1)S(1)} %pad_maximum_fusion), channel_id=1, source_target_pairs={{0,3},{1,0},{2,1},{3,2},{4,7},{5,4},{6,5},{7,6},{8,11},{9,8},{10,9... | collective-permute-start | bytes 1585160 | tf_op jit(solution)/shard_map/ppermute | solution.py:118
  37.9 3.1 %collective-permute-start.1 = (bf16[2,1032,128]{2,1,0:T(8,128)(2,1)S(1)}, bf16[2,1032,128]{2,1,0:T(8,128)(2,1)}, u32[]{:S(2)}, u32[]{:S(2)}) collective-permute-start(bf16[2,1032,128]{2,1,0:T(8,128)(2,1)S(1)} %pad_maximum_fusion), channel_id=1, source_target_pairs={{0,2},{1,3},{2,0},{3,1},{4,6},{5,7},{6,4},{7,5},{8,10},{9,11},{10,... | collective-permute-start | bytes 1585160 | tf_op jit(solution)/shard_map/ppermute | solution.py:118
  41.0 1.9 %collective-permute-start = (bf16[2,1032,128]{2,1,0:T(8,128)(2,1)S(1)}, bf16[2,1032,128]{2,1,0:T(8,128)(2,1)}, u32[]{:S(2)}, u32[]{:S(2)}) collective-permute-start(bf16[2,1032,128]{2,1,0:T(8,128)(2,1)S(1)} %pad_maximum_fusion), channel_id=1, source_target_pairs={{0,1},{1,2},{2,3},{3,0},{4,5},{5,6},{6,7},{7,4},{8,9},{9,10},{10,1... | collective-permute-start | bytes 1585160 | tf_op jit(solution)/shard_map/ppermute | solution.py:118
  42.9 0.8 reduce.23
  43.7 0.9 reshape.281
  44.6 3.4 %all-to-all-start.1 = ((bf16[8,2,8192]{2,1,0:T(2,128)(2,1)}), bf16[8,2,8192]{2,1,0:T(2,128)(2,1)S(1)}, u32[]{:S(2)}, u32[]{:S(2)}) async-start(bf16[8,2,8192]{2,1,0:T(2,128)(2,1)} %reshape.281), calls=%async_computation.1 | async-start | bytes 524288 | tf_op jit(solution)/shard_map/all_to_all | solution.py:114
  48.1 13.1 %all-to-all-done.1 = bf16[8,2,8192]{2,1,0:T(2,128)(2,1)S(1)} async-done(((bf16[8,2,8192]{2,1,0:T(2,128)(2,1)}), bf16[8,2,8192]{2,1,0:T(2,128)(2,1)S(1)}, u32[]{:S(2)}, u32[]{:S(2)}) %all-to-all-start.1) | async-done | bytes 262176 | tf_op jit(solution)/shard_map/all_to_all | solution.py:114
  61.2 0.3 reshape.282
  61.5 1.6 %reduce.3 = bf16[8,16384]{1,0:T(8,128)(2,1)S(1)} reduce(bf16[8,1,16384]{2,1,0:T(2,128)(2,1)S(1)} %reshape.282, bf16[]{:T(256)} %constant.73), dimensions={1}, to_apply=%all_to_all.27.reduce_sub_computation | reduce | bytes 524290 | tf_op jit(solution)/shard_map/all_to_all | solution.py:114
  63.0 0.8 reshape.250
  63.8 0.1 reshape_reshape.3.query_ref
  64.0 3.5 %shard_map.64 = (f32[1024,128]{1,0:T(8,128)S(1)}, f32[1024,1]{1,0:T(8,128)S(1)}, f32[1024,1]{1,0:T(8,128)S(1)}) custom-call(bf16[1024,128]{1,0:T(8,128)(2,1)S(1)} %reshape_reshape.3.query_ref, bf16[1024,128]{1,0:T(8,128)(2,1)S(1)} %get-tuple-element.52.key_ref, bf16[1024,128]{1,0:T(8,128)(2,1)S(1)} %get-tuple-element.51.value_ref), custom_call_target="tpu_custom_call" | custom-call | flops 805306368 | bytes 1318912 | tf_op jit(solution)/shard_map/pallas_call | solution.py:50
  67.5 0.0 collective-permute-done.2
  67.5 3.5 %shard_map.67 = (f32[1024,128]{1,0:T(8,128)S(1)}, f32[1024,1]{1,0:T(8,128)S(1)}, f32[1024,1]{1,0:T(8,128)S(1)}) custom-call(bf16[1024,128]{1,0:T(8,128)(2,1)S(1)} %reshape_reshape.3.query_ref, bf16[1024,128]{1,0:T(8,128)(2,1)S(1)} %get-tuple-element.58.key_ref, bf16[1024,128]{1,0:T(8,128)(2,1)S(1)} %get-tuple-element.57.value_ref), custom_call_target="tpu_custom_call" | custom-call | flops 805306368 | bytes 1318912 | tf_op jit(solution)/shard_map/pallas_call | solution.py:50
  71.1 1.1 slice_bitcast_fusion.2
  72.1 3.5 %shard_map.66 = (f32[1024,128]{1,0:T(8,128)S(1)}, f32[1024,1]{1,0:T(8,128)S(1)}, f32[1024,1]{1,0:T(8,128)S(1)}) custom-call(bf16[1024,128]{1,0:T(8,128)(2,1)S(1)} %reshape_reshape.3.query_ref, bf16[1024,128]{1,0:T(8,128)(2,1)S(1)} %get-tuple-element.56.key_ref, bf16[1024,128]{1,0:T(8,128)(2,1)S(1)} %get-tuple-element.55.value_ref), custom_call_target="tpu_custom_call" | custom-call | flops 805306368 | bytes 1318912 | tf_op jit(solution)/shard_map/pallas_call | solution.py:50
  75.6 1.1 slice_bitcast_fusion.4
  76.7 3.5 %shard_map.65 = (f32[1024,128]{1,0:T(8,128)S(1)}, f32[1024,1]{1,0:T(8,128)S(1)}, f32[1024,1]{1,0:T(8,128)S(1)}) custom-call(bf16[1024,128]{1,0:T(8,128)(2,1)S(1)} %reshape_reshape.3.query_ref, bf16[1024,128]{1,0:T(8,128)(2,1)S(1)} %get-tuple-element.54.key_ref, bf16[1024,128]{1,0:T(8,128)(2,1)S(1)} %get-tuple-element.53.value_ref), custom_call_target="tpu_custom_call" | custom-call | flops 805306368 | bytes 1318912 | tf_op jit(solution)/shard_map/pallas_call | solution.py:50
  80.2 0.0 copy-start.1
  80.2 1.2 add_reduce_fusion
  81.4 0.1 reshape.247
  81.5 0.1 reshape.253
  81.6 0.7 slice_bitcast_fusion.9
  82.3 0.7 slice_bitcast_fusion.10
  83.0 0.2 fusion.38
  83.2 0.1 copy.49
  83.4 0.3 fusion.11
  83.7 0.6 add_bitcast_fusion
  84.3 0.4 fusion
  84.6 0.3 copy.82
  85.0 0.1 copy.80
  85.1 0.1 copy.51
  85.2 0.1 reshape.255
  85.3 0.1 concatenate.23
  85.4 0.6 copy.47
  86.1 34.2 %all_to_all.35 = f32[128,1,1040]{2,1,0:T(1,128)S(1)} all-to-all(f32[128,1,1040]{2,1,0:T(1,128)S(1)} %copy.47), channel_id=1, replica_groups=mesh['grp'=16,'w'=8,'zq'=4] {'grp','w'}, dimensions={0} | all-to-all | bytes 1064960 | tf_op jit(solution)/shard_map/all_to_all | solution.py:168
  120.3 0.1 fusion.12
  120.4 0.1 copy.48
  120.5 0.2 fusion.2
  120.7 0.1 bitcast_divide_fusion
  120.8 0.4 broadcast_in_dim.38
  121.2 18.3 %all_to_all.36 = f32[16,1,8192]{2,1,0:T(1,128)S(1)} all-to-all(f32[16,1,8192]{2,1,0:T(1,128)S(1)} %broadcast_in_dim.38), channel_id=1, replica_groups=mesh['grp'=16,'w'=8,'zq'=4] {'grp'}, dimensions={0} | all-to-all | bytes 1048576 | tf_op jit(solution)/shard_map/all_to_all | solution.py:180
  139.5 1.1 copy.81
  (26 shorter events, 0.5 us)
Async XLA Ops:
  5.0 11.4 %copy-start = (bf16[16,8192]{1,0:T(8,128)(2,1)S(1)}, bf16[16,8192]{1,0:T(8,128)(2,1)}, u32[]{:S(2)}) copy-start(bf16[16,8192]{1,0:T(8,128)(2,1)} %param.6) | copy-start | bytes 786436
  6.0 10.6 %copy-start.2 = (s32[512]{0:T(512)S(1)}, s32[512]{0:T(512)}, u32[]{:S(2)}) copy-start(s32[512]{0:T(512)} %param.11) | copy-start | bytes 6148
  6.0 28.0 %all-to-all-start = ((bf16[8,2,16512]{2,1,0:T(2,128)(2,1)}), bf16[8,2,16512]{2,1,0:T(2,128)(2,1)S(1)}, u32[]{:S(2)}, u32[]{:S(2)}) async-start(bf16[8,2,16512]{2,1,0:T(2,128)(2,1)} %reshape.279), calls=%async_computation | async-start | bytes 1056768 | tf_op jit(solution)/shard_map/all_to_all | solution.py:93
  35.5 32.0 %collective-permute-start.2 = (bf16[2,1032,128]{2,1,0:T(8,128)(2,1)S(1)}, bf16[2,1032,128]{2,1,0:T(8,128)(2,1)S(1)}, u32[]{:S(2)}, u32[]{:S(2)}) collective-permute-start(bf16[2,1032,128]{2,1,0:T(8,128)(2,1)S(1)} %pad_maximum_fusion), channel_id=1, source_target_pairs={{0,3},{1,0},{2,1},{3,2},{4,7},{5,4},{6,5},{7,6},{8,11},{9,8},{10,9... | collective-permute-start | bytes 1585160 | tf_op jit(solution)/shard_map/ppermute | solution.py:118
  37.9 33.2 %collective-permute-start.1 = (bf16[2,1032,128]{2,1,0:T(8,128)(2,1)S(1)}, bf16[2,1032,128]{2,1,0:T(8,128)(2,1)}, u32[]{:S(2)}, u32[]{:S(2)}) collective-permute-start(bf16[2,1032,128]{2,1,0:T(8,128)(2,1)S(1)} %pad_maximum_fusion), channel_id=1, source_target_pairs={{0,2},{1,3},{2,0},{3,1},{4,6},{5,7},{6,4},{7,5},{8,10},{9,11},{10,... | collective-permute-start | bytes 1585160 | tf_op jit(solution)/shard_map/ppermute | solution.py:118
  41.0 34.7 %collective-permute-start = (bf16[2,1032,128]{2,1,0:T(8,128)(2,1)S(1)}, bf16[2,1032,128]{2,1,0:T(8,128)(2,1)}, u32[]{:S(2)}, u32[]{:S(2)}) collective-permute-start(bf16[2,1032,128]{2,1,0:T(8,128)(2,1)S(1)} %pad_maximum_fusion), channel_id=1, source_target_pairs={{0,1},{1,2},{2,3},{3,0},{4,5},{5,6},{6,7},{7,4},{8,9},{9,10},{10,1... | collective-permute-start | bytes 1585160 | tf_op jit(solution)/shard_map/ppermute | solution.py:118
  44.6 16.6 %all-to-all-start.1 = ((bf16[8,2,8192]{2,1,0:T(2,128)(2,1)}), bf16[8,2,8192]{2,1,0:T(2,128)(2,1)S(1)}, u32[]{:S(2)}, u32[]{:S(2)}) async-start(bf16[8,2,8192]{2,1,0:T(2,128)(2,1)} %reshape.281), calls=%async_computation.1 | async-start | bytes 524288 | tf_op jit(solution)/shard_map/all_to_all | solution.py:114
  80.2 2.8 %copy-start.1 = (bf16[128,8,128]{2,1,0:T(8,128)(2,1)S(1)}, bf16[128,8,128]{2,1,0:T(8,128)(2,1)}, u32[]{:S(2)}) copy-start(bf16[128,8,128]{2,1,0:T(8,128)(2,1)} %reshape.250) | copy-start | bytes 786436

commit v12 on v10

--- a/solution.py
+++ b/solution.py
@@ -24,54 +24,55 @@
     )
 
 
-def attend_kernel(inverse_root, query_ref, key_ref, value_ref, sum_ref, peak_ref, total_ref):
+def attend_kernel(
+    inverse_root, query_ref, key_ref, value_ref, sum_in, peak_in, total_in, sum_ref, peak_ref, total_ref
+):
     scores = lax.dot_general(
         query_ref[...],
         key_ref[...],
         (((1,), (1,)), ((), ())),
         preferred_element_type=jnp.float32,
     ) * inverse_root
-    peak = jnp.max(scores, axis=1, keepdims=True)
+    old_peak = peak_in[...]
+    peak = jnp.maximum(old_peak, jnp.max(scores, axis=1, keepdims=True))
+    scale = jnp.exp(old_peak - peak)
     weights = jnp.exp(scores - peak)
-    total_ref[...] = jnp.sum(weights, axis=1, keepdims=True)
+    total_ref[...] = total_in[...] * scale + jnp.sum(weights, axis=1, keepdims=True)
     peak_ref[...] = peak
     high = weights.astype(jnp.bfloat16)
     low = (weights - high.astype(jnp.float32)).astype(jnp.bfloat16)
     values = value_ref[...]
-    sum_ref[...] = jnp.dot(high, values, preferred_element_type=jnp.float32) + jnp.dot(
-        low, values, preferred_element_type=jnp.float32
-    )
-
-
-def attend_prefix(query_rows, keys, values, inverse_root):
+    sum_ref[...] = sum_in[...] * scale + (
+        jnp.dot(high, values, preferred_element_type=jnp.float32)
+        + jnp.dot(low, values, preferred_element_type=jnp.float32)
+    )
+
+
+def attend_prefix(query_rows, keys, values, inverse_root, state):
     count, width = query_rows.shape
     length = keys.shape[0]
     tile = 256
+    row_block = pl.BlockSpec((tile, width), lambda i: (i, 0))
+    column_block = pl.BlockSpec((tile, 1), lambda i: (i, 0))
+    whole = pl.BlockSpec((length, width), lambda i: (0, 0))
     return pl.pallas_call(
         functools.partial(attend_kernel, inverse_root),
         grid=(count // tile,),
-        in_specs=[
-            pl.BlockSpec((tile, width), lambda i: (i, 0)),
-            pl.BlockSpec((length, width), lambda i: (0, 0)),
-            pl.BlockSpec((length, width), lambda i: (0, 0)),
-        ],
-        out_specs=[
-            pl.BlockSpec((tile, width), lambda i: (i, 0)),
-            pl.BlockSpec((tile, 1), lambda i: (i, 0)),
-            pl.BlockSpec((tile, 1), lambda i: (i, 0)),
-        ],
+        in_specs=[row_block, whole, whole, row_block, column_block, column_block],
+        out_specs=[row_block, column_block, column_block],
         out_shape=[
             jax.ShapeDtypeStruct((count, width), jnp.float32),
             jax.ShapeDtypeStruct((count, 1), jnp.float32),
             jax.ShapeDtypeStruct((count, 1), jnp.float32),
         ],
+        input_output_aliases={3: 0, 4: 1, 5: 2},
         compiler_params=pltpu.CompilerParams(vmem_limit_bytes=48 * 1024 * 1024),
         cost_estimate=pl.CostEstimate(
             flops=6 * count * length * width,
             transcendentals=count * length,
-            bytes_accessed=2 * count * width + 4 * length * width + 4 * count * (width + 2),
+            bytes_accessed=2 * count * width + 4 * length * width + 8 * count * (width + 2),
         ),
-    )(query_rows, keys, values)
+    )(query_rows, keys, values, *state)
 
 
 def local(queries, prefix_keys, prefix_values, draft_keys, draft_values, draft_offset):
@@ -125,14 +126,15 @@
 
     block_rows = ways * rows
     query_rows = query_block.reshape(block_rows * group_heads, HD)
-    pieces = [
-        attend_prefix(query_rows, block[0, :local_keys], block[1, :local_keys], inverse_root)
-        for block in blocks
-    ]
-    prefix_peak = functools.reduce(jnp.maximum, [piece[1] for piece in pieces])
-    piece_scales = [jnp.exp(piece[1] - prefix_peak) for piece in pieces]
-    prefix_total = sum(piece[2] * scale for piece, scale in zip(pieces, piece_scales))
-    prefix_sum = sum(piece[0] * scale for piece, scale in zip(pieces, piece_scales))
+    rows_total = block_rows * group_heads
+    state = (
+        jnp.zeros((rows_total, HD), jnp.float32),
+        jnp.full((rows_total, 1), -jnp.inf, jnp.float32),
+        jnp.zeros((rows_total, 1), jnp.float32),
+    )
+    for block in blocks:
+        state = attend_prefix(query_rows, block[0, :local_keys], block[1, :local_keys], inverse_root, state)
+    prefix_sum, prefix_peak, prefix_total = state
     prefix_sum = prefix_sum.reshape(block_rows, group_heads, HD)
     prefix_peak = prefix_peak.reshape(block_rows, group_heads)
     prefix_total = prefix_total.reshape(block_rows, group_heads)

time: 136 us -> 140 us (1.029)
  the two profiles are of different devices: /device:TPU:6 before, /device:TPU:1 now
where the time goes in v12:
time: 140 us
  blocking collectives  55 us (39%)
  waiting for transfers between devices  28.6 us (20%)
  starting transfers between devices  18.6 us (13%)
  Pallas kernels  16.7 us (12%)
  local copies, waits for them, and re-layouts  15.5 us (11%)
  other arithmetic  3.79 us (3%)
    all_to_all x1, blocking collectives, local(): parts = lax.all_to_all(packed, ('grp', 'w'), 0, 0, tiled=True)  35.4 us
    all_to_all x1, waiting for transfers between devices, local(): got = lax.all_to_all(send, 'w', 0, 0, tiled=True)  23.2 us
    all_to_all x1, blocking collectives, local(): attended = lax.all_to_all(attended, 'grp', 0, 0, tiled=True)  19.7 us
    pallas_call x4, Pallas kernels, attend_prefix(): pl.pallas_call(functools.partial(attend_kernel, inverse_root), grid=(coun...  16.7 us
    all_to_all x1, starting transfers between devices, local(): got = lax.all_to_all(send, 'w', 0, 0, tiled=True)  10.9 us
    unnamed x21, local copies, waits for them, and re-layouts  8.06 us
    ppermute x3, starting transfers between devices, local(): lax.ppermute(both_here, 'zq', [(i, (i + shift) % quarters) for i in range...  7.72 us
    ppermute x3, waiting for transfers between devices, local(): lax.ppermute(both_here, 'zq', [(i, (i + shift) % quarters) for i in range...  5.42 us
  transfers between devices with their start and end apart: 4, of which 2 were waited for; matrix products, arithmetic and copies ran while one was open for 2% of the time, Pallas kernels for 9%

profile of v12, /device:TPU:1, one launch (start us, length us, event | category | flops | bytes accessed | tf_op | source)
XLA Modules:
  0.0 139.5 jit_solution(10885336462433403341)
XLA Ops:
  0.0 0.7 reduce.1
  0.7 0.7 reduce.2
  1.4 1.1 copy.104
  2.5 1.0 copy.105
  3.5 1.0 copy.106
  4.6 0.5 broadcast.198
  5.1 1.2 reduce.10
  6.4 0.0 copy-start.3
  6.4 1.1 reshape.269
  7.5 10.9 %all-to-all-start = ((bf16[8,2,24704]{2,1,0:T(2,128)(2,1)}), bf16[8,2,24704]{2,1,0:T(2,128)(2,1)S(1)}, u32[]{:S(2)}, u32[]{:S(2)}) async-start(bf16[8,2,24704]{2,1,0:T(2,128)(2,1)} %reshape.269), calls=%async_computation | async-start | bytes 1581056 | tf_op jit(solution)/shard_map/all_to_all | solution.py:96
  18.4 0.1 add_add_fusion
  18.4 0.1 add.105
  18.5 0.0 copy-done.3
  18.5 0.1 reshape.244
  18.7 0.1 reshape.245
  18.7 0.1 compare_and_fusion
  18.8 23.2 %all-to-all-done = bf16[8,2,24704]{2,1,0:T(2,128)(2,1)S(1)} async-done(((bf16[8,2,24704]{2,1,0:T(2,128)(2,1)}), bf16[8,2,24704]{2,1,0:T(2,128)(2,1)S(1)}, u32[]{:S(2)}, u32[]{:S(2)}) %all-to-all-start) | async-done | bytes 790560 | tf_op jit(solution)/shard_map/all_to_all | solution.py:96
  42.0 2.5 %reshape.270 = bf16[8,1,49408]{2,1,0:T(2,128)(2,1)S(1)} reshape(bf16[8,2,24704]{2,1,0:T(2,128)(2,1)S(1)} %all-to-all-done) | data formatting | bytes 1581056
  44.5 0.1 copy.124
  44.6 0.1 fusion.32
  44.7 0.1 reshape.240
  44.8 0.1 reshape.241
  45.0 0.1 pad_maximum_fusion
  45.1 3.5 %collective-permute-start.2 = (bf16[2,1032,128]{2,1,0:T(8,128)(2,1)S(1)}, bf16[2,1032,128]{2,1,0:T(8,128)(2,1)}, u32[]{:S(2)}, u32[]{:S(2)}) collective-permute-start(bf16[2,1032,128]{2,1,0:T(8,128)(2,1)S(1)} %pad_maximum_fusion), channel_id=1, source_target_pairs={{0,1},{1,2},{2,3},{3,0},{4,5},{5,6},{6,7},{7,4},{8,9},{9,10},{10,1... | collective-permute-start | bytes 1585160 | tf_op jit(solution)/shard_map/ppermute | solution.py:120
  48.6 0.1 reshape_reshape.3.query_ref
  48.7 0.8 reshape.246
  49.5 2.2 %collective-permute-start.1 = (bf16[2,1032,128]{2,1,0:T(8,128)(2,1)S(1)}, bf16[2,1032,128]{2,1,0:T(8,128)(2,1)S(1)}, u32[]{:S(2)}, u32[]{:S(2)}) collective-permute-start(bf16[2,1032,128]{2,1,0:T(8,128)(2,1)S(1)} %pad_maximum_fusion), channel_id=1, source_target_pairs={{0,2},{1,3},{2,0},{3,1},{4,6},{5,7},{6,4},{7,5},{8,10},{9,11},{10,... | collective-permute-start | bytes 1585160 | tf_op jit(solution)/shard_map/ppermute | solution.py:120
  51.7 2.1 %collective-permute-start = (bf16[2,1032,128]{2,1,0:T(8,128)(2,1)S(1)}, bf16[2,1032,128]{2,1,0:T(8,128)(2,1)S(1)}, u32[]{:S(2)}, u32[]{:S(2)}) collective-permute-start(bf16[2,1032,128]{2,1,0:T(8,128)(2,1)S(1)} %pad_maximum_fusion), channel_id=1, source_target_pairs={{0,3},{1,0},{2,1},{3,2},{4,7},{5,4},{6,5},{7,6},{8,11},{9,8},{10,9... | collective-permute-start | bytes 1585160 | tf_op jit(solution)/shard_map/ppermute | solution.py:120
  53.9 4.2 %shard_map.64 = (f32[1024,128]{1,0:T(8,128)S(1)}, f32[1024,1]{1,0:T(8,128)S(1)}, f32[1024,1]{1,0:T(8,128)S(1)}) custom-call(bf16[1024,128]{1,0:T(8,128)(2,1)S(1)} %reshape_reshape.3.query_ref, bf16[1024,128]{1,0:T(8,128)(2,1)S(1)} %slice_bitcast_fusion.1.key_ref, ...), custom_call_target="tpu_custom_call", output_to_operand_aliasing={{0}: (3, {}), {1}: (4, {}), {2}: (5, {})} | custom-call | flops 805306368 | bytes 1851392 | tf_op jit(solution)/shard_map/pallas_call | solution.py:58
  58.1 0.0 collective-permute-done.2
  58.2 1.1 slice_bitcast_fusion.2
  59.2 4.2 %shard_map.65 = (f32[1024,128]{1,0:T(8,128)S(1)}, f32[1024,1]{1,0:T(8,128)S(1)}, f32[1024,1]{1,0:T(8,128)S(1)}) custom-call(bf16[1024,128]{1,0:T(8,128)(2,1)S(1)} %reshape_reshape.3.query_ref, bf16[1024,128]{1,0:T(8,128)(2,1)S(1)} %get-tuple-element.45.key_ref, ...), custom_call_target="tpu_custom_call", output_to_operand_aliasing={{0}: (3, {}), {1}: (4, {}), {2}: (5, {})} | custom-call | flops 805306368 | bytes 1851392 | tf_op jit(solution)/shard_map/pallas_call | solution.py:58
  63.4 5.4 %collective-permute-done.1 = bf16[2,1032,128]{2,1,0:T(8,128)(2,1)S(1)} collective-permute-done((bf16[2,1032,128]{2,1,0:T(8,128)(2,1)S(1)}, bf16[2,1032,128]{2,1,0:T(8,128)(2,1)S(1)}, u32[]{:S(2)}, u32[]{:S(2)}) %collective-permute-start.1) | collective-permute-done | bytes 528416 | tf_op jit(solution)/shard_map/ppermute | solution.py:120
  68.9 4.2 %shard_map.66 = (f32[1024,128]{1,0:T(8,128)S(1)}, f32[1024,1]{1,0:T(8,128)S(1)}, f32[1024,1]{1,0:T(8,128)S(1)}) custom-call(bf16[1024,128]{1,0:T(8,128)(2,1)S(1)} %reshape_reshape.3.query_ref, bf16[1024,128]{1,0:T(8,128)(2,1)S(1)} %get-tuple-element.47.key_ref, ...), custom_call_target="tpu_custom_call", output_to_operand_aliasing={{0}: (3, {}), {1}: (4, {}), {2}: (5, {})} | custom-call | flops 805306368 | bytes 1851392 | tf_op jit(solution)/shard_map/pallas_call | solution.py:58
  73.1 0.0 copy-done
  73.1 0.0 collective-permute-done
  73.1 0.0 copy-start.1
  73.2 0.0 copy-start.2
  73.2 4.1 %shard_map.67 = (f32[1024,128]{1,0:T(8,128)S(1)}, f32[1024,1]{1,0:T(8,128)S(1)}, f32[1024,1]{1,0:T(8,128)S(1)}) custom-call(bf16[1024,128]{1,0:T(8,128)(2,1)S(1)} %reshape_reshape.3.query_ref, bf16[1024,128]{1,0:T(8,128)(2,1)S(1)} %get-tuple-element.49.key_ref, ...), custom_call_target="tpu_custom_call", output_to_operand_aliasing={{0}: (3, {}), {1}: (4, {}), {2}: (5, {})} | custom-call | flops 805306368 | bytes 1851392 | tf_op jit(solution)/shard_map/pallas_call | solution.py:58
  77.3 0.2 reduce.3
  77.5 0.1 reshape.249
  77.6 0.1 reshape.243
  77.7 0.2 reduce.6
  77.9 0.1 reshape.251
  78.1 0.7 slice_bitcast_fusion.10
  78.8 0.7 slice_bitcast_fusion.9
  79.5 0.7 slice_bitcast_fusion.8
  80.1 0.2 fusion.34
  80.3 0.1 copy.90
  80.5 0.1 copy.92
  80.7 0.3 fusion.7
  81.0 0.4 fusion
  81.3 0.3 copy.128
  81.6 0.1 copy.126
  81.7 0.1 concatenate.23
  81.8 0.6 copy.88
  82.5 35.4 %all_to_all.26 = f32[128,1,1040]{2,1,0:T(1,128)S(1)} all-to-all(f32[128,1,1040]{2,1,0:T(1,128)S(1)} %copy.88), channel_id=1, replica_groups=mesh['grp'=16,'w'=8,'zq'=4] {'grp','w'}, dimensions={0} | all-to-all | bytes 1064960 | tf_op jit(solution)/shard_map/all_to_all | solution.py:171
  117.9 0.1 fusion.8
  118.0 0.1 copy.89
  118.0 0.2 fusion.2
  118.3 0.1 bitcast_divide_fusion
  118.3 0.4 broadcast_in_dim.50
  118.8 19.7 %all_to_all.27 = f32[16,1,8192]{2,1,0:T(1,128)S(1)} all-to-all(f32[16,1,8192]{2,1,0:T(1,128)S(1)} %broadcast_in_dim.50), channel_id=1, replica_groups=mesh['grp'=16,'w'=8,'zq'=4] {'grp'}, dimensions={0} | all-to-all | bytes 1048576 | tf_op jit(solution)/shard_map/all_to_all | solution.py:183
  138.4 1.1 copy.127
  (31 shorter events, 0.6 us)
Async XLA Ops:
  6.4 12.2 %copy-start.3 = (s32[512]{0:T(512)S(1)}, s32[512]{0:T(512)}, u32[]{:S(2)}) copy-start(s32[512]{0:T(512)} %param.11) | copy-start | bytes 6148
  7.5 34.5 %all-to-all-start = ((bf16[8,2,24704]{2,1,0:T(2,128)(2,1)}), bf16[8,2,24704]{2,1,0:T(2,128)(2,1)S(1)}, u32[]{:S(2)}, u32[]{:S(2)}) async-start(bf16[8,2,24704]{2,1,0:T(2,128)(2,1)} %reshape.269), calls=%async_computation | async-start | bytes 1581056 | tf_op jit(solution)/shard_map/all_to_all | solution.py:96
  45.1 13.1 %collective-permute-start.2 = (bf16[2,1032,128]{2,1,0:T(8,128)(2,1)S(1)}, bf16[2,1032,128]{2,1,0:T(8,128)(2,1)}, u32[]{:S(2)}, u32[]{:S(2)}) collective-permute-start(bf16[2,1032,128]{2,1,0:T(8,128)(2,1)S(1)} %pad_maximum_fusion), channel_id=1, source_target_pairs={{0,1},{1,2},{2,3},{3,0},{4,5},{5,6},{6,7},{7,4},{8,9},{9,10},{10,1... | collective-permute-start | bytes 1585160 | tf_op jit(solution)/shard_map/ppermute | solution.py:120
  49.5 19.3 %collective-permute-start.1 = (bf16[2,1032,128]{2,1,0:T(8,128)(2,1)S(1)}, bf16[2,1032,128]{2,1,0:T(8,128)(2,1)S(1)}, u32[]{:S(2)}, u32[]{:S(2)}) collective-permute-start(bf16[2,1032,128]{2,1,0:T(8,128)(2,1)S(1)} %pad_maximum_fusion), channel_id=1, source_target_pairs={{0,2},{1,3},{2,0},{3,1},{4,6},{5,7},{6,4},{7,5},{8,10},{9,11},{10,... | collective-permute-start | bytes 1585160 | tf_op jit(solution)/shard_map/ppermute | solution.py:120
  51.7 21.4 %collective-permute-start = (bf16[2,1032,128]{2,1,0:T(8,128)(2,1)S(1)}, bf16[2,1032,128]{2,1,0:T(8,128)(2,1)S(1)}, u32[]{:S(2)}, u32[]{:S(2)}) collective-permute-start(bf16[2,1032,128]{2,1,0:T(8,128)(2,1)S(1)} %pad_maximum_fusion), channel_id=1, source_target_pairs={{0,3},{1,0},{2,1},{3,2},{4,7},{5,4},{6,5},{7,6},{8,11},{9,8},{10,9... | collective-permute-start | bytes 1585160 | tf_op jit(solution)/shard_map/ppermute | solution.py:120
  68.8 4.2 %copy-start = (bf16[2,1032,128]{2,1,0:T(8,128)(2,1)}, bf16[2,1032,128]{2,1,0:T(8,128)(2,1)S(1)}, u32[]{:S(2)}) copy-start(bf16[2,1032,128]{2,1,0:T(8,128)(2,1)S(1)} %collective-permute-done.1) | copy-start | bytes 1585156
  73.1 4.2 %copy-start.1 = (bf16[2,1032,128]{2,1,0:T(8,128)(2,1)}, bf16[2,1032,128]{2,1,0:T(8,128)(2,1)S(1)}, u32[]{:S(2)}) copy-start(bf16[2,1032,128]{2,1,0:T(8,128)(2,1)S(1)} %collective-permute-done) | copy-start | bytes 1585156
  73.2 7.0 %copy-start.2 = (bf16[128,8,128]{2,1,0:T(8,128)(2,1)S(1)}, bf16[128,8,128]{2,1,0:T(8,128)(2,1)}, u32[]{:S(2)}) copy-start(bf16[128,8,128]{2,1,0:T(8,128)(2,1)} %reshape.246) | copy-start | bytes 786436

commit v13 on v10

--- a/solution.py
+++ b/solution.py
@@ -46,7 +46,7 @@
 def attend_prefix(query_rows, keys, values, inverse_root):
     count, width = query_rows.shape
     length = keys.shape[0]
-    tile = 256
+    tile = 512
     return pl.pallas_call(
         functools.partial(attend_kernel, inverse_root),
         grid=(count // tile,),

time: 136 us -> 137 us (level)
  Pallas kernels: 14 us -> 15.9 us
    pallas_call x4, Pallas kernels: 14 us -> 15.9 us  [attend_prefix(): pl.pallas_call(functools.partial(attend_kernel, inverse_root), grid=(coun...]
  transfers between devices with their start and end apart: 4 -> 4, of which waited for: 2 -> 2; matrix products, arithmetic and copies ran while one was open for 1% -> 1% of each run, Pallas kernels for 8% -> 9%
where the time goes in v13:
time: 137 us; the launch traced here: 135 us
  blocking collectives  45.6 us (33%)
  waiting for transfers between devices  32.8 us (24%)
  starting transfers between devices  18.8 us (14%)
  Pallas kernels  15.9 us (12%)
  local copies, waits for them, and re-layouts  15.2 us (11%)
  other arithmetic  5.19 us (4%)
    all_to_all x1, blocking collectives, local(): parts = lax.all_to_all(packed, ('grp', 'w'), 0, 0, tiled=True)  29.9 us
    all_to_all x1, waiting for transfers between devices, local(): got = lax.all_to_all(send, 'w', 0, 0, tiled=True)  22.7 us
    pallas_call x4, Pallas kernels, attend_prefix(): pl.pallas_call(functools.partial(attend_kernel, inverse_root), grid=(coun...  15.9 us
    all_to_all x1, blocking collectives, local(): attended = lax.all_to_all(attended, 'grp', 0, 0, tiled=True)  15.7 us
    all_to_all x1, starting transfers between devices, local(): got = lax.all_to_all(send, 'w', 0, 0, tiled=True)  10.3 us
    ppermute x3, waiting for transfers between devices, local(): lax.ppermute(both_here, 'zq', [(i, (i + shift) % quarters) for i in range...  10 us
    unnamed x21, local copies, waits for them, and re-layouts  9.56 us
    ppermute x3, starting transfers between devices, local(): lax.ppermute(both_here, 'zq', [(i, (i + shift) % quarters) for i in range...  8.47 us
  transfers between devices with their start and end apart: 4, of which 2 were waited for; matrix products, arithmetic and copies ran while one was open for 1% of the time, Pallas kernels for 9%

profile of v13, /device:TPU:6, one launch (start us, length us, event | category | flops | bytes accessed | tf_op | source)
XLA Modules:
  0.0 134.6 jit_solution(11554173905063340607)
XLA Ops:
  0.0 0.7 reduce.1
  0.7 0.7 reduce.2
  1.4 1.1 copy.71
  2.5 1.0 copy.72
  3.5 1.0 copy.73
  4.6 0.5 broadcast.202
  5.1 1.2 reduce.20
  6.4 0.0 copy-start.3
  6.4 1.1 reshape.273
  7.5 10.3 %all-to-all-start = ((bf16[8,2,24704]{2,1,0:T(2,128)(2,1)}), bf16[8,2,24704]{2,1,0:T(2,128)(2,1)S(1)}, u32[]{:S(2)}, u32[]{:S(2)}) async-start(bf16[8,2,24704]{2,1,0:T(2,128)(2,1)} %reshape.273), calls=%async_computation | async-start | bytes 1581056 | tf_op jit(solution)/shard_map/all_to_all | solution.py:95
  17.8 0.1 add_add_fusion
  17.9 0.1 add.126
  18.0 0.0 copy-done.3
  18.0 0.1 reshape.244
  18.1 0.1 reshape.245
  18.2 0.1 compare_and_fusion
  18.3 22.7 %all-to-all-done = bf16[8,2,24704]{2,1,0:T(2,128)(2,1)S(1)} async-done(((bf16[8,2,24704]{2,1,0:T(2,128)(2,1)}), bf16[8,2,24704]{2,1,0:T(2,128)(2,1)S(1)}, u32[]{:S(2)}, u32[]{:S(2)}) %all-to-all-start) | async-done | bytes 790560 | tf_op jit(solution)/shard_map/all_to_all | solution.py:95
  41.0 2.5 %reshape.274 = bf16[8,1,49408]{2,1,0:T(2,128)(2,1)S(1)} reshape(bf16[8,2,24704]{2,1,0:T(2,128)(2,1)S(1)} %all-to-all-done) | data formatting | bytes 1581056
  43.5 0.1 copy.91
  43.6 0.1 fusion.36
  43.6 0.1 reshape.240
  43.8 0.1 reshape.241
  44.0 0.1 pad_maximum_fusion
  44.0 1.9 %collective-permute-start = (bf16[2,1032,128]{2,1,0:T(8,128)(2,1)S(1)}, bf16[2,1032,128]{2,1,0:T(8,128)(2,1)S(1)}, u32[]{:S(2)}, u32[]{:S(2)}) collective-permute-start(bf16[2,1032,128]{2,1,0:T(8,128)(2,1)S(1)} %pad_maximum_fusion), channel_id=1, source_target_pairs={{0,1},{1,2},{2,3},{3,0},{4,5},{5,6},{6,7},{7,4},{8,9},{9,10},{10,1... | collective-permute-start | bytes 1585160 | tf_op jit(solution)/shard_map/ppermute | solution.py:119
  46.0 0.1 reshape_reshape.3.query_ref
  46.1 0.8 reshape.246
  47.0 3.6 %collective-permute-start.2 = (bf16[2,1032,128]{2,1,0:T(8,128)(2,1)S(1)}, bf16[2,1032,128]{2,1,0:T(8,128)(2,1)S(1)}, u32[]{:S(2)}, u32[]{:S(2)}) collective-permute-start(bf16[2,1032,128]{2,1,0:T(8,128)(2,1)S(1)} %pad_maximum_fusion), channel_id=1, source_target_pairs={{0,3},{1,0},{2,1},{3,2},{4,7},{5,4},{6,5},{7,6},{8,11},{9,8},{10,9... | collective-permute-start | bytes 1585160 | tf_op jit(solution)/shard_map/ppermute | solution.py:119
  50.6 2.9 %collective-permute-start.1 = (bf16[2,1032,128]{2,1,0:T(8,128)(2,1)S(1)}, bf16[2,1032,128]{2,1,0:T(8,128)(2,1)S(1)}, u32[]{:S(2)}, u32[]{:S(2)}) collective-permute-start(bf16[2,1032,128]{2,1,0:T(8,128)(2,1)S(1)} %pad_maximum_fusion), channel_id=1, source_target_pairs={{0,2},{1,3},{2,0},{3,1},{4,6},{5,7},{6,4},{7,5},{8,10},{9,11},{10,... | collective-permute-start | bytes 1585160 | tf_op jit(solution)/shard_map/ppermute | solution.py:119
  53.5 4.0 %shard_map.64 = (f32[1024,128]{1,0:T(8,128)S(1)}, f32[1024,1]{1,0:T(8,128)S(1)}, f32[1024,1]{1,0:T(8,128)S(1)}) custom-call(bf16[1024,128]{1,0:T(8,128)(2,1)S(1)} %reshape_reshape.3.query_ref, bf16[1024,128]{1,0:T(8,128)(2,1)S(1)} %slice_bitcast_fusion.7.key_ref, bf16[1024,128]{1,0:T(8,128)(2,1)S(1)} %slice_bitcast_fusion.6.value_ref), custom_call_target="tpu_custom_call" | custom-call | flops 805306368 | bytes 1318912 | tf_op jit(solution)/shard_map/pallas_call | solution.py:50
  57.5 0.0 collective-permute-done
  57.6 4.0 %shard_map.65 = (f32[1024,128]{1,0:T(8,128)S(1)}, f32[1024,1]{1,0:T(8,128)S(1)}, f32[1024,1]{1,0:T(8,128)S(1)}) custom-call(bf16[1024,128]{1,0:T(8,128)(2,1)S(1)} %reshape_reshape.3.query_ref, bf16[1024,128]{1,0:T(8,128)(2,1)S(1)} %get-tuple-element.51.key_ref, bf16[1024,128]{1,0:T(8,128)(2,1)S(1)} %get-tuple-element.50.value_ref), custom_call_target="tpu_custom_call" | custom-call | flops 805306368 | bytes 1318912 | tf_op jit(solution)/shard_map/pallas_call | solution.py:50
  61.6 10.0 %collective-permute-done.1 = bf16[2,1032,128]{2,1,0:T(8,128)(2,1)S(1)} collective-permute-done((bf16[2,1032,128]{2,1,0:T(8,128)(2,1)S(1)}, bf16[2,1032,128]{2,1,0:T(8,128)(2,1)S(1)}, u32[]{:S(2)}, u32[]{:S(2)}) %collective-permute-start.1) | collective-permute-done | bytes 528416 | tf_op jit(solution)/shard_map/ppermute | solution.py:119
  71.6 0.7 copy-done.1
  72.4 4.0 %shard_map.66 = (f32[1024,128]{1,0:T(8,128)S(1)}, f32[1024,1]{1,0:T(8,128)S(1)}, f32[1024,1]{1,0:T(8,128)S(1)}) custom-call(bf16[1024,128]{1,0:T(8,128)(2,1)S(1)} %reshape_reshape.3.query_ref, bf16[1024,128]{1,0:T(8,128)(2,1)S(1)} %get-tuple-element.53.key_ref, bf16[1024,128]{1,0:T(8,128)(2,1)S(1)} %get-tuple-element.52.value_ref), custom_call_target="tpu_custom_call" | custom-call | flops 805306368 | bytes 1318912 | tf_op jit(solution)/shard_map/pallas_call | solution.py:50
  76.3 0.0 collective-permute-done.2
  76.3 0.0 copy-start
  76.4 0.8 copy-done
  77.1 4.0 %shard_map.67 = (f32[1024,128]{1,0:T(8,128)S(1)}, f32[1024,1]{1,0:T(8,128)S(1)}, f32[1024,1]{1,0:T(8,128)S(1)}) custom-call(bf16[1024,128]{1,0:T(8,128)(2,1)S(1)} %reshape_reshape.3.query_ref, bf16[1024,128]{1,0:T(8,128)(2,1)S(1)} %get-tuple-element.55.key_ref, bf16[1024,128]{1,0:T(8,128)(2,1)S(1)} %get-tuple-element.54.value_ref), custom_call_target="tpu_custom_call" | custom-call | flops 805306368 | bytes 1318912 | tf_op jit(solution)/shard_map/pallas_call | solution.py:50
  81.1 0.0 copy-start.2
  81.1 1.2 add_reduce_fusion
  82.3 0.1 reshape.249
  82.4 0.1 reshape.243
  82.5 0.7 slice_bitcast_fusion.8
  83.2 0.7 slice_bitcast_fusion.9
  83.8 0.2 fusion.38
  84.1 0.1 copy.62
  84.2 0.1 reshape.251
  84.3 0.1 fusion.9
  84.4 0.1 copy.64
  84.6 0.3 fusion.11
  84.8 0.6 add_bitcast_fusion
  85.5 0.4 fusion
  85.8 0.3 copy.95
  86.1 0.1 copy.93
  86.2 0.1 concatenate.23
  86.3 0.6 copy.60
  86.9 29.9 %all_to_all.26 = f32[128,1,1040]{2,1,0:T(1,128)S(1)} all-to-all(f32[128,1,1040]{2,1,0:T(1,128)S(1)} %copy.60), channel_id=1, replica_groups=mesh['grp'=16,'w'=8,'zq'=4] {'grp','w'}, dimensions={0} | all-to-all | bytes 1064960 | tf_op jit(solution)/shard_map/all_to_all | solution.py:169
  116.9 0.1 fusion.12
  117.0 0.1 copy.61
  117.1 0.2 fusion.2
  117.3 0.1 bitcast_divide_fusion
  117.4 0.4 broadcast_in_dim.38
  117.8 15.7 %all_to_all.27 = f32[16,1,8192]{2,1,0:T(1,128)S(1)} all-to-all(f32[16,1,8192]{2,1,0:T(1,128)S(1)} %broadcast_in_dim.38), channel_id=1, replica_groups=mesh['grp'=16,'w'=8,'zq'=4] {'grp'}, dimensions={0} | all-to-all | bytes 1048576 | tf_op jit(solution)/shard_map/all_to_all | solution.py:181
  133.5 1.1 copy.94
  (28 shorter events, 0.5 us)
Async XLA Ops:
  6.4 11.6 %copy-start.3 = (s32[512]{0:T(512)S(1)}, s32[512]{0:T(512)}, u32[]{:S(2)}) copy-start(s32[512]{0:T(512)} %param.11) | copy-start | bytes 6148
  7.5 33.5 %all-to-all-start = ((bf16[8,2,24704]{2,1,0:T(2,128)(2,1)}), bf16[8,2,24704]{2,1,0:T(2,128)(2,1)S(1)}, u32[]{:S(2)}, u32[]{:S(2)}) async-start(bf16[8,2,24704]{2,1,0:T(2,128)(2,1)} %reshape.273), calls=%async_computation | async-start | bytes 1581056 | tf_op jit(solution)/shard_map/all_to_all | solution.py:95
  44.0 13.5 %collective-permute-start = (bf16[2,1032,128]{2,1,0:T(8,128)(2,1)S(1)}, bf16[2,1032,128]{2,1,0:T(8,128)(2,1)S(1)}, u32[]{:S(2)}, u32[]{:S(2)}) collective-permute-start(bf16[2,1032,128]{2,1,0:T(8,128)(2,1)S(1)} %pad_maximum_fusion), channel_id=1, source_target_pairs={{0,1},{1,2},{2,3},{3,0},{4,5},{5,6},{6,7},{7,4},{8,9},{9,10},{10,1... | collective-permute-start | bytes 1585160 | tf_op jit(solution)/shard_map/ppermute | solution.py:119
  47.0 29.4 %collective-permute-start.2 = (bf16[2,1032,128]{2,1,0:T(8,128)(2,1)S(1)}, bf16[2,1032,128]{2,1,0:T(8,128)(2,1)S(1)}, u32[]{:S(2)}, u32[]{:S(2)}) collective-permute-start(bf16[2,1032,128]{2,1,0:T(8,128)(2,1)S(1)} %pad_maximum_fusion), channel_id=1, source_target_pairs={{0,3},{1,0},{2,1},{3,2},{4,7},{5,4},{6,5},{7,6},{8,11},{9,8},{10,9... | collective-permute-start | bytes 1585160 | tf_op jit(solution)/shard_map/ppermute | solution.py:119
  50.6 21.0 %collective-permute-start.1 = (bf16[2,1032,128]{2,1,0:T(8,128)(2,1)S(1)}, bf16[2,1032,128]{2,1,0:T(8,128)(2,1)S(1)}, u32[]{:S(2)}, u32[]{:S(2)}) collective-permute-start(bf16[2,1032,128]{2,1,0:T(8,128)(2,1)S(1)} %pad_maximum_fusion), channel_id=1, source_target_pairs={{0,2},{1,3},{2,0},{3,1},{4,6},{5,7},{6,4},{7,5},{8,10},{9,11},{10,... | collective-permute-start | bytes 1585160 | tf_op jit(solution)/shard_map/ppermute | solution.py:119
  71.6 0.8 copy-start.1
  76.3 0.8 copy-start
  81.1 2.7 %copy-start.2 = (bf16[128,8,128]{2,1,0:T(8,128)(2,1)S(1)}, bf16[128,8,128]{2,1,0:T(8,128)(2,1)}, u32[]{:S(2)}) copy-start(bf16[128,8,128]{2,1,0:T(8,128)(2,1)} %reshape.246) | copy-start | bytes 786436

commit v14 on v10

--- a/solution.py
+++ b/solution.py
@@ -115,13 +115,15 @@
     )
     local_keys = ways * positions
     both_here = jnp.stack([keys_here, values_here])
+    shifts = [0] + [shift for shift in range(1, quarters) if 2 * shift != quarters]
+    shifts += [shift for shift in range(1, quarters) if 2 * shift == quarters]
     blocks = [both_here] + [
         lax.ppermute(both_here, "zq", [(i, (i + shift) % quarters) for i in range(quarters)])
-        for shift in range(1, quarters)
+        for shift in shifts[1:]
     ]
     draft_k = jnp.concatenate([block[0, local_keys:] for block in blocks], axis=0)
     draft_v = jnp.concatenate([block[1, local_keys:] for block in blocks], axis=0)
-    source_quarter = (quarter - lax.iota(jnp.int32, quarters)) % quarters
+    source_quarter = (quarter - jnp.array(shifts, jnp.int32)) % quarters
 
     block_rows = ways * rows
     query_rows = query_block.reshape(block_rows * group_heads, HD)

time: 136 us -> 144 us (1.059)
  blocking collectives: 45.6 us -> 54.9 us
    all_to_all x1, blocking collectives: 29.9 us -> 34.6 us  [local(): parts = lax.all_to_all(packed, ('grp', 'w'), 0, 0, tiled=True)]
    all_to_all x1, blocking collectives: 15.7 us -> 20.3 us  [local(): attended = lax.all_to_all(attended, 'grp', 0, 0, tiled=True)]
    unnamed x21 -> x23, local copies, waits for them, and re-layouts: 9.56 us -> 9.57 us
  transfers between devices with their start and end apart: 4 -> 4, of which waited for: 2 -> 3; matrix products, arithmetic and copies ran while one was open for 1% -> 1% of each run, Pallas kernels for 8% -> 7%
where the time goes in v14:
time: 144 us; the launch traced here: 141 us
  blocking collectives  54.9 us (38%)
  waiting for transfers between devices  32.5 us (23%)
  starting transfers between devices  18.3 us (13%)
  local copies, waits for them, and re-layouts  15.2 us (11%)
  Pallas kernels  14 us (10%)
  other arithmetic  5.19 us (4%)
    all_to_all x1, blocking collectives, local(): parts = lax.all_to_all(packed, ('grp', 'w'), 0, 0, tiled=True)  34.6 us
    all_to_all x1, waiting for transfers between devices, local(): got = lax.all_to_all(send, 'w', 0, 0, tiled=True)  22.7 us
    all_to_all x1, blocking collectives, local(): attended = lax.all_to_all(attended, 'grp', 0, 0, tiled=True)  20.3 us
    pallas_call x4, Pallas kernels, attend_prefix(): pl.pallas_call(functools.partial(attend_kernel, inverse_root), grid=(coun...  14 us
    all_to_all x1, starting transfers between devices, local(): got = lax.all_to_all(send, 'w', 0, 0, tiled=True)  10.3 us
    ppermute x3, waiting for transfers between devices, local(): lax.ppermute(both_here, 'zq', [(i, (i + shift) % quarters) for i in range...  9.79 us
    unnamed x23, local copies, waits for them, and re-layouts  9.57 us
    ppermute x3, starting transfers between devices, local(): lax.ppermute(both_here, 'zq', [(i, (i + shift) % quarters) for i in range...  8.01 us
  transfers between devices with their start and end apart: 4, of which 3 were waited for; matrix products, arithmetic and copies ran while one was open for 1% of the time, Pallas kernels for 7%

profile of v14, /device:TPU:6, one launch (start us, length us, event | category | flops | bytes accessed | tf_op | source)
XLA Modules:
  0.0 141.3 jit_solution(15046292053777324662)
XLA Ops:
  0.0 0.7 reduce.1
  0.7 0.7 reduce.2
  1.4 1.1 copy.72
  2.5 1.0 copy.73
  3.5 1.0 copy.74
  4.6 0.5 broadcast.180
  5.1 1.2 reduce.20
  6.4 0.0 copy-start.4
  6.4 0.0 copy-start.3
  6.4 1.1 reshape.259
  7.5 10.3 %all-to-all-start = ((bf16[8,2,24704]{2,1,0:T(2,128)(2,1)}), bf16[8,2,24704]{2,1,0:T(2,128)(2,1)S(1)}, u32[]{:S(2)}, u32[]{:S(2)}) async-start(bf16[8,2,24704]{2,1,0:T(2,128)(2,1)} %reshape.259), calls=%async_computation | async-start | bytes 1581056 | tf_op jit(solution)/shard_map/all_to_all | solution.py:95
  17.8 0.1 add_add_fusion
  17.9 0.1 add.122
  18.0 0.1 reshape.230
  18.1 0.1 reshape.231
  18.2 0.1 compare_and_fusion
  18.3 22.7 %all-to-all-done = bf16[8,2,24704]{2,1,0:T(2,128)(2,1)S(1)} async-done(((bf16[8,2,24704]{2,1,0:T(2,128)(2,1)}), bf16[8,2,24704]{2,1,0:T(2,128)(2,1)S(1)}, u32[]{:S(2)}, u32[]{:S(2)}) %all-to-all-start) | async-done | bytes 790560 | tf_op jit(solution)/shard_map/all_to_all | solution.py:95
  41.0 2.5 %reshape.260 = bf16[8,1,49408]{2,1,0:T(2,128)(2,1)S(1)} reshape(bf16[8,2,24704]{2,1,0:T(2,128)(2,1)S(1)} %all-to-all-done) | data formatting | bytes 1581056
  43.5 0.1 copy.92
  43.6 0.1 fusion.36
  43.7 0.1 reshape.226
  43.8 0.1 reshape.227
  44.0 0.1 pad_maximum_fusion
  44.1 1.9 %collective-permute-start = (bf16[2,1032,128]{2,1,0:T(8,128)(2,1)S(1)}, bf16[2,1032,128]{2,1,0:T(8,128)(2,1)S(1)}, u32[]{:S(2)}, u32[]{:S(2)}) collective-permute-start(bf16[2,1032,128]{2,1,0:T(8,128)(2,1)S(1)} %pad_maximum_fusion), channel_id=1, source_target_pairs={{0,1},{1,2},{2,3},{3,0},{4,5},{5,6},{6,7},{7,4},{8,9},{9,10},{10,1... | collective-permute-start | bytes 1585160 | tf_op jit(solution)/shard_map/ppermute | solution.py:121
  46.0 0.1 reshape_reshape.3.query_ref
  46.1 0.8 reshape.232
  47.0 2.7 %collective-permute-start.2 = (bf16[2,1032,128]{2,1,0:T(8,128)(2,1)S(1)}, bf16[2,1032,128]{2,1,0:T(8,128)(2,1)S(1)}, u32[]{:S(2)}, u32[]{:S(2)}) collective-permute-start(bf16[2,1032,128]{2,1,0:T(8,128)(2,1)S(1)} %pad_maximum_fusion), channel_id=1, source_target_pairs={{0,2},{1,3},{2,0},{3,1},{4,6},{5,7},{6,4},{7,5},{8,10},{9,11},{10,... | collective-permute-start | bytes 1585160 | tf_op jit(solution)/shard_map/ppermute | solution.py:121
  49.7 3.4 %collective-permute-start.1 = (bf16[2,1032,128]{2,1,0:T(8,128)(2,1)S(1)}, bf16[2,1032,128]{2,1,0:T(8,128)(2,1)S(1)}, u32[]{:S(2)}, u32[]{:S(2)}) collective-permute-start(bf16[2,1032,128]{2,1,0:T(8,128)(2,1)S(1)} %pad_maximum_fusion), channel_id=1, source_target_pairs={{0,3},{1,0},{2,1},{3,2},{4,7},{5,4},{6,5},{7,6},{8,11},{9,8},{10,9... | collective-permute-start | bytes 1585160 | tf_op jit(solution)/shard_map/ppermute | solution.py:121
  53.1 3.5 %shard_map.73 = (f32[1024,128]{1,0:T(8,128)S(1)}, f32[1024,1]{1,0:T(8,128)S(1)}, f32[1024,1]{1,0:T(8,128)S(1)}) custom-call(bf16[1024,128]{1,0:T(8,128)(2,1)S(1)} %reshape_reshape.3.query_ref, bf16[1024,128]{1,0:T(8,128)(2,1)S(1)} %slice_bitcast_fusion.7.key_ref, bf16[1024,128]{1,0:T(8,128)(2,1)S(1)} %slice_bitcast_fusion.6.value_ref), custom_call_target="tpu_custom_call" | custom-call | flops 805306368 | bytes 1318912 | tf_op jit(solution)/shard_map/pallas_call | solution.py:50
  56.6 0.1 collective-permute-done
  56.8 3.5 %shard_map.74 = (f32[1024,128]{1,0:T(8,128)S(1)}, f32[1024,1]{1,0:T(8,128)S(1)}, f32[1024,1]{1,0:T(8,128)S(1)}) custom-call(bf16[1024,128]{1,0:T(8,128)(2,1)S(1)} %reshape_reshape.3.query_ref, bf16[1024,128]{1,0:T(8,128)(2,1)S(1)} %get-tuple-element.51.key_ref, bf16[1024,128]{1,0:T(8,128)(2,1)S(1)} %get-tuple-element.50.value_ref), custom_call_target="tpu_custom_call" | custom-call | flops 805306368 | bytes 1318912 | tf_op jit(solution)/shard_map/pallas_call | solution.py:50
  60.3 9.7 %collective-permute-done.1 = bf16[2,1032,128]{2,1,0:T(8,128)(2,1)S(1)} collective-permute-done((bf16[2,1032,128]{2,1,0:T(8,128)(2,1)S(1)}, bf16[2,1032,128]{2,1,0:T(8,128)(2,1)S(1)}, u32[]{:S(2)}, u32[]{:S(2)}) %collective-permute-start.1) | collective-permute-done | bytes 528416 | tf_op jit(solution)/shard_map/ppermute | solution.py:121
  70.0 0.7 copy-done.1
  70.7 3.5 %shard_map.75 = (f32[1024,128]{1,0:T(8,128)S(1)}, f32[1024,1]{1,0:T(8,128)S(1)}, f32[1024,1]{1,0:T(8,128)S(1)}) custom-call(bf16[1024,128]{1,0:T(8,128)(2,1)S(1)} %reshape_reshape.3.query_ref, bf16[1024,128]{1,0:T(8,128)(2,1)S(1)} %get-tuple-element.53.key_ref, bf16[1024,128]{1,0:T(8,128)(2,1)S(1)} %get-tuple-element.52.value_ref), custom_call_target="tpu_custom_call" | custom-call | flops 805306368 | bytes 1318912 | tf_op jit(solution)/shard_map/pallas_call | solution.py:50
  74.2 0.0 collective-permute-done.2
  74.2 0.0 copy-start
  74.3 0.8 copy-done
  75.0 3.5 %shard_map.76 = (f32[1024,128]{1,0:T(8,128)S(1)}, f32[1024,1]{1,0:T(8,128)S(1)}, f32[1024,1]{1,0:T(8,128)S(1)}) custom-call(bf16[1024,128]{1,0:T(8,128)(2,1)S(1)} %reshape_reshape.3.query_ref, bf16[1024,128]{1,0:T(8,128)(2,1)S(1)} %get-tuple-element.55.key_ref, bf16[1024,128]{1,0:T(8,128)(2,1)S(1)} %get-tuple-element.54.value_ref), custom_call_target="tpu_custom_call" | custom-call | flops 805306368 | bytes 1318912 | tf_op jit(solution)/shard_map/pallas_call | solution.py:50
  78.5 0.0 copy-start.2
  78.5 1.2 add_reduce_fusion
  79.7 0.1 reshape.235
  79.8 0.1 reshape.229
  79.9 0.7 slice_bitcast_fusion.8
  80.6 0.7 slice_bitcast_fusion.9
  81.3 0.2 fusion.38
  81.5 0.1 copy.63
  81.6 0.1 reshape.237
  81.7 0.1 fusion.9
  81.8 0.1 copy.65
  82.0 0.3 fusion.11
  82.3 0.6 add_bitcast_fusion
  82.9 0.4 fusion
  83.2 0.3 copy.96
  83.5 0.1 copy.94
  83.6 0.1 concatenate.23
  83.7 0.6 copy.61
  84.4 34.6 %all_to_all.26 = f32[128,1,1040]{2,1,0:T(1,128)S(1)} all-to-all(f32[128,1,1040]{2,1,0:T(1,128)S(1)} %copy.61), channel_id=1, replica_groups=mesh['grp'=16,'w'=8,'zq'=4] {'grp','w'}, dimensions={0} | all-to-all | bytes 1064960 | tf_op jit(solution)/shard_map/all_to_all | solution.py:171
  119.0 0.1 fusion.12
  119.1 0.1 copy.62
  119.2 0.2 fusion.2
  119.4 0.1 bitcast_divide_fusion
  119.5 0.4 broadcast_in_dim.38
  119.9 20.3 %all_to_all.27 = f32[16,1,8192]{2,1,0:T(1,128)S(1)} all-to-all(f32[16,1,8192]{2,1,0:T(1,128)S(1)} %broadcast_in_dim.38), channel_id=1, replica_groups=mesh['grp'=16,'w'=8,'zq'=4] {'grp'}, dimensions={0} | all-to-all | bytes 1048576 | tf_op jit(solution)/shard_map/all_to_all | solution.py:183
  140.2 1.1 copy.95
  (30 shorter events, 0.5 us)
Async XLA Ops:
  6.4 11.4 %copy-start.4 = (s32[4]{0:T(128)S(1)}, s32[4]{0:T(128)}, u32[]{:S(2)}) copy-start(s32[4]{0:T(128)} %constant.76) | copy-start | bytes 52
  6.4 11.6 %copy-start.3 = (s32[512]{0:T(512)S(1)}, s32[512]{0:T(512)}, u32[]{:S(2)}) copy-start(s32[512]{0:T(512)} %param.12) | copy-start | bytes 6148
  7.5 33.5 %all-to-all-start = ((bf16[8,2,24704]{2,1,0:T(2,128)(2,1)}), bf16[8,2,24704]{2,1,0:T(2,128)(2,1)S(1)}, u32[]{:S(2)}, u32[]{:S(2)}) async-start(bf16[8,2,24704]{2,1,0:T(2,128)(2,1)} %reshape.259), calls=%async_computation | async-start | bytes 1581056 | tf_op jit(solution)/shard_map/all_to_all | solution.py:95
  44.1 12.7 %collective-permute-start = (bf16[2,1032,128]{2,1,0:T(8,128)(2,1)S(1)}, bf16[2,1032,128]{2,1,0:T(8,128)(2,1)S(1)}, u32[]{:S(2)}, u32[]{:S(2)}) collective-permute-start(bf16[2,1032,128]{2,1,0:T(8,128)(2,1)S(1)} %pad_maximum_fusion), channel_id=1, source_target_pairs={{0,1},{1,2},{2,3},{3,0},{4,5},{5,6},{6,7},{7,4},{8,9},{9,10},{10,1... | collective-permute-start | bytes 1585160 | tf_op jit(solution)/shard_map/ppermute | solution.py:121
  47.0 27.2 %collective-permute-start.2 = (bf16[2,1032,128]{2,1,0:T(8,128)(2,1)S(1)}, bf16[2,1032,128]{2,1,0:T(8,128)(2,1)S(1)}, u32[]{:S(2)}, u32[]{:S(2)}) collective-permute-start(bf16[2,1032,128]{2,1,0:T(8,128)(2,1)S(1)} %pad_maximum_fusion), channel_id=1, source_target_pairs={{0,2},{1,3},{2,0},{3,1},{4,6},{5,7},{6,4},{7,5},{8,10},{9,11},{10,... | collective-permute-start | bytes 1585160 | tf_op jit(solution)/shard_map/ppermute | solution.py:121
  49.7 20.2 %collective-permute-start.1 = (bf16[2,1032,128]{2,1,0:T(8,128)(2,1)S(1)}, bf16[2,1032,128]{2,1,0:T(8,128)(2,1)S(1)}, u32[]{:S(2)}, u32[]{:S(2)}) collective-permute-start(bf16[2,1032,128]{2,1,0:T(8,128)(2,1)S(1)} %pad_maximum_fusion), channel_id=1, source_target_pairs={{0,3},{1,0},{2,1},{3,2},{4,7},{5,4},{6,5},{7,6},{8,11},{9,8},{10,9... | collective-permute-start | bytes 1585160 | tf_op jit(solution)/shard_map/ppermute | solution.py:121
  69.9 0.8 copy-start.1
  74.2 0.8 copy-start
  78.5 2.7 %copy-start.2 = (bf16[128,8,128]{2,1,0:T(8,128)(2,1)S(1)}, bf16[128,8,128]{2,1,0:T(8,128)(2,1)}, u32[]{:S(2)}) copy-start(bf16[128,8,128]{2,1,0:T(8,128)(2,1)} %reshape.232) | copy-start | bytes 786436

commit v15 on v13

--- a/solution.py
+++ b/solution.py
@@ -46,7 +46,7 @@
 def attend_prefix(query_rows, keys, values, inverse_root):
     count, width = query_rows.shape
     length = keys.shape[0]
-    tile = 512
+    tile = 128
     return pl.pallas_call(
         functools.partial(attend_kernel, inverse_root),
         grid=(count // tile,),

time: 137 us -> 139 us (1.015)
  Pallas kernels: 15.9 us -> 19.9 us
  waiting for transfers between devices: 32.8 us -> 30.9 us
    pallas_call x4, Pallas kernels: 15.9 us -> 19.9 us  [attend_prefix(): pl.pallas_call(functools.partial(attend_kernel, inverse_root), grid=(coun...]
    ppermute x3, waiting for transfers between devices: 10 us -> 8.17 us  [local(): lax.ppermute(both_here, 'zq', [(i, (i + shift) % quarters) for i in range...]
  transfers between devices with their start and end apart: 4 -> 4, of which waited for: 2 -> 2; matrix products, arithmetic and copies ran while one was open for 1% -> 1% of each run, Pallas kernels for 9% -> 11%
where the time goes in v15:
time: 139 us; the launch traced here: 137 us
  blocking collectives  45.6 us (33%)
  waiting for transfers between devices  30.9 us (22%)
  Pallas kernels  19.9 us (14%)
  starting transfers between devices  18.6 us (13%)
  local copies, waits for them, and re-layouts  15.2 us (11%)
  other arithmetic  5.19 us (4%)
    all_to_all x1, blocking collectives, local(): parts = lax.all_to_all(packed, ('grp', 'w'), 0, 0, tiled=True)  29.9 us
    all_to_all x1, waiting for transfers between devices, local(): got = lax.all_to_all(send, 'w', 0, 0, tiled=True)  22.7 us
    pallas_call x4, Pallas kernels, attend_prefix(): pl.pallas_call(functools.partial(attend_kernel, inverse_root), grid=(coun...  19.9 us
    all_to_all x1, blocking collectives, local(): attended = lax.all_to_all(attended, 'grp', 0, 0, tiled=True)  15.7 us
    all_to_all x1, starting transfers between devices, local(): got = lax.all_to_all(send, 'w', 0, 0, tiled=True)  10.3 us
    unnamed x21, local copies, waits for them, and re-layouts  9.56 us
    ppermute x3, starting transfers between devices, local(): lax.ppermute(both_here, 'zq', [(i, (i + shift) % quarters) for i in range...  8.29 us
    ppermute x3, waiting for transfers between devices, local(): lax.ppermute(both_here, 'zq', [(i, (i + shift) % quarters) for i in range...  8.17 us
  transfers between devices with their start and end apart: 4, of which 2 were waited for; matrix products, arithmetic and copies ran while one was open for 1% of the time, Pallas kernels for 11%

profile of v15, /device:TPU:6, one launch (start us, length us, event | category | flops | bytes accessed | tf_op | source)
XLA Modules:
  0.0 136.7 jit_solution(14418498724534354983)
XLA Ops:
  0.0 0.7 reduce.1
  0.7 0.7 reduce.2
  1.4 1.1 copy.71
  2.5 1.0 copy.72
  3.5 1.0 copy.73
  4.6 0.5 broadcast.202
  5.1 1.2 reduce.20
  6.4 0.0 copy-start.3
  6.4 1.1 reshape.273
  7.5 10.3 %all-to-all-start = ((bf16[8,2,24704]{2,1,0:T(2,128)(2,1)}), bf16[8,2,24704]{2,1,0:T(2,128)(2,1)S(1)}, u32[]{:S(2)}, u32[]{:S(2)}) async-start(bf16[8,2,24704]{2,1,0:T(2,128)(2,1)} %reshape.273), calls=%async_computation | async-start | bytes 1581056 | tf_op jit(solution)/shard_map/all_to_all | solution.py:95
  17.8 0.1 add_add_fusion
  17.9 0.1 add.126
  18.0 0.0 copy-done.3
  18.0 0.1 reshape.244
  18.1 0.1 reshape.245
  18.2 0.1 compare_and_fusion
  18.3 22.7 %all-to-all-done = bf16[8,2,24704]{2,1,0:T(2,128)(2,1)S(1)} async-done(((bf16[8,2,24704]{2,1,0:T(2,128)(2,1)}), bf16[8,2,24704]{2,1,0:T(2,128)(2,1)S(1)}, u32[]{:S(2)}, u32[]{:S(2)}) %all-to-all-start) | async-done | bytes 790560 | tf_op jit(solution)/shard_map/all_to_all | solution.py:95
  41.0 2.5 %reshape.274 = bf16[8,1,49408]{2,1,0:T(2,128)(2,1)S(1)} reshape(bf16[8,2,24704]{2,1,0:T(2,128)(2,1)S(1)} %all-to-all-done) | data formatting | bytes 1581056
  43.5 0.1 copy.91
  43.6 0.1 fusion.36
  43.6 0.1 reshape.240
  43.8 0.1 reshape.241
  44.0 0.1 pad_maximum_fusion
  44.0 1.9 %collective-permute-start = (bf16[2,1032,128]{2,1,0:T(8,128)(2,1)S(1)}, bf16[2,1032,128]{2,1,0:T(8,128)(2,1)S(1)}, u32[]{:S(2)}, u32[]{:S(2)}) collective-permute-start(bf16[2,1032,128]{2,1,0:T(8,128)(2,1)S(1)} %pad_maximum_fusion), channel_id=1, source_target_pairs={{0,1},{1,2},{2,3},{3,0},{4,5},{5,6},{6,7},{7,4},{8,9},{9,10},{10,1... | collective-permute-start | bytes 1585160 | tf_op jit(solution)/shard_map/ppermute | solution.py:119
  46.0 0.1 reshape_reshape.3.query_ref
  46.1 0.8 reshape.246
  47.0 3.6 %collective-permute-start.2 = (bf16[2,1032,128]{2,1,0:T(8,128)(2,1)S(1)}, bf16[2,1032,128]{2,1,0:T(8,128)(2,1)S(1)}, u32[]{:S(2)}, u32[]{:S(2)}) collective-permute-start(bf16[2,1032,128]{2,1,0:T(8,128)(2,1)S(1)} %pad_maximum_fusion), channel_id=1, source_target_pairs={{0,3},{1,0},{2,1},{3,2},{4,7},{5,4},{6,5},{7,6},{8,11},{9,8},{10,9... | collective-permute-start | bytes 1585160 | tf_op jit(solution)/shard_map/ppermute | solution.py:119
  50.6 2.7 %collective-permute-start.1 = (bf16[2,1032,128]{2,1,0:T(8,128)(2,1)S(1)}, bf16[2,1032,128]{2,1,0:T(8,128)(2,1)S(1)}, u32[]{:S(2)}, u32[]{:S(2)}) collective-permute-start(bf16[2,1032,128]{2,1,0:T(8,128)(2,1)S(1)} %pad_maximum_fusion), channel_id=1, source_target_pairs={{0,2},{1,3},{2,0},{3,1},{4,6},{5,7},{6,4},{7,5},{8,10},{9,11},{10,... | collective-permute-start | bytes 1585160 | tf_op jit(solution)/shard_map/ppermute | solution.py:119
  53.3 5.0 %shard_map.64 = (f32[1024,128]{1,0:T(8,128)S(1)}, f32[1024,1]{1,0:T(8,128)S(1)}, f32[1024,1]{1,0:T(8,128)S(1)}) custom-call(bf16[1024,128]{1,0:T(8,128)(2,1)S(1)} %reshape_reshape.3.query_ref, bf16[1024,128]{1,0:T(8,128)(2,1)S(1)} %slice_bitcast_fusion.7.key_ref, bf16[1024,128]{1,0:T(8,128)(2,1)S(1)} %slice_bitcast_fusion.6.value_ref), custom_call_target="tpu_custom_call" | custom-call | flops 805306368 | bytes 1318912 | tf_op jit(solution)/shard_map/pallas_call | solution.py:50
  58.4 0.0 collective-permute-done
  58.4 5.0 %shard_map.65 = (f32[1024,128]{1,0:T(8,128)S(1)}, f32[1024,1]{1,0:T(8,128)S(1)}, f32[1024,1]{1,0:T(8,128)S(1)}) custom-call(bf16[1024,128]{1,0:T(8,128)(2,1)S(1)} %reshape_reshape.3.query_ref, bf16[1024,128]{1,0:T(8,128)(2,1)S(1)} %get-tuple-element.51.key_ref, bf16[1024,128]{1,0:T(8,128)(2,1)S(1)} %get-tuple-element.50.value_ref), custom_call_target="tpu_custom_call" | custom-call | flops 805306368 | bytes 1318912 | tf_op jit(solution)/shard_map/pallas_call | solution.py:50
  63.4 8.2 %collective-permute-done.1 = bf16[2,1032,128]{2,1,0:T(8,128)(2,1)S(1)} collective-permute-done((bf16[2,1032,128]{2,1,0:T(8,128)(2,1)S(1)}, bf16[2,1032,128]{2,1,0:T(8,128)(2,1)S(1)}, u32[]{:S(2)}, u32[]{:S(2)}) %collective-permute-start.1) | collective-permute-done | bytes 528416 | tf_op jit(solution)/shard_map/ppermute | solution.py:119
  71.6 0.7 copy-done.1
  72.4 5.0 %shard_map.66 = (f32[1024,128]{1,0:T(8,128)S(1)}, f32[1024,1]{1,0:T(8,128)S(1)}, f32[1024,1]{1,0:T(8,128)S(1)}) custom-call(bf16[1024,128]{1,0:T(8,128)(2,1)S(1)} %reshape_reshape.3.query_ref, bf16[1024,128]{1,0:T(8,128)(2,1)S(1)} %get-tuple-element.53.key_ref, bf16[1024,128]{1,0:T(8,128)(2,1)S(1)} %get-tuple-element.52.value_ref), custom_call_target="tpu_custom_call" | custom-call | flops 805306368 | bytes 1318912 | tf_op jit(solution)/shard_map/pallas_call | solution.py:50
  77.3 0.0 collective-permute-done.2
  77.4 0.0 copy-start
  77.4 0.8 copy-done
  78.2 5.0 %shard_map.67 = (f32[1024,128]{1,0:T(8,128)S(1)}, f32[1024,1]{1,0:T(8,128)S(1)}, f32[1024,1]{1,0:T(8,128)S(1)}) custom-call(bf16[1024,128]{1,0:T(8,128)(2,1)S(1)} %reshape_reshape.3.query_ref, bf16[1024,128]{1,0:T(8,128)(2,1)S(1)} %get-tuple-element.55.key_ref, bf16[1024,128]{1,0:T(8,128)(2,1)S(1)} %get-tuple-element.54.value_ref), custom_call_target="tpu_custom_call" | custom-call | flops 805306368 | bytes 1318912 | tf_op jit(solution)/shard_map/pallas_call | solution.py:50
  83.1 0.0 copy-start.2
  83.2 1.2 add_reduce_fusion
  84.3 0.1 reshape.249
  84.4 0.1 reshape.243
  84.5 0.7 slice_bitcast_fusion.8
  85.2 0.7 slice_bitcast_fusion.9
  85.9 0.2 fusion.38
  86.1 0.1 copy.62
  86.2 0.1 reshape.251
  86.3 0.1 fusion.9
  86.4 0.1 copy.64
  86.6 0.3 fusion.11
  86.9 0.6 add_bitcast_fusion
  87.5 0.4 fusion
  87.8 0.3 copy.95
  88.2 0.1 copy.93
  88.3 0.1 concatenate.23
  88.4 0.6 copy.60
  89.0 29.9 %all_to_all.26 = f32[128,1,1040]{2,1,0:T(1,128)S(1)} all-to-all(f32[128,1,1040]{2,1,0:T(1,128)S(1)} %copy.60), channel_id=1, replica_groups=mesh['grp'=16,'w'=8,'zq'=4] {'grp','w'}, dimensions={0} | all-to-all | bytes 1064960 | tf_op jit(solution)/shard_map/all_to_all | solution.py:169
  119.0 0.1 fusion.12
  119.1 0.1 copy.61
  119.1 0.2 fusion.2
  119.4 0.1 bitcast_divide_fusion
  119.4 0.4 broadcast_in_dim.38
  119.9 15.7 %all_to_all.27 = f32[16,1,8192]{2,1,0:T(1,128)S(1)} all-to-all(f32[16,1,8192]{2,1,0:T(1,128)S(1)} %broadcast_in_dim.38), channel_id=1, replica_groups=mesh['grp'=16,'w'=8,'zq'=4] {'grp'}, dimensions={0} | all-to-all | bytes 1048576 | tf_op jit(solution)/shard_map/all_to_all | solution.py:181
  135.6 1.1 copy.94
  (28 shorter events, 0.5 us)
Async XLA Ops:
  6.4 11.6 %copy-start.3 = (s32[512]{0:T(512)S(1)}, s32[512]{0:T(512)}, u32[]{:S(2)}) copy-start(s32[512]{0:T(512)} %param.11) | copy-start | bytes 6148
  7.5 33.5 %all-to-all-start = ((bf16[8,2,24704]{2,1,0:T(2,128)(2,1)}), bf16[8,2,24704]{2,1,0:T(2,128)(2,1)S(1)}, u32[]{:S(2)}, u32[]{:S(2)}) async-start(bf16[8,2,24704]{2,1,0:T(2,128)(2,1)} %reshape.273), calls=%async_computation | async-start | bytes 1581056 | tf_op jit(solution)/shard_map/all_to_all | solution.py:95
  44.0 14.3 %collective-permute-start = (bf16[2,1032,128]{2,1,0:T(8,128)(2,1)S(1)}, bf16[2,1032,128]{2,1,0:T(8,128)(2,1)S(1)}, u32[]{:S(2)}, u32[]{:S(2)}) collective-permute-start(bf16[2,1032,128]{2,1,0:T(8,128)(2,1)S(1)} %pad_maximum_fusion), channel_id=1, source_target_pairs={{0,1},{1,2},{2,3},{3,0},{4,5},{5,6},{6,7},{7,4},{8,9},{9,10},{10,1... | collective-permute-start | bytes 1585160 | tf_op jit(solution)/shard_map/ppermute | solution.py:119
  47.0 30.4 %collective-permute-start.2 = (bf16[2,1032,128]{2,1,0:T(8,128)(2,1)S(1)}, bf16[2,1032,128]{2,1,0:T(8,128)(2,1)S(1)}, u32[]{:S(2)}, u32[]{:S(2)}) collective-permute-start(bf16[2,1032,128]{2,1,0:T(8,128)(2,1)S(1)} %pad_maximum_fusion), channel_id=1, source_target_pairs={{0,3},{1,0},{2,1},{3,2},{4,7},{5,4},{6,5},{7,6},{8,11},{9,8},{10,9... | collective-permute-start | bytes 1585160 | tf_op jit(solution)/shard_map/ppermute | solution.py:119
  50.6 21.0 %collective-permute-start.1 = (bf16[2,1032,128]{2,1,0:T(8,128)(2,1)S(1)}, bf16[2,1032,128]{2,1,0:T(8,128)(2,1)S(1)}, u32[]{:S(2)}, u32[]{:S(2)}) collective-permute-start(bf16[2,1032,128]{2,1,0:T(8,128)(2,1)S(1)} %pad_maximum_fusion), channel_id=1, source_target_pairs={{0,2},{1,3},{2,0},{3,1},{4,6},{5,7},{6,4},{7,5},{8,10},{9,11},{10,... | collective-permute-start | bytes 1585160 | tf_op jit(solution)/shard_map/ppermute | solution.py:119
  71.6 0.8 copy-start.1
  77.4 0.8 copy-start
  83.1 2.7 %copy-start.2 = (bf16[128,8,128]{2,1,0:T(8,128)(2,1)S(1)}, bf16[128,8,128]{2,1,0:T(8,128)(2,1)}, u32[]{:S(2)}) copy-start(bf16[128,8,128]{2,1,0:T(8,128)(2,1)} %reshape.246) | copy-start | bytes 786436

commit v16 on v10

--- a/solution.py
+++ b/solution.py
@@ -115,13 +115,13 @@
     )
     local_keys = ways * positions
     both_here = jnp.stack([keys_here, values_here])
-    blocks = [both_here] + [
-        lax.ppermute(both_here, "zq", [(i, (i + shift) % quarters) for i in range(quarters)])
-        for shift in range(1, quarters)
-    ]
+    def swap(value, mask):
+        return lax.ppermute(value, "zq", [(i, i ^ mask) for i in range(quarters)])
+    across = swap(both_here, 2)
+    blocks = [both_here, swap(both_here, 1), across, swap(across, 1)]
     draft_k = jnp.concatenate([block[0, local_keys:] for block in blocks], axis=0)
     draft_v = jnp.concatenate([block[1, local_keys:] for block in blocks], axis=0)
-    source_quarter = (quarter - lax.iota(jnp.int32, quarters)) % quarters
+    source_quarter = jnp.bitwise_xor(quarter, lax.iota(jnp.int32, quarters))
 
     block_rows = ways * rows
     query_rows = query_block.reshape(block_rows * group_heads, HD)

time: 136 us -> 137 us (level)
  blocking collectives: 45.6 us -> 53.1 us
  waiting for transfers between devices: 33.9 us -> 29.5 us
  starting transfers between devices: 18.6 us -> 16.9 us
    all_to_all x1, blocking collectives: 29.9 us -> 34.4 us  [local(): parts = lax.all_to_all(packed, ('grp', 'w'), 0, 0, tiled=True)]
    ppermute x3, waiting for transfers between devices: 11.1 us -> 6.77 us  [swap(): return lax.ppermute(value, 'zq', [(i, i ^ mask) for i in range(quarters)])]
    all_to_all x1, blocking collectives: 15.7 us -> 18.7 us  [local(): attended = lax.all_to_all(attended, 'grp', 0, 0, tiled=True)]
    ppermute x3, starting transfers between devices: 8.29 us -> 6.55 us  [swap(): return lax.ppermute(value, 'zq', [(i, i ^ mask) for i in range(quarters)])]
    unnamed x21 -> x17, local copies, waits for them, and re-layouts: 9.56 us -> 8.05 us
  transfers between devices with their start and end apart: 4 -> 4, of which waited for: 2 -> 2; matrix products, arithmetic and copies ran while one was open for 1% -> 2% of each run, Pallas kernels for 8% -> 8%
where the time goes in v16:
time: 137 us; the launch traced here: 134 us
  blocking collectives  53.1 us (39%)
  waiting for transfers between devices  29.5 us (22%)
  starting transfers between devices  16.9 us (12%)
  local copies, waits for them, and re-layouts  14 us (10%)
  Pallas kernels  14 us (10%)
  other arithmetic  5.19 us (4%)
    all_to_all x1, blocking collectives, local(): parts = lax.all_to_all(packed, ('grp', 'w'), 0, 0, tiled=True)  34.4 us
    all_to_all x1, waiting for transfers between devices, local(): got = lax.all_to_all(send, 'w', 0, 0, tiled=True)  22.7 us
    all_to_all x1, blocking collectives, local(): attended = lax.all_to_all(attended, 'grp', 0, 0, tiled=True)  18.7 us
    pallas_call x4, Pallas kernels, attend_prefix(): pl.pallas_call(functools.partial(attend_kernel, inverse_root), grid=(coun...  14 us
    all_to_all x1, starting transfers between devices, local(): got = lax.all_to_all(send, 'w', 0, 0, tiled=True)  10.3 us
    unnamed x17, local copies, waits for them, and re-layouts  8.05 us
    ppermute x3, waiting for transfers between devices, swap(): return lax.ppermute(value, 'zq', [(i, i ^ mask) for i in range(quarters)])  6.77 us
    ppermute x3, starting transfers between devices, swap(): return lax.ppermute(value, 'zq', [(i, i ^ mask) for i in range(quarters)])  6.55 us
  transfers between devices with their start and end apart: 4, of which 2 were waited for; matrix products, arithmetic and copies ran while one was open for 2% of the time, Pallas kernels for 8%

profile of v16, /device:TPU:6, one launch (start us, length us, event | category | flops | bytes accessed | tf_op | source)
XLA Modules:
  0.0 133.9 jit_solution(1953836845697790685)
XLA Ops:
  0.0 0.7 reduce.1
  0.7 0.7 reduce.2
  1.4 1.1 copy.71
  2.5 1.0 copy.72
  3.5 1.0 copy.73
  4.6 0.5 broadcast.175
  5.1 1.2 reduce.20
  6.4 0.0 copy-start.1
  6.4 1.1 reshape.262
  7.5 10.3 %all-to-all-start = ((bf16[8,2,24704]{2,1,0:T(2,128)(2,1)}), bf16[8,2,24704]{2,1,0:T(2,128)(2,1)S(1)}, u32[]{:S(2)}, u32[]{:S(2)}) async-start(bf16[8,2,24704]{2,1,0:T(2,128)(2,1)} %reshape.262), calls=%async_computation | async-start | bytes 1581056 | tf_op jit(solution)/shard_map/all_to_all | solution.py:95
  17.8 0.1 add_add_fusion
  17.9 0.1 add.115
  18.0 0.0 copy-done.1
  18.0 0.1 reshape.233
  18.1 0.1 reshape.234
  18.2 0.1 compare_and_fusion
  18.3 22.7 %all-to-all-done = bf16[8,2,24704]{2,1,0:T(2,128)(2,1)S(1)} async-done(((bf16[8,2,24704]{2,1,0:T(2,128)(2,1)}), bf16[8,2,24704]{2,1,0:T(2,128)(2,1)S(1)}, u32[]{:S(2)}, u32[]{:S(2)}) %all-to-all-start) | async-done | bytes 790560 | tf_op jit(solution)/shard_map/all_to_all | solution.py:95
  41.0 2.5 %reshape.263 = bf16[8,1,49408]{2,1,0:T(2,128)(2,1)S(1)} reshape(bf16[8,2,24704]{2,1,0:T(2,128)(2,1)S(1)} %all-to-all-done) | data formatting | bytes 1581056
  43.5 0.1 copy.91
  43.6 0.1 fusion.35
  43.6 0.1 reshape.229
  43.8 0.1 reshape.230
  44.0 0.1 pad_maximum_fusion
  44.0 2.7 %collective-permute-start.1 = (bf16[2,1032,128]{2,1,0:T(8,128)(2,1)S(1)}, bf16[2,1032,128]{2,1,0:T(8,128)(2,1)}, u32[]{:S(2)}, u32[]{:S(2)}) collective-permute-start(bf16[2,1032,128]{2,1,0:T(8,128)(2,1)S(1)} %pad_maximum_fusion), channel_id=1, source_target_pairs={{0,2},{1,3},{2,0},{3,1},{4,6},{5,7},{6,4},{7,5},{8,10},{9,11},{10,... | collective-permute-start | bytes 1585160 | tf_op jit(solution)/shard_map/ppermute | solution.py:119
  46.8 0.1 reshape_reshape.3.query_ref
  46.9 0.8 reshape.235
  47.8 1.9 %collective-permute-start = (bf16[2,1032,128]{2,1,0:T(8,128)(2,1)S(1)}, bf16[2,1032,128]{2,1,0:T(8,128)(2,1)S(1)}, u32[]{:S(2)}, u32[]{:S(2)}) collective-permute-start(bf16[2,1032,128]{2,1,0:T(8,128)(2,1)S(1)} %pad_maximum_fusion), channel_id=1, source_target_pairs={{0,1},{1,0},{2,3},{3,2},{4,5},{5,4},{6,7},{7,6},{8,9},{9,8},{10,11... | collective-permute-start | bytes 1585160 | tf_op jit(solution)/shard_map/ppermute | solution.py:119
  49.7 3.5 %shard_map.64 = (f32[1024,128]{1,0:T(8,128)S(1)}, f32[1024,1]{1,0:T(8,128)S(1)}, f32[1024,1]{1,0:T(8,128)S(1)}) custom-call(bf16[1024,128]{1,0:T(8,128)(2,1)S(1)} %reshape_reshape.3.query_ref, bf16[1024,128]{1,0:T(8,128)(2,1)S(1)} %slice_bitcast_fusion.7.key_ref, bf16[1024,128]{1,0:T(8,128)(2,1)S(1)} %slice_bitcast_fusion.6.value_ref), custom_call_target="tpu_custom_call" | custom-call | flops 805306368 | bytes 1318912 | tf_op jit(solution)/shard_map/pallas_call | solution.py:50
  53.2 6.8 %collective-permute-done.1 = bf16[2,1032,128]{2,1,0:T(8,128)(2,1)} collective-permute-done((bf16[2,1032,128]{2,1,0:T(8,128)(2,1)S(1)}, bf16[2,1032,128]{2,1,0:T(8,128)(2,1)}, u32[]{:S(2)}, u32[]{:S(2)}) %collective-permute-start.1) | collective-permute-done | bytes 528416 | tf_op jit(solution)/shard_map/ppermute | solution.py:119
  60.0 1.9 %collective-permute-start.2 = (bf16[2,1032,128]{2,1,0:T(8,128)(2,1)}, bf16[2,1032,128]{2,1,0:T(8,128)(2,1)S(1)}, u32[]{:S(2)}, u32[]{:S(2)}) collective-permute-start(bf16[2,1032,128]{2,1,0:T(8,128)(2,1)} %collective-permute-done.1), channel_id=1, source_target_pairs={{0,1},{1,0},{2,3},{3,2},{4,5},{5,4},{6,7},{7,6},{8,9},{9,8},{10,11... | collective-permute-start | bytes 1585160 | tf_op jit(solution)/shard_map/ppermute | solution.py:119
  61.9 1.1 slice_bitcast_fusion.2
  63.0 0.0 collective-permute-done
  63.0 3.5 %shard_map.65 = (f32[1024,128]{1,0:T(8,128)S(1)}, f32[1024,1]{1,0:T(8,128)S(1)}, f32[1024,1]{1,0:T(8,128)S(1)}) custom-call(bf16[1024,128]{1,0:T(8,128)(2,1)S(1)} %reshape_reshape.3.query_ref, bf16[1024,128]{1,0:T(8,128)(2,1)S(1)} %get-tuple-element.51.key_ref, bf16[1024,128]{1,0:T(8,128)(2,1)S(1)} %get-tuple-element.50.value_ref), custom_call_target="tpu_custom_call" | custom-call | flops 805306368 | bytes 1318912 | tf_op jit(solution)/shard_map/pallas_call | solution.py:50
  66.5 3.5 %shard_map.66 = (f32[1024,128]{1,0:T(8,128)S(1)}, f32[1024,1]{1,0:T(8,128)S(1)}, f32[1024,1]{1,0:T(8,128)S(1)}) custom-call(bf16[1024,128]{1,0:T(8,128)(2,1)S(1)} %reshape_reshape.3.query_ref, bf16[1024,128]{1,0:T(8,128)(2,1)S(1)} %get-tuple-element.53.key_ref, bf16[1024,128]{1,0:T(8,128)(2,1)S(1)} %get-tuple-element.52.value_ref), custom_call_target="tpu_custom_call" | custom-call | flops 805306368 | bytes 1318912 | tf_op jit(solution)/shard_map/pallas_call | solution.py:50
  70.0 0.7 slice_bitcast_fusion.9
  70.7 0.0 collective-permute-done.2
  70.8 3.5 %shard_map.67 = (f32[1024,128]{1,0:T(8,128)S(1)}, f32[1024,1]{1,0:T(8,128)S(1)}, f32[1024,1]{1,0:T(8,128)S(1)}) custom-call(bf16[1024,128]{1,0:T(8,128)(2,1)S(1)} %reshape_reshape.3.query_ref, bf16[1024,128]{1,0:T(8,128)(2,1)S(1)} %get-tuple-element.55.key_ref, bf16[1024,128]{1,0:T(8,128)(2,1)S(1)} %get-tuple-element.54.value_ref), custom_call_target="tpu_custom_call" | custom-call | flops 805306368 | bytes 1318912 | tf_op jit(solution)/shard_map/pallas_call | solution.py:50
  74.3 0.0 copy-start
  74.3 1.2 add_reduce_fusion
  75.4 0.1 reshape.238
  75.5 0.1 reshape.232
  75.6 0.0 copy-done
  75.7 0.2 fusion.37
  75.9 0.1 copy.62
  76.0 0.1 reshape.240
  76.1 0.1 fusion.9
  76.2 0.1 copy.64
  76.4 0.3 fusion.11
  76.7 0.6 add_bitcast_fusion
  77.3 0.4 fusion
  77.6 0.3 copy.95
  77.9 0.1 copy.93
  78.1 0.1 concatenate.23
  78.1 0.6 copy.60
  78.8 34.4 %all_to_all.26 = f32[128,1,1040]{2,1,0:T(1,128)S(1)} all-to-all(f32[128,1,1040]{2,1,0:T(1,128)S(1)} %copy.60), channel_id=1, replica_groups=mesh['grp'=16,'w'=8,'zq'=4] {'grp','w'}, dimensions={0} | all-to-all | bytes 1064960 | tf_op jit(solution)/shard_map/all_to_all | solution.py:169
  113.2 0.1 fusion.12
  113.3 0.1 copy.61
  113.4 0.2 fusion.2
  113.6 0.1 bitcast_divide_fusion
  113.7 0.4 broadcast_in_dim.38
  114.1 18.7 %all_to_all.27 = f32[16,1,8192]{2,1,0:T(1,128)S(1)} all-to-all(f32[16,1,8192]{2,1,0:T(1,128)S(1)} %broadcast_in_dim.38), channel_id=1, replica_groups=mesh['grp'=16,'w'=8,'zq'=4] {'grp'}, dimensions={0} | all-to-all | bytes 1048576 | tf_op jit(solution)/shard_map/all_to_all | solution.py:181
  132.8 1.1 copy.94
  (26 shorter events, 0.5 us)
Async XLA Ops:
  6.4 11.6 %copy-start.1 = (s32[512]{0:T(512)S(1)}, s32[512]{0:T(512)}, u32[]{:S(2)}) copy-start(s32[512]{0:T(512)} %param.11) | copy-start | bytes 6148
  7.5 33.5 %all-to-all-start = ((bf16[8,2,24704]{2,1,0:T(2,128)(2,1)}), bf16[8,2,24704]{2,1,0:T(2,128)(2,1)S(1)}, u32[]{:S(2)}, u32[]{:S(2)}) async-start(bf16[8,2,24704]{2,1,0:T(2,128)(2,1)} %reshape.262), calls=%async_computation | async-start | bytes 1581056 | tf_op jit(solution)/shard_map/all_to_all | solution.py:95
  44.0 15.9 %collective-permute-start.1 = (bf16[2,1032,128]{2,1,0:T(8,128)(2,1)S(1)}, bf16[2,1032,128]{2,1,0:T(8,128)(2,1)}, u32[]{:S(2)}, u32[]{:S(2)}) collective-permute-start(bf16[2,1032,128]{2,1,0:T(8,128)(2,1)S(1)} %pad_maximum_fusion), channel_id=1, source_target_pairs={{0,2},{1,3},{2,0},{3,1},{4,6},{5,7},{6,4},{7,5},{8,10},{9,11},{10,... | collective-permute-start | bytes 1585160 | tf_op jit(solution)/shard_map/ppermute | solution.py:119
  47.8 15.2 %collective-permute-start = (bf16[2,1032,128]{2,1,0:T(8,128)(2,1)S(1)}, bf16[2,1032,128]{2,1,0:T(8,128)(2,1)S(1)}, u32[]{:S(2)}, u32[]{:S(2)}) collective-permute-start(bf16[2,1032,128]{2,1,0:T(8,128)(2,1)S(1)} %pad_maximum_fusion), channel_id=1, source_target_pairs={{0,1},{1,0},{2,3},{3,2},{4,5},{5,4},{6,7},{7,6},{8,9},{9,8},{10,11... | collective-permute-start | bytes 1585160 | tf_op jit(solution)/shard_map/ppermute | solution.py:119
  60.0 10.7 %collective-permute-start.2 = (bf16[2,1032,128]{2,1,0:T(8,128)(2,1)}, bf16[2,1032,128]{2,1,0:T(8,128)(2,1)S(1)}, u32[]{:S(2)}, u32[]{:S(2)}) collective-permute-start(bf16[2,1032,128]{2,1,0:T(8,128)(2,1)} %collective-permute-done.1), channel_id=1, source_target_pairs={{0,1},{1,0},{2,3},{3,2},{4,5},{5,4},{6,7},{7,6},{8,9},{9,8},{10,11... | collective-permute-start | bytes 1585160 | tf_op jit(solution)/shard_map/ppermute | solution.py:119
  74.3 1.4 %copy-start = (bf16[128,8,128]{2,1,0:T(8,128)(2,1)S(1)}, bf16[128,8,128]{2,1,0:T(8,128)(2,1)}, u32[]{:S(2)}) copy-start(bf16[128,8,128]{2,1,0:T(8,128)(2,1)} %reshape.235) | copy-start | bytes 786436

commit v17 on v16

--- a/solution.py
+++ b/solution.py
@@ -161,21 +161,20 @@
 
     groups = lax.axis_size("grp")
     def by_destination(part):
-        part = part.reshape((ways, groups) + part.shape[1:])
-        return part.transpose((1, 0) + tuple(range(2, part.ndim))).reshape(groups * ways, -1)
+        return part.reshape(ways * groups, -1)
     packed = jnp.concatenate(
         [by_destination(summed), by_destination(peak), by_destination(totals)], axis=1
     )
-    parts = lax.all_to_all(packed, ("grp", "w"), 0, 0, tiled=True)
+    parts = lax.all_to_all(packed, ("w", "grp"), 0, 0, tiled=True)
     sum_size = group_heads * HD
-    parts = parts.reshape(groups, KV, -1)
-    part_sums = parts[:, :, :sum_size].reshape(groups, KV, group_heads, HD)
+    parts = parts.reshape(KV, groups, -1)
+    part_sums = parts[:, :, :sum_size].reshape(KV, groups, group_heads, HD)
     part_peaks = parts[:, :, sum_size : sum_size + group_heads]
     part_totals = parts[:, :, sum_size + group_heads :]
-    joined = jnp.max(part_peaks, axis=0)
-    scales = jnp.exp(part_peaks - joined[None])
-    merged_totals = jnp.sum(part_totals * scales, axis=0)
-    merged_sums = jnp.sum(part_sums * scales[..., None], axis=0)
+    joined = jnp.max(part_peaks, axis=1)
+    scales = jnp.exp(part_peaks - joined[:, None])
+    merged_totals = jnp.sum(part_totals * scales, axis=1)
+    merged_sums = jnp.sum(part_sums * scales[..., None], axis=1)
     attended = (merged_sums / merged_totals[..., None]).reshape(1, H * HD)
     attended = jnp.broadcast_to(attended[None], (groups,) + attended.shape)
     attended = lax.all_to_all(attended, "grp", 0, 0, tiled=True)

time: 137 us -> 135 us (0.985)
  local copies, waits for them, and re-layouts: 14 us -> 11.6 us
    all_to_all x1, blocking collectives: 34.4 us -> 32.1 us  [local(): parts = lax.all_to_all(packed, ('w', 'grp'), 0, 0, tiled=True)]
    all_to_all x1, blocking collectives: 18.7 us -> 20.9 us  [local(): attended = lax.all_to_all(attended, 'grp', 0, 0, tiled=True)]
    unnamed x17 -> x14, local copies, waits for them, and re-layouts: 8.05 us -> 7.95 us
  transfers between devices with their start and end apart: 4 -> 4, of which waited for: 2 -> 2; matrix products, arithmetic and copies ran while one was open for 2% -> 1% of each run, Pallas kernels for 8% -> 8%
where the time goes in v17:
time: 135 us; the launch traced here: 132 us
  blocking collectives  52.9 us (39%)
  waiting for transfers between devices  30.1 us (22%)
  starting transfers between devices  16.9 us (13%)
  Pallas kernels  14 us (10%)
  local copies, waits for them, and re-layouts  11.6 us (9%)
  other arithmetic  5.61 us (4%)
    all_to_all x1, blocking collectives, local(): parts = lax.all_to_all(packed, ('w', 'grp'), 0, 0, tiled=True)  32.1 us
    all_to_all x1, waiting for transfers between devices, local(): got = lax.all_to_all(send, 'w', 0, 0, tiled=True)  22.7 us
    all_to_all x1, blocking collectives, local(): attended = lax.all_to_all(attended, 'grp', 0, 0, tiled=True)  20.9 us
    pallas_call x4, Pallas kernels, attend_prefix(): pl.pallas_call(functools.partial(attend_kernel, inverse_root), grid=(coun...  14 us
    all_to_all x1, starting transfers between devices, local(): got = lax.all_to_all(send, 'w', 0, 0, tiled=True)  10.3 us
    unnamed x14, local copies, waits for them, and re-layouts  7.95 us
    ppermute x3, waiting for transfers between devices, swap(): return lax.ppermute(value, 'zq', [(i, i ^ mask) for i in range(quarters)])  7.34 us
    ppermute x3, starting transfers between devices, swap(): return lax.ppermute(value, 'zq', [(i, i ^ mask) for i in range(quarters)])  6.57 us
  transfers between devices with their start and end apart: 4, of which 2 were waited for; matrix products, arithmetic and copies ran while one was open for 1% of the time, Pallas kernels for 8%

profile of v17, /device:TPU:6, one launch (start us, length us, event | category | flops | bytes accessed | tf_op | source)
XLA Modules:
  0.0 132.3 jit_solution(8266217479373380763)
XLA Ops:
  0.0 0.7 reduce.1
  0.7 0.7 reduce.2
  1.4 1.1 copy.42
  2.5 1.0 copy.43
  3.5 1.0 copy.44
  4.6 0.5 broadcast.174
  5.1 1.2 reduce.19
  6.4 0.0 copy-start
  6.4 1.1 reshape.238
  7.5 10.3 %all-to-all-start = ((bf16[8,2,24704]{2,1,0:T(2,128)(2,1)}), bf16[8,2,24704]{2,1,0:T(2,128)(2,1)S(1)}, u32[]{:S(2)}, u32[]{:S(2)}) async-start(bf16[8,2,24704]{2,1,0:T(2,128)(2,1)} %reshape.238), calls=%async_computation | async-start | bytes 1581056 | tf_op jit(solution)/shard_map/all_to_all | solution.py:95
  17.8 0.1 add_add_fusion
  17.9 0.1 add.114
  18.0 0.0 copy-done
  18.0 0.1 reshape.214
  18.1 0.1 reshape.215
  18.2 0.1 compare_and_fusion
  18.3 22.7 %all-to-all-done = bf16[8,2,24704]{2,1,0:T(2,128)(2,1)S(1)} async-done(((bf16[8,2,24704]{2,1,0:T(2,128)(2,1)}), bf16[8,2,24704]{2,1,0:T(2,128)(2,1)S(1)}, u32[]{:S(2)}, u32[]{:S(2)}) %all-to-all-start) | async-done | bytes 790560 | tf_op jit(solution)/shard_map/all_to_all | solution.py:95
  41.0 2.5 %reshape.239 = bf16[8,1,49408]{2,1,0:T(2,128)(2,1)S(1)} reshape(bf16[8,2,24704]{2,1,0:T(2,128)(2,1)S(1)} %all-to-all-done) | data formatting | bytes 1581056
  43.5 0.1 copy.53
  43.6 0.1 fusion.40
  43.6 0.1 reshape.210
  43.8 0.1 reshape.211
  44.0 0.1 pad_maximum_fusion
  44.0 2.7 %collective-permute-start.1 = (bf16[2,1032,128]{2,1,0:T(8,128)(2,1)S(1)}, bf16[2,1032,128]{2,1,0:T(8,128)(2,1)S(1)}, u32[]{:S(2)}, u32[]{:S(2)}) collective-permute-start(bf16[2,1032,128]{2,1,0:T(8,128)(2,1)S(1)} %pad_maximum_fusion), channel_id=1, source_target_pairs={{0,2},{1,3},{2,0},{3,1},{4,6},{5,7},{6,4},{7,5},{8,10},{9,11},{10,... | collective-permute-start | bytes 1585160 | tf_op jit(solution)/shard_map/ppermute | solution.py:119
  46.8 0.1 reshape_reshape.3.query_ref
  46.9 0.1 reshape.216
  47.1 1.9 %collective-permute-start = (bf16[2,1032,128]{2,1,0:T(8,128)(2,1)S(1)}, bf16[2,1032,128]{2,1,0:T(8,128)(2,1)S(1)}, u32[]{:S(2)}, u32[]{:S(2)}) collective-permute-start(bf16[2,1032,128]{2,1,0:T(8,128)(2,1)S(1)} %pad_maximum_fusion), channel_id=1, source_target_pairs={{0,1},{1,0},{2,3},{3,2},{4,5},{5,4},{6,7},{7,6},{8,9},{9,8},{10,11... | collective-permute-start | bytes 1585160 | tf_op jit(solution)/shard_map/ppermute | solution.py:119
  49.0 3.5 %shard_map.64 = (f32[1024,128]{1,0:T(8,128)S(1)}, f32[1024,1]{1,0:T(8,128)S(1)}, f32[1024,1]{1,0:T(8,128)S(1)}) custom-call(bf16[1024,128]{1,0:T(8,128)(2,1)S(1)} %reshape_reshape.3.query_ref, bf16[1024,128]{1,0:T(8,128)(2,1)S(1)} %slice_bitcast_fusion.7.key_ref, bf16[1024,128]{1,0:T(8,128)(2,1)S(1)} %slice_bitcast_fusion.6.value_ref), custom_call_target="tpu_custom_call" | custom-call | flops 805306368 | bytes 1318912 | tf_op jit(solution)/shard_map/pallas_call | solution.py:50
  52.5 7.3 %collective-permute-done.1 = bf16[2,1032,128]{2,1,0:T(8,128)(2,1)S(1)} collective-permute-done((bf16[2,1032,128]{2,1,0:T(8,128)(2,1)S(1)}, bf16[2,1032,128]{2,1,0:T(8,128)(2,1)S(1)}, u32[]{:S(2)}, u32[]{:S(2)}) %collective-permute-start.1) | collective-permute-done | bytes 528416 | tf_op jit(solution)/shard_map/ppermute | solution.py:119
  59.9 1.9 %collective-permute-start.2 = (bf16[2,1032,128]{2,1,0:T(8,128)(2,1)S(1)}, bf16[2,1032,128]{2,1,0:T(8,128)(2,1)S(1)}, u32[]{:S(2)}, u32[]{:S(2)}) collective-permute-start(bf16[2,1032,128]{2,1,0:T(8,128)(2,1)S(1)} %collective-permute-done.1), channel_id=1, source_target_pairs={{0,1},{1,0},{2,3},{3,2},{4,5},{5,4},{6,7},{7,6},{8,9},{9,8},{10,11... | collective-permute-start | bytes 1585160 | tf_op jit(solution)/shard_map/ppermute | solution.py:119
  61.8 0.0 collective-permute-done
  61.9 3.5 %shard_map.65 = (f32[1024,128]{1,0:T(8,128)S(1)}, f32[1024,1]{1,0:T(8,128)S(1)}, f32[1024,1]{1,0:T(8,128)S(1)}) custom-call(bf16[1024,128]{1,0:T(8,128)(2,1)S(1)} %reshape_reshape.3.query_ref, bf16[1024,128]{1,0:T(8,128)(2,1)S(1)} %get-tuple-element.51.key_ref, bf16[1024,128]{1,0:T(8,128)(2,1)S(1)} %get-tuple-element.50.value_ref), custom_call_target="tpu_custom_call" | custom-call | flops 805306368 | bytes 1318912 | tf_op jit(solution)/shard_map/pallas_call | solution.py:50
  65.4 3.5 %shard_map.66 = (f32[1024,128]{1,0:T(8,128)S(1)}, f32[1024,1]{1,0:T(8,128)S(1)}, f32[1024,1]{1,0:T(8,128)S(1)}) custom-call(bf16[1024,128]{1,0:T(8,128)(2,1)S(1)} %reshape_reshape.3.query_ref, bf16[1024,128]{1,0:T(8,128)(2,1)S(1)} %get-tuple-element.53.key_ref, bf16[1024,128]{1,0:T(8,128)(2,1)S(1)} %get-tuple-element.52.value_ref), custom_call_target="tpu_custom_call" | custom-call | flops 805306368 | bytes 1318912 | tf_op jit(solution)/shard_map/pallas_call | solution.py:50
  68.9 0.0 collective-permute-done.2
  69.0 3.5 %shard_map.67 = (f32[1024,128]{1,0:T(8,128)S(1)}, f32[1024,1]{1,0:T(8,128)S(1)}, f32[1024,1]{1,0:T(8,128)S(1)}) custom-call(bf16[1024,128]{1,0:T(8,128)(2,1)S(1)} %reshape_reshape.3.query_ref, bf16[1024,128]{1,0:T(8,128)(2,1)S(1)} %get-tuple-element.55.key_ref, bf16[1024,128]{1,0:T(8,128)(2,1)S(1)} %get-tuple-element.54.value_ref), custom_call_target="tpu_custom_call" | custom-call | flops 805306368 | bytes 1318912 | tf_op jit(solution)/shard_map/pallas_call | solution.py:50
  72.5 1.1 fusion.4
  73.6 0.6 add_bitcast_fusion
  74.2 0.2 copy.36
  74.5 0.1 reshape.218
  74.6 0.1 reshape.213
  74.8 0.2 fusion.42
  75.1 0.3 fusion.11
  75.4 0.3 fusion
  75.7 0.9 copy.38
  76.6 32.1 %all_to_all.26 = f32[128,1,1040]{2,1,0:T(1,128)S(1)} all-to-all(f32[128,1,1040]{2,1,0:T(1,128)S(1)} %copy.38), channel_id=1, replica_groups=mesh['grp'=16,'w'=8,'zq'=4] {'w','grp'}, dimensions={0} | all-to-all | bytes 1064960 | tf_op jit(solution)/shard_map/all_to_all | solution.py:168
  108.7 0.7 fusion.12
  109.4 0.2 mul.141
  109.6 0.1 mul.142
  109.7 0.1 fusion.2
  109.9 0.1 bitcast_divide_fusion
  109.9 0.4 broadcast_in_dim.38
  110.3 20.9 %all_to_all.27 = f32[16,1,8192]{2,1,0:T(1,128)S(1)} all-to-all(f32[16,1,8192]{2,1,0:T(1,128)S(1)} %broadcast_in_dim.38), channel_id=1, replica_groups=mesh['grp'=16,'w'=8,'zq'=4] {'grp'}, dimensions={0} | all-to-all | bytes 1048576 | tf_op jit(solution)/shard_map/all_to_all | solution.py:180
  131.2 1.1 copy.54
  (28 shorter events, 0.5 us)
Async XLA Ops:
  6.4 11.6 %copy-start = (s32[512]{0:T(512)S(1)}, s32[512]{0:T(512)}, u32[]{:S(2)}) copy-start(s32[512]{0:T(512)} %param.11) | copy-start | bytes 6148
  7.5 33.5 %all-to-all-start = ((bf16[8,2,24704]{2,1,0:T(2,128)(2,1)}), bf16[8,2,24704]{2,1,0:T(2,128)(2,1)S(1)}, u32[]{:S(2)}, u32[]{:S(2)}) async-start(bf16[8,2,24704]{2,1,0:T(2,128)(2,1)} %reshape.238), calls=%async_computation | async-start | bytes 1581056 | tf_op jit(solution)/shard_map/all_to_all | solution.py:95
  44.0 15.8 %collective-permute-start.1 = (bf16[2,1032,128]{2,1,0:T(8,128)(2,1)S(1)}, bf16[2,1032,128]{2,1,0:T(8,128)(2,1)S(1)}, u32[]{:S(2)}, u32[]{:S(2)}) collective-permute-start(bf16[2,1032,128]{2,1,0:T(8,128)(2,1)S(1)} %pad_maximum_fusion), channel_id=1, source_target_pairs={{0,2},{1,3},{2,0},{3,1},{4,6},{5,7},{6,4},{7,5},{8,10},{9,11},{10,... | collective-permute-start | bytes 1585160 | tf_op jit(solution)/shard_map/ppermute | solution.py:119
  47.1 14.8 %collective-permute-start = (bf16[2,1032,128]{2,1,0:T(8,128)(2,1)S(1)}, bf16[2,1032,128]{2,1,0:T(8,128)(2,1)S(1)}, u32[]{:S(2)}, u32[]{:S(2)}) collective-permute-start(bf16[2,1032,128]{2,1,0:T(8,128)(2,1)S(1)} %pad_maximum_fusion), channel_id=1, source_target_pairs={{0,1},{1,0},{2,3},{3,2},{4,5},{5,4},{6,7},{7,6},{8,9},{9,8},{10,11... | collective-permute-start | bytes 1585160 | tf_op jit(solution)/shard_map/ppermute | solution.py:119
  59.9 9.1 %collective-permute-start.2 = (bf16[2,1032,128]{2,1,0:T(8,128)(2,1)S(1)}, bf16[2,1032,128]{2,1,0:T(8,128)(2,1)S(1)}, u32[]{:S(2)}, u32[]{:S(2)}) collective-permute-start(bf16[2,1032,128]{2,1,0:T(8,128)(2,1)S(1)} %collective-permute-done.1), channel_id=1, source_target_pairs={{0,1},{1,0},{2,3},{3,2},{4,5},{5,4},{6,7},{7,6},{8,9},{9,8},{10,11... | collective-permute-start | bytes 1585160 | tf_op jit(solution)/shard_map/ppermute | solution.py:119

commit v18 on v12

--- a/solution.py
+++ b/solution.py
@@ -116,13 +116,13 @@
     )
     local_keys = ways * positions
     both_here = jnp.stack([keys_here, values_here])
-    blocks = [both_here] + [
-        lax.ppermute(both_here, "zq", [(i, (i + shift) % quarters) for i in range(quarters)])
-        for shift in range(1, quarters)
-    ]
+    def swap(value, mask):
+        return lax.ppermute(value, "zq", [(i, i ^ mask) for i in range(quarters)])
+    across = swap(both_here, 2)
+    blocks = [both_here, swap(both_here, 1), across, swap(across, 1)]
     draft_k = jnp.concatenate([block[0, local_keys:] for block in blocks], axis=0)
     draft_v = jnp.concatenate([block[1, local_keys:] for block in blocks], axis=0)
-    source_quarter = (quarter - lax.iota(jnp.int32, quarters)) % quarters
+    source_quarter = jnp.bitwise_xor(quarter, lax.iota(jnp.int32, quarters))
 
     block_rows = ways * rows
     query_rows = query_block.reshape(block_rows * group_heads, HD)
@@ -163,21 +163,20 @@
 
     groups = lax.axis_size("grp")
     def by_destination(part):
-        part = part.reshape((ways, groups) + part.shape[1:])
-        return part.transpose((1, 0) + tuple(range(2, part.ndim))).reshape(groups * ways, -1)
+        return part.reshape(ways * groups, -1)
     packed = jnp.concatenate(
         [by_destination(summed), by_destination(peak), by_destination(totals)], axis=1
     )
-    parts = lax.all_to_all(packed, ("grp", "w"), 0, 0, tiled=True)
+    parts = lax.all_to_all(packed, ("w", "grp"), 0, 0, tiled=True)
     sum_size = group_heads * HD
-    parts = parts.reshape(groups, KV, -1)
-    part_sums = parts[:, :, :sum_size].reshape(groups, KV, group_heads, HD)
+    parts = parts.reshape(KV, groups, -1)
+    part_sums = parts[:, :, :sum_size].reshape(KV, groups, group_heads, HD)
     part_peaks = parts[:, :, sum_size : sum_size + group_heads]
     part_totals = parts[:, :, sum_size + group_heads :]
-    joined = jnp.max(part_peaks, axis=0)
-    scales = jnp.exp(part_peaks - joined[None])
-    merged_totals = jnp.sum(part_totals * scales, axis=0)
-    merged_sums = jnp.sum(part_sums * scales[..., None], axis=0)
+    joined = jnp.max(part_peaks, axis=1)
+    scales = jnp.exp(part_peaks - joined[:, None])
+    merged_totals = jnp.sum(part_totals * scales, axis=1)
+    merged_sums = jnp.sum(part_sums * scales[..., None], axis=1)
     attended = (merged_sums / merged_totals[..., None]).reshape(1, H * HD)
     attended = jnp.broadcast_to(attended[None], (groups,) + attended.shape)
     attended = lax.all_to_all(attended, "grp", 0, 0, tiled=True)

time: 140 us -> 137 us (0.979)
  the two profiles are of different devices: /device:TPU:1 before, /device:TPU:6 now
where the time goes in v18:
time: 137 us; the launch traced here: 135 us
  blocking collectives  52.9 us (39%)
  waiting for transfers between devices  29.4 us (21%)
  starting transfers between devices  16.9 us (12%)
  Pallas kernels  16.5 us (12%)
  local copies, waits for them, and re-layouts  13.4 us (10%)
  other arithmetic  4.29 us (3%)
    all_to_all x1, blocking collectives, local(): parts = lax.all_to_all(packed, ('w', 'grp'), 0, 0, tiled=True)  32.1 us
    all_to_all x1, waiting for transfers between devices, local(): got = lax.all_to_all(send, 'w', 0, 0, tiled=True)  22.7 us
    all_to_all x1, blocking collectives, local(): attended = lax.all_to_all(attended, 'grp', 0, 0, tiled=True)  20.9 us
    pallas_call x4, Pallas kernels, attend_prefix(): pl.pallas_call(functools.partial(attend_kernel, inverse_root), grid=(coun...  16.5 us
    all_to_all x1, starting transfers between devices, local(): got = lax.all_to_all(send, 'w', 0, 0, tiled=True)  10.3 us
    unnamed x14, local copies, waits for them, and re-layouts  7.95 us
    ppermute x3, waiting for transfers between devices, swap(): return lax.ppermute(value, 'zq', [(i, i ^ mask) for i in range(quarters)])  6.67 us
    ppermute x3, starting transfers between devices, swap(): return lax.ppermute(value, 'zq', [(i, i ^ mask) for i in range(quarters)])  6.57 us
  transfers between devices with their start and end apart: 4, of which 2 were waited for; matrix products, arithmetic and copies ran while one was open for 2% of the time, Pallas kernels for 9%

profile of v18, /device:TPU:6, one launch (start us, length us, event | category | flops | bytes accessed | tf_op | source)
XLA Modules:
  0.0 134.7 jit_solution(4481815344617361403)
XLA Ops:
  0.0 0.7 reduce.1
  0.7 0.7 reduce.2
  1.4 1.1 copy.68
  2.5 1.0 copy.69
  3.5 1.0 copy.70
  4.6 0.5 broadcast.170
  5.1 1.2 reduce.9
  6.4 0.0 copy-start
  6.4 1.1 reshape.234
  7.5 10.3 %all-to-all-start = ((bf16[8,2,24704]{2,1,0:T(2,128)(2,1)}), bf16[8,2,24704]{2,1,0:T(2,128)(2,1)S(1)}, u32[]{:S(2)}, u32[]{:S(2)}) async-start(bf16[8,2,24704]{2,1,0:T(2,128)(2,1)} %reshape.234), calls=%async_computation | async-start | bytes 1581056 | tf_op jit(solution)/shard_map/all_to_all | solution.py:96
  17.8 0.1 add_add_fusion
  17.9 0.1 add.93
  18.0 0.0 copy-done
  18.0 0.1 reshape.214
  18.1 0.1 reshape.215
  18.2 0.1 compare_and_fusion
  18.3 22.7 %all-to-all-done = bf16[8,2,24704]{2,1,0:T(2,128)(2,1)S(1)} async-done(((bf16[8,2,24704]{2,1,0:T(2,128)(2,1)}), bf16[8,2,24704]{2,1,0:T(2,128)(2,1)S(1)}, u32[]{:S(2)}, u32[]{:S(2)}) %all-to-all-start) | async-done | bytes 790560 | tf_op jit(solution)/shard_map/all_to_all | solution.py:96
  41.0 2.5 %reshape.235 = bf16[8,1,49408]{2,1,0:T(2,128)(2,1)S(1)} reshape(bf16[8,2,24704]{2,1,0:T(2,128)(2,1)S(1)} %all-to-all-done) | data formatting | bytes 1581056
  43.5 0.1 copy.79
  43.6 0.1 fusion.36
  43.6 0.1 reshape.210
  43.8 0.1 reshape.211
  44.0 0.1 pad_maximum_fusion
  44.0 2.7 %collective-permute-start = (bf16[2,1032,128]{2,1,0:T(8,128)(2,1)S(1)}, bf16[2,1032,128]{2,1,0:T(8,128)(2,1)}, u32[]{:S(2)}, u32[]{:S(2)}) collective-permute-start(bf16[2,1032,128]{2,1,0:T(8,128)(2,1)S(1)} %pad_maximum_fusion), channel_id=1, source_target_pairs={{0,2},{1,3},{2,0},{3,1},{4,6},{5,7},{6,4},{7,5},{8,10},{9,11},{10,... | collective-permute-start | bytes 1585160 | tf_op jit(solution)/shard_map/ppermute | solution.py:120
  46.8 0.1 reshape_reshape.3.query_ref
  46.9 0.1 reshape.216
  47.1 1.9 %collective-permute-start.2 = (bf16[2,1032,128]{2,1,0:T(8,128)(2,1)S(1)}, bf16[2,1032,128]{2,1,0:T(8,128)(2,1)S(1)}, u32[]{:S(2)}, u32[]{:S(2)}) collective-permute-start(bf16[2,1032,128]{2,1,0:T(8,128)(2,1)S(1)} %pad_maximum_fusion), channel_id=1, source_target_pairs={{0,1},{1,0},{2,3},{3,2},{4,5},{5,4},{6,7},{7,6},{8,9},{9,8},{10,11... | collective-permute-start | bytes 1585160 | tf_op jit(solution)/shard_map/ppermute | solution.py:120
  49.2 4.1 %shard_map.64 = (f32[1024,128]{1,0:T(8,128)S(1)}, f32[1024,1]{1,0:T(8,128)S(1)}, f32[1024,1]{1,0:T(8,128)S(1)}) custom-call(bf16[1024,128]{1,0:T(8,128)(2,1)S(1)} %reshape_reshape.3.query_ref, bf16[1024,128]{1,0:T(8,128)(2,1)S(1)} %slice_bitcast_fusion.1.key_ref, ...), custom_call_target="tpu_custom_call", output_to_operand_aliasing={{0}: (3, {}), {1}: (4, {}), {2}: (5, {})} | custom-call | flops 805306368 | bytes 1851392 | tf_op jit(solution)/shard_map/pallas_call | solution.py:58
  53.3 6.7 %collective-permute-done = bf16[2,1032,128]{2,1,0:T(8,128)(2,1)} collective-permute-done((bf16[2,1032,128]{2,1,0:T(8,128)(2,1)S(1)}, bf16[2,1032,128]{2,1,0:T(8,128)(2,1)}, u32[]{:S(2)}, u32[]{:S(2)}) %collective-permute-start) | collective-permute-done | bytes 528416 | tf_op jit(solution)/shard_map/ppermute | solution.py:120
  60.0 1.9 %collective-permute-start.1 = (bf16[2,1032,128]{2,1,0:T(8,128)(2,1)}, bf16[2,1032,128]{2,1,0:T(8,128)(2,1)S(1)}, u32[]{:S(2)}, u32[]{:S(2)}) collective-permute-start(bf16[2,1032,128]{2,1,0:T(8,128)(2,1)} %collective-permute-done), channel_id=1, source_target_pairs={{0,1},{1,0},{2,3},{3,2},{4,5},{5,4},{6,7},{7,6},{8,9},{9,8},{10,11... | collective-permute-start | bytes 1585160 | tf_op jit(solution)/shard_map/ppermute | solution.py:120
  61.9 1.1 slice_bitcast_fusion.4
  63.0 0.0 collective-permute-done.2
  63.0 4.1 %shard_map.65 = (f32[1024,128]{1,0:T(8,128)S(1)}, f32[1024,1]{1,0:T(8,128)S(1)}, f32[1024,1]{1,0:T(8,128)S(1)}) custom-call(bf16[1024,128]{1,0:T(8,128)(2,1)S(1)} %reshape_reshape.3.query_ref, bf16[1024,128]{1,0:T(8,128)(2,1)S(1)} %get-tuple-element.45.key_ref, ...), custom_call_target="tpu_custom_call", output_to_operand_aliasing={{0}: (3, {}), {1}: (4, {}), {2}: (5, {})} | custom-call | flops 805306368 | bytes 1851392 | tf_op jit(solution)/shard_map/pallas_call | solution.py:58
  67.2 4.1 %shard_map.66 = (f32[1024,128]{1,0:T(8,128)S(1)}, f32[1024,1]{1,0:T(8,128)S(1)}, f32[1024,1]{1,0:T(8,128)S(1)}) custom-call(bf16[1024,128]{1,0:T(8,128)(2,1)S(1)} %reshape_reshape.3.query_ref, bf16[1024,128]{1,0:T(8,128)(2,1)S(1)} %get-tuple-element.47.key_ref, ...), custom_call_target="tpu_custom_call", output_to_operand_aliasing={{0}: (3, {}), {1}: (4, {}), {2}: (5, {})} | custom-call | flops 805306368 | bytes 1851392 | tf_op jit(solution)/shard_map/pallas_call | solution.py:58
  71.3 0.7 slice_bitcast_fusion.9
  72.0 0.0 collective-permute-done.1
  72.0 4.1 %shard_map.67 = (f32[1024,128]{1,0:T(8,128)S(1)}, f32[1024,1]{1,0:T(8,128)S(1)}, f32[1024,1]{1,0:T(8,128)S(1)}) custom-call(bf16[1024,128]{1,0:T(8,128)(2,1)S(1)} %reshape_reshape.3.query_ref, bf16[1024,128]{1,0:T(8,128)(2,1)S(1)} %get-tuple-element.49.key_ref, ...), custom_call_target="tpu_custom_call", output_to_operand_aliasing={{0}: (3, {}), {1}: (4, {}), {2}: (5, {})} | custom-call | flops 805306368 | bytes 1851392 | tf_op jit(solution)/shard_map/pallas_call | solution.py:58
  76.2 0.2 copy.57
  76.4 0.2 reduce.3
  76.6 0.2 reduce.5
  76.8 0.1 reshape.218
  77.0 0.1 reshape.213
  77.1 0.2 fusion.38
  77.5 0.3 fusion.7
  77.7 0.3 fusion
  78.1 0.9 copy.59
  79.0 32.1 %all_to_all.26 = f32[128,1,1040]{2,1,0:T(1,128)S(1)} all-to-all(f32[128,1,1040]{2,1,0:T(1,128)S(1)} %copy.59), channel_id=1, replica_groups=mesh['grp'=16,'w'=8,'zq'=4] {'w','grp'}, dimensions={0} | all-to-all | bytes 1064960 | tf_op jit(solution)/shard_map/all_to_all | solution.py:170
  111.1 0.7 fusion.8
  111.8 0.2 mul.73
  112.0 0.1 mul.74
  112.1 0.1 fusion.2
  112.2 0.1 bitcast_divide_fusion
  112.3 0.4 broadcast_in_dim.50
  112.7 20.9 %all_to_all.27 = f32[16,1,8192]{2,1,0:T(1,128)S(1)} all-to-all(f32[16,1,8192]{2,1,0:T(1,128)S(1)} %broadcast_in_dim.50), channel_id=1, replica_groups=mesh['grp'=16,'w'=8,'zq'=4] {'grp'}, dimensions={0} | all-to-all | bytes 1048576 | tf_op jit(solution)/shard_map/all_to_all | solution.py:182
  133.6 1.1 copy.80
  (29 shorter events, 0.6 us)
Async XLA Ops:
  6.4 11.6 %copy-start = (s32[512]{0:T(512)S(1)}, s32[512]{0:T(512)}, u32[]{:S(2)}) copy-start(s32[512]{0:T(512)} %param.11) | copy-start | bytes 6148
  7.5 33.5 %all-to-all-start = ((bf16[8,2,24704]{2,1,0:T(2,128)(2,1)}), bf16[8,2,24704]{2,1,0:T(2,128)(2,1)S(1)}, u32[]{:S(2)}, u32[]{:S(2)}) async-start(bf16[8,2,24704]{2,1,0:T(2,128)(2,1)} %reshape.234), calls=%async_computation | async-start | bytes 1581056 | tf_op jit(solution)/shard_map/all_to_all | solution.py:96
  44.0 15.9 %collective-permute-start = (bf16[2,1032,128]{2,1,0:T(8,128)(2,1)S(1)}, bf16[2,1032,128]{2,1,0:T(8,128)(2,1)}, u32[]{:S(2)}, u32[]{:S(2)}) collective-permute-start(bf16[2,1032,128]{2,1,0:T(8,128)(2,1)S(1)} %pad_maximum_fusion), channel_id=1, source_target_pairs={{0,2},{1,3},{2,0},{3,1},{4,6},{5,7},{6,4},{7,5},{8,10},{9,11},{10,... | collective-permute-start | bytes 1585160 | tf_op jit(solution)/shard_map/ppermute | solution.py:120
  47.1 15.9 %collective-permute-start.2 = (bf16[2,1032,128]{2,1,0:T(8,128)(2,1)S(1)}, bf16[2,1032,128]{2,1,0:T(8,128)(2,1)S(1)}, u32[]{:S(2)}, u32[]{:S(2)}) collective-permute-start(bf16[2,1032,128]{2,1,0:T(8,128)(2,1)S(1)} %pad_maximum_fusion), channel_id=1, source_target_pairs={{0,1},{1,0},{2,3},{3,2},{4,5},{5,4},{6,7},{7,6},{8,9},{9,8},{10,11... | collective-permute-start | bytes 1585160 | tf_op jit(solution)/shard_map/ppermute | solution.py:120
  60.0 12.0 %collective-permute-start.1 = (bf16[2,1032,128]{2,1,0:T(8,128)(2,1)}, bf16[2,1032,128]{2,1,0:T(8,128)(2,1)S(1)}, u32[]{:S(2)}, u32[]{:S(2)}) collective-permute-start(bf16[2,1032,128]{2,1,0:T(8,128)(2,1)} %collective-permute-done), channel_id=1, source_target_pairs={{0,1},{1,0},{2,3},{3,2},{4,5},{5,4},{6,7},{7,6},{8,9},{9,8},{10,11... | collective-permute-start | bytes 1585160 | tf_op jit(solution)/shard_map/ppermute | solution.py:120
